TPU v7x, 1024 devices: a whole 8x8x8 slice. The times are simulated.
1024 devices in a mesh: gx: 64 (over y_lo, x, core), gy: 16 (over z, y_hi).
Axes of the slice: x: 8, y: 8 (y_hi: 2, y_lo: 4; y = y_hi * 4 + y_lo), z: 8, core: 2. Of those that a mesh axis runs over, the one named last changes fastest.
Arguments:
- velocity: float32 [512, 128, 128], P('gx', 'gy'), may hold values from -6 to 6
- cotangent: float32 [512, 128, 128], P('gx', 'gy'), may hold values from -6 to 6
- block_ids: int32 [64, 16, 128], P('gx', 'gy'), may hold values from 0 to 127, as said below
- fluid_count: int32 [64, 16], P('gx', 'gy'), may hold values from 32 to 128, as said below
- fluid_cells: int32 [64, 16, 8192], P('gx', 'gy'), may hold values 0 or 1
- w_in: bfloat16 [64, 7], replicated, may hold values from -2 to 2
- w_mid: bfloat16 [64, 64], replicated, may hold values from -0.75 to 0.75
- w_out: bfloat16 [1, 64], replicated, may hold values from -0.75 to 0.75
Outputs:
- new_field: float32 [512, 128, 128], P('gx', 'gy')
- grad_field: float32 [512, 128, 128], P('gx', 'gy')
- grad_in: float32 [64, 7], replicated
- grad_mid: float32 [64, 64], replicated
- grad_out: float32 [1, 64], replicated
Inputs may be any that keep to these rules, and one draw needn't show every extreme that they name: `block_ids`: within one device's list the block numbers are distinct. `fluid_count`: some device's list is wholly live.
All inputs are finite; a program needn't handle non-finite values. No bound on the sum of `fluid_cells` on one device may be relied on, other than what follows from the above.
Results may differ from a plain program's by a relative error of at most 0.018.
Values sent between devices are 32-bit elements; how exact they have to be, the bound alone decides.
No kernel may reach another device: no remote copies, remote signals or barrier semaphores. Data moves between devices by JAX's collectives and lax.ppermute only.
A program may use at most 32 MiB of HBM per device.

v0:
```python
import jax
import jax.numpy as jnp
from jax import lax
from jax.sharding import PartitionSpec as P

viscosity = 0.1


def padded_2(cells, sides, width):
    for axis, dim in sides:
        count = lax.axis_size(axis)
        head = lax.slice_in_dim(cells, 0, width, axis=dim)
        tail = lax.slice_in_dim(cells, cells.shape[dim] - width, cells.shape[dim], axis=dim)
        cells = jnp.concatenate(
            [
                lax.ppermute(tail, axis, [(i, (i + 1) % count) for i in range(count)]),
                cells,
                lax.ppermute(head, axis, [((i + 1) % count, i) for i in range(count)]),
            ],
            axis=dim,
        )
    return cells


def to_blocks(field):
    lead = field.shape[:-3]
    sizex, sizey, sizez = field.shape[-3:]
    count = len(lead)
    shaped = field.reshape(lead + (sizex // 4, 4, sizey // 4, 4, sizez // 4, 4))
    order = list(range(count)) + [count, count + 2, count + 4, count + 1, count + 3, count + 5]
    return shaped.transpose(order).reshape(lead + (sizex * sizey * sizez // 64, 64))


def from_blocks(blocks, sizex, sizey, sizez):
    lead = blocks.shape[:-2]
    count = len(lead)
    shaped = blocks.reshape(lead + (sizex // 4, sizey // 4, sizez // 4, 4, 4, 4))
    order = list(range(count)) + [count, count + 3, count + 1, count + 4, count + 2, count + 5]
    return shaped.transpose(order).reshape(lead + (sizex, sizey, sizez))


def closure_tile(padded, cotile, ids, count, fluid, w_in, w_mid, w_out):
    sizex = padded.shape[0] - 2
    sizey = padded.shape[1] - 2
    sizez = padded.shape[2]
    slots = ids.shape[0]
    nblocks = sizex * sizey * sizez // 64
    center = padded[1:-1, 1:-1]
    stencil = jnp.stack(
        [
            center,
            padded[2:, 1:-1],
            padded[:-2, 1:-1],
            padded[1:-1, 2:],
            padded[1:-1, :-2],
            jnp.roll(center, -1, 2),
            jnp.roll(center, 1, 2),
        ]
    ).astype(jnp.bfloat16)
    chosen = jnp.take(to_blocks(stencil), ids, axis=1).reshape(7, slots * 64)
    live = (jnp.arange(slots) < count).astype(jnp.float32)
    weight = (fluid.reshape(slots, 64).astype(jnp.float32) * live[:, None]).reshape(slots * 64)
    h1 = jnp.tanh(jnp.dot(w_in, chosen, preferred_element_type=jnp.float32)).astype(jnp.bfloat16)
    h2 = jnp.tanh(jnp.dot(w_mid, h1, preferred_element_type=jnp.float32)).astype(jnp.bfloat16)
    closure = jnp.dot(w_out, h2, preferred_element_type=jnp.float32)[0] * weight
    corr_blocks = jnp.zeros((nblocks, 64), jnp.float32).at[ids].add(closure.reshape(slots, 64))
    corr = from_blocks(corr_blocks, sizex, sizey, sizez)
    cot_sel = jnp.take(to_blocks(cotile), ids, axis=0).reshape(slots * 64)
    dcl = (cot_sel * weight).astype(jnp.bfloat16)
    h2f = h2.astype(jnp.float32)
    h1f = h1.astype(jnp.float32)
    dh2 = jnp.dot(w_out.T, dcl[None, :], preferred_element_type=jnp.float32)
    da2 = (dh2 * (1.0 - h2f * h2f)).astype(jnp.bfloat16)
    dh1 = jnp.dot(w_mid.T, da2, preferred_element_type=jnp.float32)
    da1 = (dh1 * (1.0 - h1f * h1f)).astype(jnp.bfloat16)
    dfeat = jnp.dot(w_in.T, da1, preferred_element_type=jnp.float32)
    dims = (((1,), (1,)), ((), ()))
    gin = lax.dot_general(da1, chosen, dims, preferred_element_type=jnp.float32)
    gmid = lax.dot_general(da2, h1, dims, preferred_element_type=jnp.float32)
    gout = lax.dot_general(dcl[None, :], h2, dims, preferred_element_type=jnp.float32)
    dense = jnp.zeros((7, nblocks, 64), jnp.float32).at[:, ids].add(dfeat.reshape(7, slots, 64))
    dense = from_blocks(dense, sizex, sizey, sizez)
    local = dense[0] + jnp.roll(dense[5], 1, 2) + jnp.roll(dense[6], -1, 2)
    return (corr, local, dense[1:5], gin, gmid, gout)


def padded_laplace(padded):
    center = padded[1:-1, 1:-1]
    total = padded[2:, 1:-1] + padded[:-2, 1:-1] + padded[1:-1, 2:] + padded[1:-1, :-2]
    total = total + jnp.roll(center, -1, 2) + jnp.roll(center, 1, 2)
    return total - 6.0 * center


def body(velocity, cotangent, block_ids, fluid_count, fluid_cells, w_in, w_mid, w_out):
    slots = block_ids.shape[2]
    both = padded_2(jnp.stack([velocity, cotangent]), (("gx", 1), ("gy", 2)), 1)
    padded = both[0]
    cot_pad = both[1]
    corr, local, side, gin, gmid, gout = closure_tile(
        padded,
        cotangent,
        block_ids.reshape(slots),
        fluid_count[0, 0],
        fluid_cells.reshape(slots * 64),
        w_in,
        w_mid,
        w_out,
    )
    new_field = velocity + viscosity * padded_laplace(padded) + corr
    beside_all = padded_2(side, (("gx", 1), ("gy", 2)), 1)
    beside = (
        beside_all[0, :-2, 1:-1]
        + beside_all[1, 2:, 1:-1]
        + beside_all[2, 1:-1, :-2]
        + beside_all[3, 1:-1, 2:]
    )
    grad_field = cotangent + viscosity * padded_laplace(cot_pad) + local + beside
    flat = jnp.concatenate([gin.reshape(-1), gmid.reshape(-1), gout.reshape(-1)])
    total = lax.psum(flat, ("gx", "gy"))
    scale = 1.0 / jnp.sqrt(jnp.float32(lax.axis_size("gx") * lax.axis_size("gy") * slots * 64))
    total = total * scale
    width = gmid.shape[0]
    grad_in = total[: width * 7].reshape(width, 7)
    grad_mid = total[width * 7 : width * 7 + width * width].reshape(width, width)
    grad_out = total[width * 7 + width * width :].reshape(1, width)
    return (new_field, grad_field, grad_in, grad_mid, grad_out)


def solution(mesh):
    in_specs = (
        P("gx", "gy", None),
        P("gx", "gy", None),
        P("gx", "gy", None),
        P("gx", "gy"),
        P("gx", "gy", None),
        P(),
        P(),
        P(),
    )
    out_specs = (P("gx", "gy", None), P("gx", "gy", None), P(), P(), P())
    return jax.shard_map(body, mesh=mesh, in_specs=in_specs, out_specs=out_specs, check_vma=False)
```

profile of v0, /device:TPU:14, one launch (start us, length us, event | category | flops | bytes accessed | tf_op | source)
XLA Modules:
  0.0 230.3 jit_solution(8652441074666710420)
XLA Ops:
  1.4 1.9 collective-permute-start
  3.4 3.6 %collective-permute-start.1 = (f32[2,1,8,128]{3,2,1,0:T(8,128)S(1)}, f32[2,1,8,128]{3,2,1,0:T(8,128)S(1)}, u32[]{:S(2)}, u32[]{:S(2)}) collective-permute-start(f32[2,1,8,128]{3,2,1,0:T(8,128)S(1)} %get-tuple-element.45), channel_id=1, source_target_pairs={{16,0},{32,16},{48,32},{64,48},{80,64},{96,80},{112,96},{128,112},... | collective-permute-start | bytes 24584 | tf_op jit(solution)/shard_map/ppermute | solution.py:18
  8.6 1.8 reshape.198
  14.5 8.2 %collective-permute-start.2 = (f32[2,10,1,128]{3,2,1,0:T(1,128)S(1)}, f32[2,10,1,128]{3,2,1,0:T(1,128)S(1)}, u32[]{:S(2)}, u32[]{:S(2)}) collective-permute-start(f32[2,10,1,128]{3,2,1,0:T(1,128)S(1)} %get-tuple-element.42), channel_id=1, source_target_pairs={{0,1},{1,2},{2,3},{3,4},{4,5},{5,6},{6,7},{7,8},{8,9},{9,10},{10,1... | collective-permute-start | bytes 30728 | tf_op jit(solution)/shard_map/ppermute | solution.py:16
  22.7 16.8 %collective-permute-start.3 = (f32[2,10,1,128]{3,2,1,0:T(1,128)S(1)}, f32[2,10,1,128]{3,2,1,0:T(1,128)S(1)}, u32[]{:S(2)}, u32[]{:S(2)}) collective-permute-start(f32[2,10,1,128]{3,2,1,0:T(1,128)S(1)} %get-tuple-element.43), channel_id=1, source_target_pairs={{1,0},{2,1},{3,2},{4,3},{5,4},{6,5},{7,6},{8,7},{9,8},{10,9},{11,1... | collective-permute-start | bytes 30728 | tf_op jit(solution)/shard_map/ppermute | solution.py:18
  44.2 1.1 stack.42
  45.8 1.1 stack.36
  49.0 1.1 stack.38
  50.6 1.1 stack.37
  52.2 1.1 stack.41
  56.9 1.3 fusion.11
  60.8 5.1 %scatter_fusion = f32[7,128,64]{2,0,1:T(8,128)S(1)} fusion(f32[7,128,64]{2,0,1:T(8,128)S(1)} %broadcast_in_dim.40, s32[128]{0:T(128)S(1)} %fusion.31, f32[128,7,64]{2,1,0:T(8,128)S(1)} %copy.62), kind=kCustom, calls=%fused_computation.3 | custom fusion | flops 57344 | bytes 688640 | tf_op jit(solution)/shard_map/scatter-add | solution.py:81
  68.7 2.3 dot_general.41
  71.0 1.7 convolution_bitcast_fusion.1
  75.1 117.0 %psum.7 = f32[4608]{0:T(1024)S(1)} all-reduce(f32[4608]{0:T(1024)S(1)} %concatenate.62), channel_id=1, replica_groups=mesh['gx'=64,'gy'=16] {'gx','gy'}, use_global_device_ids=true, to_apply=%region_2.3 | all-reduce | flops 4608 | bytes 36864 | tf_op jit(solution)/shard_map/psum | solution.py:119
  192.1 1.3 multiply_reduce_fusion
  193.4 1.4 scatter_custom_fusion
  196.9 3.0 %copy.67 = f32[4,2,4,2,4,32,4]{6,5,4,3,2,1,0:T(8,128)} copy(f32[4,2,4,2,4,32,4]{5,3,1,6,4,2,0:T(2,128)S(1)} %copy-done.1) | data formatting | bytes 262144 | tf_op jit(solution)/shard_map/slice | solution.py:84
  199.9 4.9 %slice.202 = f32[4,8,8,128]{3,2,1,0:T(8,128)S(1)} reshape(f32[4,2,4,2,4,32,4]{6,5,4,3,2,1,0:T(8,128)} %copy.67) | data formatting | bytes 262144 | tf_op jit(solution)/shard_map/slice | solution.py:84
  204.8 2.1 collective-permute-start.4
  206.9 3.6 %collective-permute-start.5 = (f32[4,1,8,128]{3,2,1,0:T(8,128)S(1)}, f32[4,1,8,128]{3,2,1,0:T(8,128)S(1)}, u32[]{:S(2)}, u32[]{:S(2)}) collective-permute-start(f32[4,1,8,128]{3,2,1,0:T(8,128)S(1)} %get-tuple-element.27), channel_id=1, source_target_pairs={{16,0},{32,16},{48,32},{64,48},{80,64},{96,80},{112,96},{128,112},... | collective-permute-start | bytes 49160 | tf_op jit(solution)/shard_map/ppermute | solution.py:18
  210.6 1.4 collective-permute-done.5
  212.0 4.4 %collective-permute-start.6 = (f32[4,10,1,128]{3,2,1,0:T(1,128)S(1)}, f32[4,10,1,128]{3,2,1,0:T(1,128)S(1)}, u32[]{:S(2)}, u32[]{:S(2)}) collective-permute-start(f32[4,10,1,128]{3,2,1,0:T(1,128)S(1)} %get-tuple-element.25), channel_id=1, source_target_pairs={{0,1},{1,2},{2,3},{3,4},{4,5},{5,6},{6,7},{7,8},{8,9},{9,10},{10,1... | collective-permute-start | bytes 61448 | tf_op jit(solution)/shard_map/ppermute | solution.py:16
  216.5 7.4 %collective-permute-start.7 = (f32[4,10,1,128]{3,2,1,0:T(1,128)S(1)}, f32[4,10,1,128]{3,2,1,0:T(1,128)S(1)}, u32[]{:S(2)}, u32[]{:S(2)}) collective-permute-start(f32[4,10,1,128]{3,2,1,0:T(1,128)S(1)} %get-tuple-element.26), channel_id=1, source_target_pairs={{1,0},{2,1},{3,2},{4,3},{5,4},{6,5},{7,6},{8,7},{9,8},{10,9},{11,1... | collective-permute-start | bytes 61448 | tf_op jit(solution)/shard_map/ppermute | solution.py:18
  (150 shorter events, 33.5 us)
Async XLA Ops:
  0.6 55.8 %copy-start = (bf16[64,64]{1,0:T(8,128)(2,1)S(1)}, bf16[64,64]{1,0:T(8,128)(2,1)}, u32[]{:S(2)}) copy-start(bf16[64,64]{1,0:T(8,128)(2,1)} %param.14) | copy-start | bytes 24580
  0.6 13.9 %copy-start.2 = (f32[8,8,128]{2,1,0:T(8,128)S(1)}, f32[8,8,128]{2,1,0:T(8,128)}, u32[]{:S(2)}) copy-start(f32[8,8,128]{2,1,0:T(8,128)} %param.9) | copy-start | bytes 98308
  0.7 13.9 %copy-start.5 = (f32[8,8,128]{2,1,0:T(8,128)S(1)}, f32[8,8,128]{2,1,0:T(8,128)}, u32[]{:S(2)}) copy-start(f32[8,8,128]{2,1,0:T(8,128)} %param.8) | copy-start | bytes 98308
  0.7 38.8 %copy-start.24 = (bf16[1,64]{1,0:T(2,128)(2,1)S(1)}, bf16[1,64]{1,0:T(2,128)(2,1)}, u32[]{:S(2)}) copy-start(bf16[1,64]{1,0:T(2,128)(2,1)} %param.15) | copy-start | bytes 388
  1.4 13.0 %collective-permute-start = (f32[2,1,8,128]{3,2,1,0:T(8,128)S(1)}, f32[2,1,8,128]{3,2,1,0:T(8,128)S(1)}, u32[]{:S(2)}, u32[]{:S(2)}) collective-permute-start(f32[2,1,8,128]{3,2,1,0:T(8,128)S(1)} %get-tuple-element.44), channel_id=1, source_target_pairs={{0,16},{16,32},{32,48},{48,64},{64,80},{80,96},{96,112},{112,128},... | collective-permute-start | bytes 24584 | tf_op jit(solution)/shard_map/ppermute | solution.py:16
  3.4 11.1 %collective-permute-start.1 = (f32[2,1,8,128]{3,2,1,0:T(8,128)S(1)}, f32[2,1,8,128]{3,2,1,0:T(8,128)S(1)}, u32[]{:S(2)}, u32[]{:S(2)}) collective-permute-start(f32[2,1,8,128]{3,2,1,0:T(8,128)S(1)} %get-tuple-element.45), channel_id=1, source_target_pairs={{16,0},{32,16},{48,32},{64,48},{80,64},{96,80},{112,96},{128,112},... | collective-permute-start | bytes 24584 | tf_op jit(solution)/shard_map/ppermute | solution.py:18
  11.8 49.0 %copy-start.22 = (s32[128]{0:T(128)}, s32[128]{0:T(128)S(1)}, u32[]{:S(2)}) copy-start(s32[128]{0:T(128)S(1)} %fusion.31) | copy-start | bytes 1540
  12.5 30.0 %copy-start.20 = (f32[128]{0:T(128)}, f32[128]{0:T(128)S(1)}, u32[]{:S(2)}) copy-start(f32[128]{0:T(128)S(1)} %get-tuple-element.48) | copy-start | bytes 1540
  14.5 25.7 %collective-permute-start.2 = (f32[2,10,1,128]{3,2,1,0:T(1,128)S(1)}, f32[2,10,1,128]{3,2,1,0:T(1,128)S(1)}, u32[]{:S(2)}, u32[]{:S(2)}) collective-permute-start(f32[2,10,1,128]{3,2,1,0:T(1,128)S(1)} %get-tuple-element.42), channel_id=1, source_target_pairs={{0,1},{1,2},{2,3},{3,4},{4,5},{5,6},{6,7},{7,8},{8,9},{9,10},{10,1... | collective-permute-start | bytes 30728 | tf_op jit(solution)/shard_map/ppermute | solution.py:16
  22.7 18.1 %collective-permute-start.3 = (f32[2,10,1,128]{3,2,1,0:T(1,128)S(1)}, f32[2,10,1,128]{3,2,1,0:T(1,128)S(1)}, u32[]{:S(2)}, u32[]{:S(2)}) collective-permute-start(f32[2,10,1,128]{3,2,1,0:T(1,128)S(1)} %get-tuple-element.43), channel_id=1, source_target_pairs={{1,0},{2,1},{3,2},{4,3},{5,4},{6,5},{7,6},{8,7},{9,8},{10,9},{11,1... | collective-permute-start | bytes 30728 | tf_op jit(solution)/shard_map/ppermute | solution.py:18
  39.5 18.6 %copy-start.23 = (f32[64]{0:T(128)}, f32[64]{0:T(128)S(1)}, u32[]{:S(2)}) copy-start(f32[64]{0:T(128)S(1)} %bitcast_convert_fusion) | copy-start | bytes 772
  42.4 4.6 %copy-start.7 = (f32[8,8,127]{2,1,0:T(8,128)}, f32[8,8,127]{2,1,0:T(8,128)S(1)}, u32[]{:S(2)}) copy-start(f32[8,8,127]{2,1,0:T(8,128)S(1)} %get-tuple-element.35) | copy-start | bytes 97540
  42.4 4.6 %copy-start.9 = (f32[8,8,127]{2,1,0:T(8,128)}, f32[8,8,127]{2,1,0:T(8,128)S(1)}, u32[]{:S(2)}) copy-start(f32[8,8,127]{2,1,0:T(8,128)S(1)} %get-tuple-element.36) | copy-start | bytes 97540
  42.5 4.5 %copy-start.11 = (f32[8,8,1]{2,1,0:T(8,128)}, f32[8,8,1]{2,1,0:T(8,128)S(1)}, u32[]{:S(2)}) copy-start(f32[8,8,1]{2,1,0:T(8,128)S(1)} %get-tuple-element.33) | copy-start | bytes 772
  42.5 4.5 %copy-start.13 = (f32[8,8,1]{2,1,0:T(8,128)}, f32[8,8,1]{2,1,0:T(8,128)S(1)}, u32[]{:S(2)}) copy-start(f32[8,8,1]{2,1,0:T(8,128)S(1)} %get-tuple-element.34) | copy-start | bytes 772
  72.6 120.8 %copy-start.21 = (f32[128]{0:T(128)S(1)}, f32[128]{0:T(128)}, u32[]{:S(2)}) copy-start(f32[128]{0:T(128)} %copy-done.20) | copy-start | bytes 1540
  192.1 4.1 %copy-start.12 = (f32[8,8,1]{2,1,0:T(8,128)S(1)}, f32[8,8,1]{2,1,0:T(8,128)}, u32[]{:S(2)}) copy-start(f32[8,8,1]{2,1,0:T(8,128)} %copy-done.11) | copy-start | bytes 772
  192.1 4.1 %copy-start.14 = (f32[8,8,1]{2,1,0:T(8,128)S(1)}, f32[8,8,1]{2,1,0:T(8,128)}, u32[]{:S(2)}) copy-start(f32[8,8,1]{2,1,0:T(8,128)} %copy-done.13) | copy-start | bytes 772
  199.9 26.1 %copy-start.4 = (f32[1,2,4,2,4,32,4]{5,3,1,6,4,2,0:T(2,128)S(1)}, f32[1,2,4,2,4,32,4]{5,3,1,6,4,2,0:T(2,128)}, u32[]{:S(2)}) copy-start(f32[1,2,4,2,4,32,4]{5,3,1,6,4,2,0:T(2,128)} %get-tuple-element.20) | copy-start | bytes 98308
  204.8 22.4 %copy-start.3 = (f32[1,2,4,2,4,32,4]{5,3,1,6,4,2,0:T(2,128)S(1)}, f32[1,2,4,2,4,32,4]{5,3,1,6,4,2,0:T(2,128)}, u32[]{:S(2)}) copy-start(f32[1,2,4,2,4,32,4]{5,3,1,6,4,2,0:T(2,128)} %get-tuple-element.21) | copy-start | bytes 98308
  204.8 5.7 %collective-permute-start.4 = (f32[4,1,8,128]{3,2,1,0:T(8,128)S(1)}, f32[4,1,8,128]{3,2,1,0:T(8,128)S(1)}, u32[]{:S(2)}, u32[]{:S(2)}) collective-permute-start(f32[4,1,8,128]{3,2,1,0:T(8,128)S(1)} %get-tuple-element.28), channel_id=1, source_target_pairs={{0,16},{16,32},{32,48},{48,64},{64,80},{80,96},{96,112},{112,128},... | collective-permute-start | bytes 49160 | tf_op jit(solution)/shard_map/ppermute | solution.py:16
  206.9 5.1 %collective-permute-start.5 = (f32[4,1,8,128]{3,2,1,0:T(8,128)S(1)}, f32[4,1,8,128]{3,2,1,0:T(8,128)S(1)}, u32[]{:S(2)}, u32[]{:S(2)}) collective-permute-start(f32[4,1,8,128]{3,2,1,0:T(8,128)S(1)} %get-tuple-element.27), channel_id=1, source_target_pairs={{16,0},{32,16},{48,32},{64,48},{80,64},{96,80},{112,96},{128,112},... | collective-permute-start | bytes 49160 | tf_op jit(solution)/shard_map/ppermute | solution.py:18
  212.0 17.5 %collective-permute-start.6 = (f32[4,10,1,128]{3,2,1,0:T(1,128)S(1)}, f32[4,10,1,128]{3,2,1,0:T(1,128)S(1)}, u32[]{:S(2)}, u32[]{:S(2)}) collective-permute-start(f32[4,10,1,128]{3,2,1,0:T(1,128)S(1)} %get-tuple-element.25), channel_id=1, source_target_pairs={{0,1},{1,2},{2,3},{3,4},{4,5},{5,6},{6,7},{7,8},{8,9},{9,10},{10,1... | collective-permute-start | bytes 61448 | tf_op jit(solution)/shard_map/ppermute | solution.py:16
  216.5 13.1 %collective-permute-start.7 = (f32[4,10,1,128]{3,2,1,0:T(1,128)S(1)}, f32[4,10,1,128]{3,2,1,0:T(1,128)S(1)}, u32[]{:S(2)}, u32[]{:S(2)}) collective-permute-start(f32[4,10,1,128]{3,2,1,0:T(1,128)S(1)} %get-tuple-element.26), channel_id=1, source_target_pairs={{1,0},{2,1},{3,2},{4,3},{5,4},{6,5},{7,6},{8,7},{9,8},{10,9},{11,1... | collective-permute-start | bytes 61448 | tf_op jit(solution)/shard_map/ppermute | solution.py:18
  (9 other events, 27.2 us)
where the time goes:
time: 235 us; the launch traced here: 230 us
  blocking collectives  117 us (50%)
  starting transfers between devices  48.1 us (20%)
  local copies, waits for them, and re-layouts  42.1 us (18%)
  other arithmetic  13.2 us (6%)
  matrix products  5.93 us (3%)
    psum x1, blocking collectives, body(): total = lax.psum(flat, ('gx', 'gy'))  117 us
    ppermute x4, starting transfers between devices, padded_2(): lax.ppermute(head, axis, [((i + 1) % count, i) for i in range(count)])  31.5 us
    ppermute x4, starting transfers between devices, padded_2(): lax.ppermute(tail, axis, [(i, (i + 1) % count) for i in range(count)])  16.6 us
    another operation x15, local copies, waits for them, and re-layouts, closure_tile(): jnp.stack([center, padded[2:, 1:-1], padded[:-2, 1:-1], padded[1:-1, 2:],...  11.1 us
    slice x3, local copies, waits for them, and re-layouts, closure_tile(): return (corr, local, dense[1:5], gin, gmid, gout)  8.91 us
    scatter-add x1, other arithmetic, closure_tile(): jnp.zeros((7, nblocks, 64), jnp.float32).at[:, ids]  5.09 us
  transfers between devices with their start and end apart: 8, of which 2 were waited for; matrix products, arithmetic and copies ran while one was open for 6% of the time, Pallas kernels for 0%

commit v1 on v0

v1 whole, which is shorter than its diff:
```python
import jax
import jax.numpy as jnp
from jax import lax
from jax.sharding import PartitionSpec as P

viscosity = 0.1

GROUP_BITS = (("gx", 1), ("gy", 1))


def shift_from(face, axis, step):
    count = lax.axis_size(axis)
    return lax.ppermute(face, axis, [(i, (i + step) % count) for i in range(count)])


def group_sum(x, axis, lo, bits):
    count = lax.axis_size(axis)
    parts = [x]
    for m in range(1, 1 << bits):
        mask = m << lo
        parts.append(lax.ppermute(x, axis, [(i, i ^ mask) for i in range(count)]))
    while len(parts) > 1:
        parts = [parts[2 * k] + parts[2 * k + 1] for k in range(len(parts) // 2)]
    return parts[0]


def all_sum(x):
    for axis, chunk in GROUP_BITS:
        bits = lax.axis_size(axis).bit_length() - 1
        lo = 0
        while lo < bits:
            step = min(chunk, bits - lo)
            x = group_sum(x, axis, lo, step)
            lo += step
    return x


def from_blocks(blocks, sizex, sizey, sizez):
    lead = blocks.shape[:-2]
    count = len(lead)
    shaped = blocks.reshape(lead + (sizex // 4, sizey // 4, sizez // 4, 4, 4, 4))
    order = list(range(count)) + [count, count + 3, count + 1, count + 4, count + 2, count + 5]
    return shaped.transpose(order).reshape(lead + (sizex, sizey, sizez))


def padded_of(center, xlo, xhi, ylo, yhi):
    sizez = center.shape[-1]
    corner = jnp.zeros(center.shape[:-3] + (1, 1, sizez), center.dtype)
    mid = jnp.concatenate([ylo[..., :, None, :], center, yhi[..., :, None, :]], axis=-2)
    top = jnp.concatenate([corner, xlo[..., None, :, :], corner], axis=-2)
    bot = jnp.concatenate([corner, xhi[..., None, :, :], corner], axis=-2)
    return jnp.concatenate([top, mid, bot], axis=-3)


def padded_laplace(padded):
    center = padded[1:-1, 1:-1]
    total = padded[2:, 1:-1] + padded[:-2, 1:-1] + padded[1:-1, 2:] + padded[1:-1, :-2]
    total = total + jnp.roll(center, -1, 2) + jnp.roll(center, 1, 2)
    return total - 6.0 * center


def body(velocity, cotangent, block_ids, fluid_count, fluid_cells, w_in, w_mid, w_out):
    sizex, sizey, sizez = velocity.shape
    slots = block_ids.shape[2]
    nblocks = sizex * sizey * sizez // 64
    cells = sizex * sizey * sizez

    both = jnp.stack([velocity, cotangent])
    xlo = shift_from(both[:, -1], "gx", 1)
    xhi = shift_from(both[:, 0], "gx", -1)
    ylo = shift_from(both[:, :, -1], "gy", 1)
    yhi = shift_from(both[:, :, 0], "gy", -1)
    padded = padded_of(velocity, xlo[0], xhi[0], ylo[0], yhi[0])
    cot_pad = padded_of(cotangent, xlo[1], xhi[1], ylo[1], yhi[1])

    ids = block_ids.reshape(slots)
    live = (jnp.arange(slots) < fluid_count[0, 0]).astype(jnp.bfloat16)
    slot_w = fluid_cells.reshape(slots, 64).astype(jnp.bfloat16) * live[:, None]
    onehot = (ids[:, None] == jnp.arange(nblocks)[None, :]).astype(jnp.bfloat16)
    block_w = lax.dot_general(onehot, slot_w, (((0,), (0,)), ((), ())), preferred_element_type=jnp.float32)
    weight = from_blocks(block_w, sizex, sizey, sizez).reshape(cells)

    center = padded[1:-1, 1:-1]
    chosen = jnp.stack(
        [
            center,
            padded[2:, 1:-1],
            padded[:-2, 1:-1],
            padded[1:-1, 2:],
            padded[1:-1, :-2],
            jnp.roll(center, -1, 2),
            jnp.roll(center, 1, 2),
        ]
    ).astype(jnp.bfloat16).reshape(7, cells)
    h1 = jnp.tanh(jnp.dot(w_in, chosen, preferred_element_type=jnp.float32)).astype(jnp.bfloat16)
    h2 = jnp.tanh(jnp.dot(w_mid, h1, preferred_element_type=jnp.float32)).astype(jnp.bfloat16)
    corr = jnp.dot(w_out, h2, preferred_element_type=jnp.float32)[0] * weight
    dcl = (cotangent.reshape(cells) * weight).astype(jnp.bfloat16)
    h2f = h2.astype(jnp.float32)
    h1f = h1.astype(jnp.float32)
    dh2 = jnp.dot(w_out.T, dcl[None, :], preferred_element_type=jnp.float32)
    da2 = (dh2 * (1.0 - h2f * h2f)).astype(jnp.bfloat16)
    dh1 = jnp.dot(w_mid.T, da2, preferred_element_type=jnp.float32)
    da1 = (dh1 * (1.0 - h1f * h1f)).astype(jnp.bfloat16)
    dfeat = jnp.dot(w_in.T, da1, preferred_element_type=jnp.float32).reshape(7, sizex, sizey, sizez)
    dims = (((1,), (1,)), ((), ()))
    gin = lax.dot_general(da1, chosen, dims, preferred_element_type=jnp.float32)
    gmid = lax.dot_general(da2, h1, dims, preferred_element_type=jnp.float32)
    gout = lax.dot_general(dcl[None, :], h2, dims, preferred_element_type=jnp.float32)

    new_field = velocity + viscosity * padded_laplace(padded) + corr.reshape(sizex, sizey, sizez)

    from_xlo = shift_from(dfeat[1, -1], "gx", 1)
    from_xhi = shift_from(dfeat[2, 0], "gx", -1)
    from_ylo = shift_from(dfeat[3, :, -1], "gy", 1)
    from_yhi = shift_from(dfeat[4, :, 0], "gy", -1)
    side1 = jnp.concatenate([from_xlo[None], dfeat[1, :-1]], axis=0)
    side2 = jnp.concatenate([dfeat[2, 1:], from_xhi[None]], axis=0)
    side3 = jnp.concatenate([from_ylo[:, None], dfeat[3, :, :-1]], axis=1)
    side4 = jnp.concatenate([dfeat[4, :, 1:], from_yhi[:, None]], axis=1)
    local = dfeat[0] + jnp.roll(dfeat[5], 1, 2) + jnp.roll(dfeat[6], -1, 2)
    grad_field = cotangent + viscosity * padded_laplace(cot_pad) + local + (side1 + side2 + side3 + side4)

    flat = jnp.concatenate([gin.reshape(-1), gmid.reshape(-1), gout.reshape(-1)])
    total = all_sum(flat)
    scale = 1.0 / jnp.sqrt(jnp.float32(lax.axis_size("gx") * lax.axis_size("gy") * slots * 64))
    total = total * scale
    width = gmid.shape[0]
    grad_in = total[: width * 7].reshape(width, 7)
    grad_mid = total[width * 7 : width * 7 + width * width].reshape(width, width)
    grad_out = total[width * 7 + width * width :].reshape(1, width)
    return (new_field, grad_field, grad_in, grad_mid, grad_out)


def solution(mesh):
    in_specs = (
        P("gx", "gy", None),
        P("gx", "gy", None),
        P("gx", "gy", None),
        P("gx", "gy"),
        P("gx", "gy", None),
        P(),
        P(),
        P(),
    )
    out_specs = (P("gx", "gy", None), P("gx", "gy", None), P(), P(), P())
    return jax.shard_map(body, mesh=mesh, in_specs=in_specs, out_specs=out_specs, check_vma=False)
```

time: 235 us -> 130 us (0.55); the launches traced: 230 us -> 129 us
  blocking collectives: 117 us -> 0 us
  waiting for transfers between devices: 2.02 us -> 35.1 us
  local copies, waits for them, and re-layouts: 42.1 us -> 9.03 us
  starting transfers between devices: 48.1 us -> 75.7 us
  other arithmetic: 13.2 us -> 2.6 us
    psum x1 -> x0, blocking collectives: 117 us -> none  [body(): total = lax.psum(flat, ('gx', 'gy'))]
    ppermute x8 -> x18, waiting for transfers between devices: 2.02 us -> 35.1 us  [the longest x10 35 us: group_sum(): parts.append(lax.ppermute(x, axis, [(i, i ^ mask) for i in range(count)]))]
    ppermute x8 -> x18, starting transfers between devices: 48.1 us -> 75.7 us  [the longest x8 45.6 us: shift_from(): lax.ppermute(face, axis, [(i, (i + step) % count) for i in range(count)])]
    slice x12 -> x8, local copies, waits for them, and re-layouts: 11.4 us -> 0.25 us  [the longest x3 0.22 us: body(): local = dfeat[0] + jnp.roll(dfeat[5], 1, 2) + jnp.roll(dfeat[6], -1, 2)]
    another operation x16 -> x12, local copies, waits for them, and re-layouts: 11.2 us -> 2.51 us  [the longest x2 1.29 us: body(): weight = from_blocks(block_w, sizex, sizey, sizez).reshape(cells)]
    scatter-add x2 -> x0, other arithmetic: 6.45 us -> none  [the longest x1 5.09 us: closure_tile(): jnp.zeros((7, nblocks, 64), jnp.float32).at[:, ids]]
    reshape x10 -> x0, local copies, waits for them, and re-layouts: 4.51 us -> none  [the longest x1 1.83 us: to_blocks(): shaped = field.reshape(lead + (sizex // 4, 4, sizey // 4, 4, sizez // 4, 4))]
    dot_general x7 -> x9, matrix products: 5.93 us -> 5.01 us  [the longest x1 0.93 us: body(): lax.dot_general(onehot, slot_w, (((0,), (0,)), ((), ())), preferred_eleme...]
  transfers between devices with their start and end apart: 8 -> 18, of which waited for: 2 -> 9; matrix products, arithmetic and copies ran while one was open for 6% -> 8% of each run, Pallas kernels for 0% -> 0%
where the time goes in v1:
time: 130 us; the launch traced here: 129 us
  starting transfers between devices  75.7 us (58%)
  waiting for transfers between devices  35.1 us (27%)
  local copies, waits for them, and re-layouts  9.03 us (7%)
  matrix products  5.01 us (4%)
  other arithmetic  2.6 us (2%)
  between operations  1.91 us (1%)
    ppermute x8, starting transfers between devices, shift_from(): lax.ppermute(face, axis, [(i, (i + step) % count) for i in range(count)])  45.6 us
    ppermute x10, waiting for transfers between devices, group_sum(): parts.append(lax.ppermute(x, axis, [(i, i ^ mask) for i in range(count)]))  35 us
    ppermute x10, starting transfers between devices, group_sum(): parts.append(lax.ppermute(x, axis, [(i, i ^ mask) for i in range(count)]))  30.2 us
    slice x4, local copies, waits for them, and re-layouts, padded_laplace(): total = total + jnp.roll(center, -1, 2) + jnp.roll(center, 1, 2)  2.8 us
  transfers between devices with their start and end apart: 18, of which 9 were waited for; matrix products, arithmetic and copies ran while one was open for 8% of the time, Pallas kernels for 0%

profile of v1, /device:TPU:14, one launch (start us, length us, event | category | flops | bytes accessed | tf_op | source)
XLA Modules:
  0.0 129.3 jit_solution(13030406088635573582)
XLA Ops:
  1.5 8.2 %collective-permute-start = (f32[2,8,128]{2,1,0:T(8,128)S(1)}, f32[2,8,128]{2,1,0:T(8,128)S(1)}, u32[]{:S(2)}, u32[]{:S(2)}) collective-permute-start(f32[2,8,128]{2,1,0:T(8,128)S(1)} %get-tuple-element.28), channel_id=1, source_target_pairs={{0,1},{1,2},{2,3},{3,4},{4,5},{5,6},{6,7},{7,8},{8,9},{9,10},{10,1... | collective-permute-start | bytes 24584 | tf_op jit(solution)/shard_map/ppermute | solution.py:13
  9.7 16.8 %collective-permute-start.1 = (f32[2,8,128]{2,1,0:T(8,128)S(1)}, f32[2,8,128]{2,1,0:T(8,128)S(1)}, u32[]{:S(2)}, u32[]{:S(2)}) collective-permute-start(f32[2,8,128]{2,1,0:T(8,128)S(1)} %get-tuple-element.29), channel_id=1, source_target_pairs={{0,15},{1,0},{2,1},{3,2},{4,3},{5,4},{6,5},{7,6},{8,7},{9,8},{10,9... | collective-permute-start | bytes 24584 | tf_op jit(solution)/shard_map/ppermute | solution.py:13
  26.4 2.5 %collective-permute-start.2 = (f32[2,8,128]{2,0,1:T(2,128)S(1)}, f32[2,8,128]{2,0,1:T(2,128)S(1)}, u32[]{:S(2)}, u32[]{:S(2)}) collective-permute-start(f32[2,8,128]{2,0,1:T(2,128)S(1)} %bitcast.151), channel_id=1, source_target_pairs={{0,1008},{16,0},{32,16},{48,32},{64,48},{80,64},{96,80},{112,96},{... | collective-permute-start | bytes 24584 | tf_op jit(solution)/shard_map/ppermute | solution.py:13
  29.0 1.9 %collective-permute-start.3 = (f32[2,8,128]{2,0,1:T(2,128)S(1)}, f32[2,8,128]{2,0,1:T(2,128)S(1)}, u32[]{:S(2)}, u32[]{:S(2)}) collective-permute-start(f32[2,8,128]{2,0,1:T(2,128)S(1)} %bitcast.150), channel_id=1, source_target_pairs={{0,16},{16,32},{32,48},{48,64},{64,80},{80,96},{96,112},{112,128},... | collective-permute-start | bytes 24584 | tf_op jit(solution)/shard_map/ppermute | solution.py:13
  42.5 4.7 %collective-permute-start.8 = (f32[4608]{0:T(1024)S(1)}, f32[4608]{0:T(1024)S(1)}, u32[]{:S(2)}, u32[]{:S(2)}) collective-permute-start(f32[4608]{0:T(1024)S(1)} %concatenate.107), channel_id=1, source_target_pairs={{0,16},{16,0},{32,48},{48,32},{64,80},{80,64},{96,112},{112,96},{1... | collective-permute-start | bytes 55304 | tf_op jit(solution)/shard_map/ppermute | solution.py:21
  50.2 3.5 %collective-permute-done.9 = f32[4608]{0:T(1024)S(1)} collective-permute-done((f32[4608]{0:T(1024)S(1)}, f32[4608]{0:T(1024)S(1)}, u32[]{:S(2)}, u32[]{:S(2)}) %collective-permute-start.9) | collective-permute-done | bytes 18464 | tf_op jit(solution)/shard_map/ppermute | solution.py:21
  53.7 2.1 %collective-permute-start.10 = (f32[4608]{0:T(1024)S(1)}, f32[4608]{0:T(1024)S(1)}, u32[]{:S(2)}, u32[]{:S(2)}) collective-permute-start(f32[4608]{0:T(1024)S(1)} %add.119), channel_id=1, source_target_pairs={{0,64},{16,80},{32,96},{48,112},{64,0},{80,16},{96,32},{112,48},{1... | collective-permute-start | bytes 55304 | tf_op jit(solution)/shard_map/ppermute | solution.py:21
  55.9 4.3 %collective-permute-done.10 = f32[4608]{0:T(1024)S(1)} collective-permute-done((f32[4608]{0:T(1024)S(1)}, f32[4608]{0:T(1024)S(1)}, u32[]{:S(2)}, u32[]{:S(2)}) %collective-permute-start.10) | collective-permute-done | bytes 18464 | tf_op jit(solution)/shard_map/ppermute | solution.py:21
  60.3 4.5 %collective-permute-start.11 = (f32[4608]{0:T(1024)S(1)}, f32[4608]{0:T(1024)S(1)}, u32[]{:S(2)}, u32[]{:S(2)}) collective-permute-start(f32[4608]{0:T(1024)S(1)} %add.120), channel_id=1, source_target_pairs={{0,128},{16,144},{32,160},{48,176},{64,192},{80,208},{96,224},{112... | collective-permute-start | bytes 55304 | tf_op jit(solution)/shard_map/ppermute | solution.py:21
  64.8 5.1 %collective-permute-done.11 = f32[4608]{0:T(1024)S(1)} collective-permute-done((f32[4608]{0:T(1024)S(1)}, f32[4608]{0:T(1024)S(1)}, u32[]{:S(2)}, u32[]{:S(2)}) %collective-permute-start.11) | collective-permute-done | bytes 18464 | tf_op jit(solution)/shard_map/ppermute | solution.py:21
  69.9 2.7 %collective-permute-start.12 = (f32[4608]{0:T(1024)S(1)}, f32[4608]{0:T(1024)S(1)}, u32[]{:S(2)}, u32[]{:S(2)}) collective-permute-start(f32[4608]{0:T(1024)S(1)} %add.121), channel_id=1, source_target_pairs={{0,256},{16,272},{32,288},{48,304},{64,320},{80,336},{96,352},{112... | collective-permute-start | bytes 55304 | tf_op jit(solution)/shard_map/ppermute | solution.py:21
  72.6 1.9 %collective-permute-start.6 = (f32[8,128]{1,0:T(8,128)S(1)}, f32[8,128]{1,0:T(8,128)S(1)}, u32[]{:S(2)}, u32[]{:S(2)}) collective-permute-start(f32[8,128]{1,0:T(8,128)S(1)} %bitcast.157), channel_id=1, source_target_pairs={{0,1},{1,2},{2,3},{3,4},{4,5},{5,6},{6,7},{7,8},{8,9},{9,10},{10,1... | collective-permute-start | bytes 12296 | tf_op jit(solution)/shard_map/ppermute | solution.py:13
  74.5 9.9 %collective-permute-start.7 = (f32[8,128]{1,0:T(8,128)S(1)}, f32[8,128]{1,0:T(8,128)S(1)}, u32[]{:S(2)}, u32[]{:S(2)}) collective-permute-start(f32[8,128]{1,0:T(8,128)S(1)} %bitcast.156), channel_id=1, source_target_pairs={{0,15},{1,0},{2,1},{3,2},{4,3},{5,4},{6,5},{7,6},{8,7},{9,8},{10,9... | collective-permute-start | bytes 12296 | tf_op jit(solution)/shard_map/ppermute | solution.py:13
  84.4 1.9 %collective-permute-start.5 = (f32[8,128]{1,0:T(8,128)S(1)}, f32[8,128]{1,0:T(8,128)S(1)}, u32[]{:S(2)}, u32[]{:S(2)}) collective-permute-start(f32[8,128]{1,0:T(8,128)S(1)} %get-tuple-element.24), channel_id=1, source_target_pairs={{0,1008},{16,0},{32,16},{48,32},{64,48},{80,64},{96,80},{112,96},{... | collective-permute-start | bytes 12296 | tf_op jit(solution)/shard_map/ppermute | solution.py:13
  86.4 2.4 %collective-permute-start.4 = (f32[8,128]{1,0:T(8,128)S(1)}, f32[8,128]{1,0:T(8,128)S(1)}, u32[]{:S(2)}, u32[]{:S(2)}) collective-permute-start(f32[8,128]{1,0:T(8,128)S(1)} %get-tuple-element.25), channel_id=1, source_target_pairs={{0,16},{16,32},{32,48},{48,64},{64,80},{80,96},{96,112},{112,128},... | collective-permute-start | bytes 12296 | tf_op jit(solution)/shard_map/ppermute | solution.py:13
  89.1 4.7 %collective-permute-start.13 = (f32[4608]{0:T(1024)S(1)}, f32[4608]{0:T(1024)S(1)}, u32[]{:S(2)}, u32[]{:S(2)}) collective-permute-start(f32[4608]{0:T(1024)S(1)} %add.122), channel_id=1, source_target_pairs={{0,512},{16,528},{32,544},{48,560},{64,576},{80,592},{96,608},{112... | collective-permute-start | bytes 55304 | tf_op jit(solution)/shard_map/ppermute | solution.py:21
  95.7 1.9 %collective-permute-start.14 = (f32[4608]{0:T(1024)S(1)}, f32[4608]{0:T(1024)S(1)}, u32[]{:S(2)}, u32[]{:S(2)}) collective-permute-start(f32[4608]{0:T(1024)S(1)} %add.123), channel_id=1, source_target_pairs={{0,1},{1,0},{2,3},{3,2},{4,5},{5,4},{6,7},{7,6},{8,9},{9,8},{10,11... | collective-permute-start | bytes 55304 | tf_op jit(solution)/shard_map/ppermute | solution.py:21
  98.3 7.1 %collective-permute-done.14 = f32[4608]{0:T(1024)S(1)} collective-permute-done((f32[4608]{0:T(1024)S(1)}, f32[4608]{0:T(1024)S(1)}, u32[]{:S(2)}, u32[]{:S(2)}) %collective-permute-start.14) | collective-permute-done | bytes 18464 | tf_op jit(solution)/shard_map/ppermute | solution.py:21
  105.4 1.9 %collective-permute-start.15 = (f32[4608]{0:T(1024)S(1)}, f32[4608]{0:T(1024)S(1)}, u32[]{:S(2)}, u32[]{:S(2)}) collective-permute-start(f32[4608]{0:T(1024)S(1)} %add.124), channel_id=1, source_target_pairs={{0,2},{1,3},{2,0},{3,1},{4,6},{5,7},{6,4},{7,5},{8,10},{9,11},{10,... | collective-permute-start | bytes 55304 | tf_op jit(solution)/shard_map/ppermute | solution.py:21
  107.3 3.7 %collective-permute-done.15 = f32[4608]{0:T(1024)S(1)} collective-permute-done((f32[4608]{0:T(1024)S(1)}, f32[4608]{0:T(1024)S(1)}, u32[]{:S(2)}, u32[]{:S(2)}) %collective-permute-start.15) | collective-permute-done | bytes 18464 | tf_op jit(solution)/shard_map/ppermute | solution.py:21
  111.0 1.9 %collective-permute-start.16 = (f32[4608]{0:T(1024)S(1)}, f32[4608]{0:T(1024)S(1)}, u32[]{:S(2)}, u32[]{:S(2)}) collective-permute-start(f32[4608]{0:T(1024)S(1)} %add.125), channel_id=1, source_target_pairs={{0,4},{1,5},{2,6},{3,7},{4,0},{5,1},{6,2},{7,3},{8,12},{9,13},{10,... | collective-permute-start | bytes 55304 | tf_op jit(solution)/shard_map/ppermute | solution.py:21
  113.1 4.5 %collective-permute-done.16 = f32[4608]{0:T(1024)S(1)} collective-permute-done((f32[4608]{0:T(1024)S(1)}, f32[4608]{0:T(1024)S(1)}, u32[]{:S(2)}, u32[]{:S(2)}) %collective-permute-start.16) | collective-permute-done | bytes 18464 | tf_op jit(solution)/shard_map/ppermute | solution.py:21
  117.6 3.9 %collective-permute-start.17 = (f32[4608]{0:T(1024)S(1)}, f32[4608]{0:T(1024)S(1)}, u32[]{:S(2)}, u32[]{:S(2)}) collective-permute-start(f32[4608]{0:T(1024)S(1)} %add.126), channel_id=1, source_target_pairs={{0,8},{1,9},{2,10},{3,11},{4,12},{5,13},{6,14},{7,15},{8,0},{9,1},... | collective-permute-start | bytes 55304 | tf_op jit(solution)/shard_map/ppermute | solution.py:21
  122.3 4.9 %collective-permute-done.17 = f32[4608]{0:T(1024)S(1)} collective-permute-done((f32[4608]{0:T(1024)S(1)}, f32[4608]{0:T(1024)S(1)}, u32[]{:S(2)}, u32[]{:S(2)}) %collective-permute-start.17) | collective-permute-done | bytes 18464 | tf_op jit(solution)/shard_map/ppermute | solution.py:21
  (102 shorter events, 20.5 us)
Async XLA Ops:
  0.6 38.8 %copy-start = (bf16[64,64]{1,0:T(8,128)(2,1)S(1)}, bf16[64,64]{1,0:T(8,128)(2,1)}, u32[]{:S(2)}) copy-start(bf16[64,64]{1,0:T(8,128)(2,1)} %param.14) | copy-start | bytes 24580
  1.5 36.9 %collective-permute-start = (f32[2,8,128]{2,1,0:T(8,128)S(1)}, f32[2,8,128]{2,1,0:T(8,128)S(1)}, u32[]{:S(2)}, u32[]{:S(2)}) collective-permute-start(f32[2,8,128]{2,1,0:T(8,128)S(1)} %get-tuple-element.28), channel_id=1, source_target_pairs={{0,1},{1,2},{2,3},{3,4},{4,5},{5,6},{6,7},{7,8},{8,9},{9,10},{10,1... | collective-permute-start | bytes 24584 | tf_op jit(solution)/shard_map/ppermute | solution.py:13
  9.7 28.9 %collective-permute-start.1 = (f32[2,8,128]{2,1,0:T(8,128)S(1)}, f32[2,8,128]{2,1,0:T(8,128)S(1)}, u32[]{:S(2)}, u32[]{:S(2)}) collective-permute-start(f32[2,8,128]{2,1,0:T(8,128)S(1)} %get-tuple-element.29), channel_id=1, source_target_pairs={{0,15},{1,0},{2,1},{3,2},{4,3},{5,4},{6,5},{7,6},{8,7},{9,8},{10,9... | collective-permute-start | bytes 24584 | tf_op jit(solution)/shard_map/ppermute | solution.py:13
  26.4 11.9 %collective-permute-start.2 = (f32[2,8,128]{2,0,1:T(2,128)S(1)}, f32[2,8,128]{2,0,1:T(2,128)S(1)}, u32[]{:S(2)}, u32[]{:S(2)}) collective-permute-start(f32[2,8,128]{2,0,1:T(2,128)S(1)} %bitcast.151), channel_id=1, source_target_pairs={{0,1008},{16,0},{32,16},{48,32},{64,48},{80,64},{96,80},{112,96},{... | collective-permute-start | bytes 24584 | tf_op jit(solution)/shard_map/ppermute | solution.py:13
  29.0 9.5 %collective-permute-start.3 = (f32[2,8,128]{2,0,1:T(2,128)S(1)}, f32[2,8,128]{2,0,1:T(2,128)S(1)}, u32[]{:S(2)}, u32[]{:S(2)}) collective-permute-start(f32[2,8,128]{2,0,1:T(2,128)S(1)} %bitcast.150), channel_id=1, source_target_pairs={{0,16},{16,32},{32,48},{48,64},{64,80},{80,96},{96,112},{112,128},... | collective-permute-start | bytes 24584 | tf_op jit(solution)/shard_map/ppermute | solution.py:13
  36.8 1.3 %copy-start.4 = (bf16[1,64]{1,0:T(2,128)(2,1)S(1)}, bf16[1,64]{1,0:T(2,128)(2,1)}, u32[]{:S(2)}) copy-start(bf16[1,64]{1,0:T(2,128)(2,1)} %param.15) | copy-start | bytes 388
  36.8 1.3 %copy-start.1 = (f32[8,8,128]{2,1,0:T(8,128)S(1)}, f32[8,8,128]{2,1,0:T(8,128)}, u32[]{:S(2)}) copy-start(f32[8,8,128]{2,1,0:T(8,128)} %param.9) | copy-start | bytes 98308
  36.8 1.4 %copy-start.2 = (f32[8,8,128]{2,1,0:T(8,128)S(1)}, f32[8,8,128]{2,1,0:T(8,128)}, u32[]{:S(2)}) copy-start(f32[8,8,128]{2,1,0:T(8,128)} %param.8) | copy-start | bytes 98308
  37.5 1.5 %copy-start.3 = (bf16[64,7]{0,1:T(8,128)(2,1)S(1)}, bf16[64,7]{0,1:T(8,128)(2,1)}, u32[]{:S(2)}) copy-start(bf16[64,7]{0,1:T(8,128)(2,1)} %param.13) | copy-start | bytes 2692
  42.5 5.5 %collective-permute-start.8 = (f32[4608]{0:T(1024)S(1)}, f32[4608]{0:T(1024)S(1)}, u32[]{:S(2)}, u32[]{:S(2)}) collective-permute-start(f32[4608]{0:T(1024)S(1)} %concatenate.107), channel_id=1, source_target_pairs={{0,16},{16,0},{32,48},{48,32},{64,80},{80,64},{96,112},{112,96},{1... | collective-permute-start | bytes 55304 | tf_op jit(solution)/shard_map/ppermute | solution.py:21
  48.0 5.7 %collective-permute-start.9 = (f32[4608]{0:T(1024)S(1)}, f32[4608]{0:T(1024)S(1)}, u32[]{:S(2)}, u32[]{:S(2)}) collective-permute-start(f32[4608]{0:T(1024)S(1)} %add.118), channel_id=1, source_target_pairs={{0,32},{16,48},{32,0},{48,16},{64,96},{80,112},{96,64},{112,80},{1... | collective-permute-start | bytes 55304 | tf_op jit(solution)/shard_map/ppermute | solution.py:21
  53.7 6.6 %collective-permute-start.10 = (f32[4608]{0:T(1024)S(1)}, f32[4608]{0:T(1024)S(1)}, u32[]{:S(2)}, u32[]{:S(2)}) collective-permute-start(f32[4608]{0:T(1024)S(1)} %add.119), channel_id=1, source_target_pairs={{0,64},{16,80},{32,96},{48,112},{64,0},{80,16},{96,32},{112,48},{1... | collective-permute-start | bytes 55304 | tf_op jit(solution)/shard_map/ppermute | solution.py:21
  60.3 9.6 %collective-permute-start.11 = (f32[4608]{0:T(1024)S(1)}, f32[4608]{0:T(1024)S(1)}, u32[]{:S(2)}, u32[]{:S(2)}) collective-permute-start(f32[4608]{0:T(1024)S(1)} %add.120), channel_id=1, source_target_pairs={{0,128},{16,144},{32,160},{48,176},{64,192},{80,208},{96,224},{112... | collective-permute-start | bytes 55304 | tf_op jit(solution)/shard_map/ppermute | solution.py:21
  69.9 19.2 %collective-permute-start.12 = (f32[4608]{0:T(1024)S(1)}, f32[4608]{0:T(1024)S(1)}, u32[]{:S(2)}, u32[]{:S(2)}) collective-permute-start(f32[4608]{0:T(1024)S(1)} %add.121), channel_id=1, source_target_pairs={{0,256},{16,272},{32,288},{48,304},{64,320},{80,336},{96,352},{112... | collective-permute-start | bytes 55304 | tf_op jit(solution)/shard_map/ppermute | solution.py:21
  72.6 48.9 %collective-permute-start.6 = (f32[8,128]{1,0:T(8,128)S(1)}, f32[8,128]{1,0:T(8,128)S(1)}, u32[]{:S(2)}, u32[]{:S(2)}) collective-permute-start(f32[8,128]{1,0:T(8,128)S(1)} %bitcast.157), channel_id=1, source_target_pairs={{0,1},{1,2},{2,3},{3,4},{4,5},{5,6},{6,7},{7,8},{8,9},{9,10},{10,1... | collective-permute-start | bytes 12296 | tf_op jit(solution)/shard_map/ppermute | solution.py:13
  74.5 47.0 %collective-permute-start.7 = (f32[8,128]{1,0:T(8,128)S(1)}, f32[8,128]{1,0:T(8,128)S(1)}, u32[]{:S(2)}, u32[]{:S(2)}) collective-permute-start(f32[8,128]{1,0:T(8,128)S(1)} %bitcast.156), channel_id=1, source_target_pairs={{0,15},{1,0},{2,1},{3,2},{4,3},{5,4},{6,5},{7,6},{8,7},{9,8},{10,9... | collective-permute-start | bytes 12296 | tf_op jit(solution)/shard_map/ppermute | solution.py:13
  84.4 37.1 %collective-permute-start.5 = (f32[8,128]{1,0:T(8,128)S(1)}, f32[8,128]{1,0:T(8,128)S(1)}, u32[]{:S(2)}, u32[]{:S(2)}) collective-permute-start(f32[8,128]{1,0:T(8,128)S(1)} %get-tuple-element.24), channel_id=1, source_target_pairs={{0,1008},{16,0},{32,16},{48,32},{64,48},{80,64},{96,80},{112,96},{... | collective-permute-start | bytes 12296 | tf_op jit(solution)/shard_map/ppermute | solution.py:13
  86.4 35.1 %collective-permute-start.4 = (f32[8,128]{1,0:T(8,128)S(1)}, f32[8,128]{1,0:T(8,128)S(1)}, u32[]{:S(2)}, u32[]{:S(2)}) collective-permute-start(f32[8,128]{1,0:T(8,128)S(1)} %get-tuple-element.25), channel_id=1, source_target_pairs={{0,16},{16,32},{32,48},{48,64},{64,80},{80,96},{96,112},{112,128},... | collective-permute-start | bytes 12296 | tf_op jit(solution)/shard_map/ppermute | solution.py:13
  89.1 6.6 %collective-permute-start.13 = (f32[4608]{0:T(1024)S(1)}, f32[4608]{0:T(1024)S(1)}, u32[]{:S(2)}, u32[]{:S(2)}) collective-permute-start(f32[4608]{0:T(1024)S(1)} %add.122), channel_id=1, source_target_pairs={{0,512},{16,528},{32,544},{48,560},{64,576},{80,592},{96,608},{112... | collective-permute-start | bytes 55304 | tf_op jit(solution)/shard_map/ppermute | solution.py:21
  95.7 9.7 %collective-permute-start.14 = (f32[4608]{0:T(1024)S(1)}, f32[4608]{0:T(1024)S(1)}, u32[]{:S(2)}, u32[]{:S(2)}) collective-permute-start(f32[4608]{0:T(1024)S(1)} %add.123), channel_id=1, source_target_pairs={{0,1},{1,0},{2,3},{3,2},{4,5},{5,4},{6,7},{7,6},{8,9},{9,8},{10,11... | collective-permute-start | bytes 55304 | tf_op jit(solution)/shard_map/ppermute | solution.py:21
  105.4 5.7 %collective-permute-start.15 = (f32[4608]{0:T(1024)S(1)}, f32[4608]{0:T(1024)S(1)}, u32[]{:S(2)}, u32[]{:S(2)}) collective-permute-start(f32[4608]{0:T(1024)S(1)} %add.124), channel_id=1, source_target_pairs={{0,2},{1,3},{2,0},{3,1},{4,6},{5,7},{6,4},{7,5},{8,10},{9,11},{10,... | collective-permute-start | bytes 55304 | tf_op jit(solution)/shard_map/ppermute | solution.py:21
  111.0 6.6 %collective-permute-start.16 = (f32[4608]{0:T(1024)S(1)}, f32[4608]{0:T(1024)S(1)}, u32[]{:S(2)}, u32[]{:S(2)}) collective-permute-start(f32[4608]{0:T(1024)S(1)} %add.125), channel_id=1, source_target_pairs={{0,4},{1,5},{2,6},{3,7},{4,0},{5,1},{6,2},{7,3},{8,12},{9,13},{10,... | collective-permute-start | bytes 55304 | tf_op jit(solution)/shard_map/ppermute | solution.py:21
  117.6 9.6 %collective-permute-start.17 = (f32[4608]{0:T(1024)S(1)}, f32[4608]{0:T(1024)S(1)}, u32[]{:S(2)}, u32[]{:S(2)}) collective-permute-start(f32[4608]{0:T(1024)S(1)} %add.126), channel_id=1, source_target_pairs={{0,8},{1,9},{2,10},{3,11},{4,12},{5,13},{6,14},{7,15},{8,0},{9,1},... | collective-permute-start | bytes 55304 | tf_op jit(solution)/shard_map/ppermute | solution.py:21

commit v2 on v1

--- a/solution.py
+++ b/solution.py
@@ -4,8 +4,6 @@
 from jax.sharding import PartitionSpec as P
 
 viscosity = 0.1
-
-GROUP_BITS = (("gx", 1), ("gy", 1))
 
 
 def shift_from(face, axis, step):
@@ -24,14 +22,36 @@
     return parts[0]
 
 
+def torus_rounds():
+    def decode(i):
+        gx, gy = divmod(i, 16)
+        return {"core": gx % 2, "x": (gx // 2) % 8, "y": (gy % 2) * 4 + gx // 16, "z": gy // 2}
+
+    def encode(c):
+        return ((c["y"] % 4) * 16 + c["x"] * 2 + c["core"]) * 16 + c["z"] * 2 + c["y"] // 4
+
+    rounds = []
+    for ring, size in (("core", 2), ("x", 8), ("y", 8), ("z", 8)):
+        steps = [(lambda v, b=b: v ^ b) for b in (1, 2, 4, 8) if 2 * b < size]
+        steps.append(lambda v, size=size: size - 1 - v)
+        for step in steps:
+            pairs = []
+            for i in range(1024):
+                c = decode(i)
+                c[ring] = step(c[ring])
+                pairs.append((i, encode(c)))
+            rounds.append(pairs)
+    return rounds
+
+
 def all_sum(x):
-    for axis, chunk in GROUP_BITS:
-        bits = lax.axis_size(axis).bit_length() - 1
-        lo = 0
-        while lo < bits:
-            step = min(chunk, bits - lo)
-            x = group_sum(x, axis, lo, step)
-            lo += step
+    if (lax.axis_size("gx"), lax.axis_size("gy")) == (64, 16):
+        for pairs in torus_rounds():
+            x = x + lax.ppermute(x, ("gx", "gy"), pairs)
+        return x
+    for axis in ("gx", "gy"):
+        for lo in range(lax.axis_size(axis).bit_length() - 1):
+            x = group_sum(x, axis, lo, 1)
     return x
 
 
@@ -114,6 +134,10 @@
     from_xhi = shift_from(dfeat[2, 0], "gx", -1)
     from_ylo = shift_from(dfeat[3, :, -1], "gy", 1)
     from_yhi = shift_from(dfeat[4, :, 0], "gy", -1)
+
+    flat = jnp.concatenate([gin.reshape(-1), gmid.reshape(-1), gout.reshape(-1)])
+    flat, from_xlo, from_xhi, from_ylo, from_yhi = lax.optimization_barrier((flat, from_xlo, from_xhi, from_ylo, from_yhi))
+    total = all_sum(flat)
     side1 = jnp.concatenate([from_xlo[None], dfeat[1, :-1]], axis=0)
     side2 = jnp.concatenate([dfeat[2, 1:], from_xhi[None]], axis=0)
     side3 = jnp.concatenate([from_ylo[:, None], dfeat[3, :, :-1]], axis=1)
@@ -121,8 +145,6 @@
     local = dfeat[0] + jnp.roll(dfeat[5], 1, 2) + jnp.roll(dfeat[6], -1, 2)
     grad_field = cotangent + viscosity * padded_laplace(cot_pad) + local + (side1 + side2 + side3 + side4)
 
-    flat = jnp.concatenate([gin.reshape(-1), gmid.reshape(-1), gout.reshape(-1)])
-    total = all_sum(flat)
     scale = 1.0 / jnp.sqrt(jnp.float32(lax.axis_size("gx") * lax.axis_size("gy") * slots * 64))
     total = total * scale
     width = gmid.shape[0]

time: 130 us -> 131 us (level)
  starting transfers between devices: 75.7 us -> 86 us
  waiting for transfers between devices: 35.1 us -> 26.3 us
    ppermute x10, waiting for transfers between devices: 35 us -> 25.6 us  [all_sum(): x = x + lax.ppermute(x, ('gx', 'gy'), pairs)]
    ppermute x10, starting transfers between devices: 30.2 us -> 38.1 us  [all_sum(): x = x + lax.ppermute(x, ('gx', 'gy'), pairs)]
    ppermute x8, starting transfers between devices: 45.6 us -> 47.9 us  [shift_from(): lax.ppermute(face, axis, [(i, (i + step) % count) for i in range(count)])]
  transfers between devices with their start and end apart: 18 -> 18, of which waited for: 9 -> 11; matrix products, arithmetic and copies ran while one was open for 8% -> 7% of each run, Pallas kernels for 0% -> 0%
where the time goes in v2:
time: 131 us; the launch traced here: 130 us
  starting transfers between devices  86 us (66%)
  waiting for transfers between devices  26.3 us (20%)
  local copies, waits for them, and re-layouts  8.21 us (6%)
  matrix products  4.99 us (4%)
  other arithmetic  2.6 us (2%)
  between operations  1.89 us (1%)
    ppermute x8, starting transfers between devices, shift_from(): lax.ppermute(face, axis, [(i, (i + step) % count) for i in range(count)])  47.9 us
    ppermute x10, starting transfers between devices, all_sum(): x = x + lax.ppermute(x, ('gx', 'gy'), pairs)  38.1 us
    ppermute x10, waiting for transfers between devices, all_sum(): x = x + lax.ppermute(x, ('gx', 'gy'), pairs)  25.6 us
  transfers between devices with their start and end apart: 18, of which 11 were waited for; matrix products, arithmetic and copies ran while one was open for 7% of the time, Pallas kernels for 0%

profile of v2, /device:TPU:14, one launch (start us, length us, event | category | flops | bytes accessed | tf_op | source)
XLA Modules:
  0.0 129.9 jit_solution(13565802285564790636)
XLA Ops:
  1.5 8.2 %collective-permute-start = (f32[2,8,128]{2,1,0:T(8,128)S(1)}, f32[2,8,128]{2,1,0:T(8,128)S(1)}, u32[]{:S(2)}, u32[]{:S(2)}) collective-permute-start(f32[2,8,128]{2,1,0:T(8,128)S(1)} %get-tuple-element.38), channel_id=1, source_target_pairs={{0,1},{1,2},{2,3},{3,4},{4,5},{5,6},{6,7},{7,8},{8,9},{9,10},{10,1... | collective-permute-start | bytes 24584 | tf_op jit(solution)/shard_map/ppermute | solution.py:11
  9.7 16.8 %collective-permute-start.1 = (f32[2,8,128]{2,1,0:T(8,128)S(1)}, f32[2,8,128]{2,1,0:T(8,128)S(1)}, u32[]{:S(2)}, u32[]{:S(2)}) collective-permute-start(f32[2,8,128]{2,1,0:T(8,128)S(1)} %get-tuple-element.39), channel_id=1, source_target_pairs={{0,15},{1,0},{2,1},{3,2},{4,3},{5,4},{6,5},{7,6},{8,7},{9,8},{10,9... | collective-permute-start | bytes 24584 | tf_op jit(solution)/shard_map/ppermute | solution.py:11
  26.4 2.5 %collective-permute-start.2 = (f32[2,8,128]{2,0,1:T(2,128)S(1)}, f32[2,8,128]{2,0,1:T(2,128)S(1)}, u32[]{:S(2)}, u32[]{:S(2)}) collective-permute-start(f32[2,8,128]{2,0,1:T(2,128)S(1)} %bitcast.151), channel_id=1, source_target_pairs={{0,1008},{16,0},{32,16},{48,32},{64,48},{80,64},{96,80},{112,96},{... | collective-permute-start | bytes 24584 | tf_op jit(solution)/shard_map/ppermute | solution.py:11
  29.0 1.9 %collective-permute-start.3 = (f32[2,8,128]{2,0,1:T(2,128)S(1)}, f32[2,8,128]{2,0,1:T(2,128)S(1)}, u32[]{:S(2)}, u32[]{:S(2)}) collective-permute-start(f32[2,8,128]{2,0,1:T(2,128)S(1)} %bitcast.150), channel_id=1, source_target_pairs={{0,16},{16,32},{32,48},{48,64},{64,80},{80,96},{96,112},{112,128},... | collective-permute-start | bytes 24584 | tf_op jit(solution)/shard_map/ppermute | solution.py:11
  41.2 3.7 %collective-permute-start.5 = (f32[8,128]{1,0:T(8,128)S(1)}, f32[8,128]{1,0:T(8,128)S(1)}, u32[]{:S(2)}, u32[]{:S(2)}) collective-permute-start(f32[8,128]{1,0:T(8,128)S(1)} %get-tuple-element.34), channel_id=1, source_target_pairs={{0,1008},{16,0},{32,16},{48,32},{64,48},{80,64},{96,80},{112,96},{... | collective-permute-start | bytes 12296 | tf_op jit(solution)/shard_map/ppermute | solution.py:11
  44.9 3.0 %collective-permute-start.4 = (f32[8,128]{1,0:T(8,128)S(1)}, f32[8,128]{1,0:T(8,128)S(1)}, u32[]{:S(2)}, u32[]{:S(2)}) collective-permute-start(f32[8,128]{1,0:T(8,128)S(1)} %get-tuple-element.35), channel_id=1, source_target_pairs={{0,16},{16,32},{32,48},{48,64},{64,80},{80,96},{96,112},{112,128},... | collective-permute-start | bytes 12296 | tf_op jit(solution)/shard_map/ppermute | solution.py:11
  47.9 1.9 %collective-permute-start.6 = (f32[8,128]{1,0:T(8,128)S(1)}, f32[8,128]{1,0:T(8,128)S(1)}, u32[]{:S(2)}, u32[]{:S(2)}) collective-permute-start(f32[8,128]{1,0:T(8,128)S(1)} %bitcast.157), channel_id=1, source_target_pairs={{0,1},{1,2},{2,3},{3,4},{4,5},{5,6},{6,7},{7,8},{8,9},{9,10},{10,1... | collective-permute-start | bytes 12296 | tf_op jit(solution)/shard_map/ppermute | solution.py:11
  49.8 9.9 %collective-permute-start.7 = (f32[8,128]{1,0:T(8,128)S(1)}, f32[8,128]{1,0:T(8,128)S(1)}, u32[]{:S(2)}, u32[]{:S(2)}) collective-permute-start(f32[8,128]{1,0:T(8,128)S(1)} %bitcast.156), channel_id=1, source_target_pairs={{0,15},{1,0},{2,1},{3,2},{4,3},{5,4},{6,5},{7,6},{8,7},{9,8},{10,9... | collective-permute-start | bytes 12296 | tf_op jit(solution)/shard_map/ppermute | solution.py:11
  61.1 4.6 %collective-permute-start.8 = (f32[4608]{0:T(1024)S(1)}, f32[4608]{0:T(1024)S(1)}, u32[]{:S(2)}, u32[]{:S(2)}) collective-permute-start(f32[4608]{0:T(1024)S(1)} %concatenate.103), channel_id=1, source_target_pairs={{0,16},{1,17},{2,18},{3,19},{4,20},{5,21},{6,22},{7,23},{8,24},{9,... | collective-permute-start | bytes 55304 | tf_op jit(solution)/shard_map/ppermute | solution.py:50
  66.5 1.9 %collective-permute-start.9 = (f32[4608]{0:T(1024)S(1)}, f32[4608]{0:T(1024)S(1)}, u32[]{:S(2)}, u32[]{:S(2)}) collective-permute-start(f32[4608]{0:T(1024)S(1)} %add.118), channel_id=1, source_target_pairs={{0,32},{1,33},{2,34},{3,35},{4,36},{5,37},{6,38},{7,39},{8,40},{9,... | collective-permute-start | bytes 55304 | tf_op jit(solution)/shard_map/ppermute | solution.py:50
  68.4 3.7 %collective-permute-done.9 = f32[4608]{0:T(1024)S(1)} collective-permute-done((f32[4608]{0:T(1024)S(1)}, f32[4608]{0:T(1024)S(1)}, u32[]{:S(2)}, u32[]{:S(2)}) %collective-permute-start.9) | collective-permute-done | bytes 18464 | tf_op jit(solution)/shard_map/ppermute | solution.py:50
  72.2 1.9 %collective-permute-start.10 = (f32[4608]{0:T(1024)S(1)}, f32[4608]{0:T(1024)S(1)}, u32[]{:S(2)}, u32[]{:S(2)}) collective-permute-start(f32[4608]{0:T(1024)S(1)} %add.119), channel_id=1, source_target_pairs={{0,64},{1,65},{2,66},{3,67},{4,68},{5,69},{6,70},{7,71},{8,72},{9,... | collective-permute-start | bytes 55304 | tf_op jit(solution)/shard_map/ppermute | solution.py:50
  74.2 4.6 %collective-permute-done.10 = f32[4608]{0:T(1024)S(1)} collective-permute-done((f32[4608]{0:T(1024)S(1)}, f32[4608]{0:T(1024)S(1)}, u32[]{:S(2)}, u32[]{:S(2)}) %collective-permute-start.10) | collective-permute-done | bytes 18464 | tf_op jit(solution)/shard_map/ppermute | solution.py:50
  78.7 4.9 %collective-permute-start.11 = (f32[4608]{0:T(1024)S(1)}, f32[4608]{0:T(1024)S(1)}, u32[]{:S(2)}, u32[]{:S(2)}) collective-permute-start(f32[4608]{0:T(1024)S(1)} %add.120), channel_id=1, source_target_pairs={{0,224},{1,225},{2,226},{3,227},{4,228},{5,229},{6,230},{7,231},{8... | collective-permute-start | bytes 55304 | tf_op jit(solution)/shard_map/ppermute | solution.py:50
  83.7 1.9 %collective-permute-done.11 = f32[4608]{0:T(1024)S(1)} collective-permute-done((f32[4608]{0:T(1024)S(1)}, f32[4608]{0:T(1024)S(1)}, u32[]{:S(2)}, u32[]{:S(2)}) %collective-permute-start.11) | collective-permute-done | bytes 18464 | tf_op jit(solution)/shard_map/ppermute | solution.py:50
  85.6 2.7 %collective-permute-start.12 = (f32[4608]{0:T(1024)S(1)}, f32[4608]{0:T(1024)S(1)}, u32[]{:S(2)}, u32[]{:S(2)}) collective-permute-start(f32[4608]{0:T(1024)S(1)} %add.121), channel_id=1, source_target_pairs={{0,256},{1,257},{2,258},{3,259},{4,260},{5,261},{6,262},{7,263},{8... | collective-permute-start | bytes 55304 | tf_op jit(solution)/shard_map/ppermute | solution.py:50
  88.7 2.6 %collective-permute-done.12 = f32[4608]{0:T(1024)S(1)} collective-permute-done((f32[4608]{0:T(1024)S(1)}, f32[4608]{0:T(1024)S(1)}, u32[]{:S(2)}, u32[]{:S(2)}) %collective-permute-start.12) | collective-permute-done | bytes 18464 | tf_op jit(solution)/shard_map/ppermute | solution.py:50
  91.3 5.3 %collective-permute-start.13 = (f32[4608]{0:T(1024)S(1)}, f32[4608]{0:T(1024)S(1)}, u32[]{:S(2)}, u32[]{:S(2)}) collective-permute-start(f32[4608]{0:T(1024)S(1)} %add.122), channel_id=1, source_target_pairs={{0,512},{1,513},{2,514},{3,515},{4,516},{5,517},{6,518},{7,519},{8... | collective-permute-start | bytes 55304 | tf_op jit(solution)/shard_map/ppermute | solution.py:50
  98.4 1.9 %collective-permute-start.14 = (f32[4608]{0:T(1024)S(1)}, f32[4608]{0:T(1024)S(1)}, u32[]{:S(2)}, u32[]{:S(2)}) collective-permute-start(f32[4608]{0:T(1024)S(1)} %add.123), channel_id=1, source_target_pairs={{0,769},{1,768},{2,771},{3,770},{4,773},{5,772},{6,775},{7,774},{8... | collective-permute-start | bytes 55304 | tf_op jit(solution)/shard_map/ppermute | solution.py:50
  101.1 4.2 %collective-permute-done.14 = f32[4608]{0:T(1024)S(1)} collective-permute-done((f32[4608]{0:T(1024)S(1)}, f32[4608]{0:T(1024)S(1)}, u32[]{:S(2)}, u32[]{:S(2)}) %collective-permute-start.14) | collective-permute-done | bytes 18464 | tf_op jit(solution)/shard_map/ppermute | solution.py:50
  105.3 1.9 %collective-permute-start.15 = (f32[4608]{0:T(1024)S(1)}, f32[4608]{0:T(1024)S(1)}, u32[]{:S(2)}, u32[]{:S(2)}) collective-permute-start(f32[4608]{0:T(1024)S(1)} %add.124), channel_id=1, source_target_pairs={{0,2},{1,3},{2,0},{3,1},{4,6},{5,7},{6,4},{7,5},{8,10},{9,11},{10,... | collective-permute-start | bytes 55304 | tf_op jit(solution)/shard_map/ppermute | solution.py:50
  107.2 4.0 %collective-permute-done.15 = f32[4608]{0:T(1024)S(1)} collective-permute-done((f32[4608]{0:T(1024)S(1)}, f32[4608]{0:T(1024)S(1)}, u32[]{:S(2)}, u32[]{:S(2)}) %collective-permute-start.15) | collective-permute-done | bytes 18464 | tf_op jit(solution)/shard_map/ppermute | solution.py:50
  111.2 5.9 %collective-permute-start.16 = (f32[4608]{0:T(1024)S(1)}, f32[4608]{0:T(1024)S(1)}, u32[]{:S(2)}, u32[]{:S(2)}) collective-permute-start(f32[4608]{0:T(1024)S(1)} %add.125), channel_id=1, source_target_pairs={{0,4},{1,5},{2,6},{3,7},{4,0},{5,1},{6,2},{7,3},{8,12},{9,13},{10,... | collective-permute-start | bytes 55304 | tf_op jit(solution)/shard_map/ppermute | solution.py:50
  118.8 7.1 %collective-permute-start.17 = (f32[4608]{0:T(1024)S(1)}, f32[4608]{0:T(1024)S(1)}, u32[]{:S(2)}, u32[]{:S(2)}) collective-permute-start(f32[4608]{0:T(1024)S(1)} %add.126), channel_id=1, source_target_pairs={{0,14},{1,15},{2,12},{3,13},{4,10},{5,11},{6,8},{7,9},{8,6},{9,7},... | collective-permute-start | bytes 55304 | tf_op jit(solution)/shard_map/ppermute | solution.py:50
  (102 shorter events, 21.0 us)
Async XLA Ops:
  0.6 37.9 %copy-start = (bf16[64,64]{1,0:T(8,128)(2,1)S(1)}, bf16[64,64]{1,0:T(8,128)(2,1)}, u32[]{:S(2)}) copy-start(bf16[64,64]{1,0:T(8,128)(2,1)} %param.14) | copy-start | bytes 24580
  1.5 36.0 %collective-permute-start = (f32[2,8,128]{2,1,0:T(8,128)S(1)}, f32[2,8,128]{2,1,0:T(8,128)S(1)}, u32[]{:S(2)}, u32[]{:S(2)}) collective-permute-start(f32[2,8,128]{2,1,0:T(8,128)S(1)} %get-tuple-element.38), channel_id=1, source_target_pairs={{0,1},{1,2},{2,3},{3,4},{4,5},{5,6},{6,7},{7,8},{8,9},{9,10},{10,1... | collective-permute-start | bytes 24584 | tf_op jit(solution)/shard_map/ppermute | solution.py:11
  9.7 27.9 %collective-permute-start.1 = (f32[2,8,128]{2,1,0:T(8,128)S(1)}, f32[2,8,128]{2,1,0:T(8,128)S(1)}, u32[]{:S(2)}, u32[]{:S(2)}) collective-permute-start(f32[2,8,128]{2,1,0:T(8,128)S(1)} %get-tuple-element.39), channel_id=1, source_target_pairs={{0,15},{1,0},{2,1},{3,2},{4,3},{5,4},{6,5},{7,6},{8,7},{9,8},{10,9... | collective-permute-start | bytes 24584 | tf_op jit(solution)/shard_map/ppermute | solution.py:11
  26.4 11.0 %collective-permute-start.2 = (f32[2,8,128]{2,0,1:T(2,128)S(1)}, f32[2,8,128]{2,0,1:T(2,128)S(1)}, u32[]{:S(2)}, u32[]{:S(2)}) collective-permute-start(f32[2,8,128]{2,0,1:T(2,128)S(1)} %bitcast.151), channel_id=1, source_target_pairs={{0,1008},{16,0},{32,16},{48,32},{64,48},{80,64},{96,80},{112,96},{... | collective-permute-start | bytes 24584 | tf_op jit(solution)/shard_map/ppermute | solution.py:11
  29.0 8.6 %collective-permute-start.3 = (f32[2,8,128]{2,0,1:T(2,128)S(1)}, f32[2,8,128]{2,0,1:T(2,128)S(1)}, u32[]{:S(2)}, u32[]{:S(2)}) collective-permute-start(f32[2,8,128]{2,0,1:T(2,128)S(1)} %bitcast.150), channel_id=1, source_target_pairs={{0,16},{16,32},{32,48},{48,64},{64,80},{80,96},{96,112},{112,128},... | collective-permute-start | bytes 24584 | tf_op jit(solution)/shard_map/ppermute | solution.py:11
  35.9 1.3 %copy-start.4 = (bf16[1,64]{1,0:T(2,128)(2,1)S(1)}, bf16[1,64]{1,0:T(2,128)(2,1)}, u32[]{:S(2)}) copy-start(bf16[1,64]{1,0:T(2,128)(2,1)} %param.15) | copy-start | bytes 388
  35.9 1.3 %copy-start.1 = (f32[8,8,128]{2,1,0:T(8,128)S(1)}, f32[8,8,128]{2,1,0:T(8,128)}, u32[]{:S(2)}) copy-start(f32[8,8,128]{2,1,0:T(8,128)} %param.9) | copy-start | bytes 98308
  35.9 1.4 %copy-start.2 = (f32[8,8,128]{2,1,0:T(8,128)S(1)}, f32[8,8,128]{2,1,0:T(8,128)}, u32[]{:S(2)}) copy-start(f32[8,8,128]{2,1,0:T(8,128)} %param.8) | copy-start | bytes 98308
  36.6 1.5 %copy-start.3 = (bf16[64,7]{0,1:T(8,128)(2,1)S(1)}, bf16[64,7]{0,1:T(8,128)(2,1)}, u32[]{:S(2)}) copy-start(bf16[64,7]{0,1:T(8,128)(2,1)} %param.13) | copy-start | bytes 2692
  41.2 19.2 %collective-permute-start.5 = (f32[8,128]{1,0:T(8,128)S(1)}, f32[8,128]{1,0:T(8,128)S(1)}, u32[]{:S(2)}, u32[]{:S(2)}) collective-permute-start(f32[8,128]{1,0:T(8,128)S(1)} %get-tuple-element.34), channel_id=1, source_target_pairs={{0,1008},{16,0},{32,16},{48,32},{64,48},{80,64},{96,80},{112,96},{... | collective-permute-start | bytes 12296 | tf_op jit(solution)/shard_map/ppermute | solution.py:11
  44.9 15.6 %collective-permute-start.4 = (f32[8,128]{1,0:T(8,128)S(1)}, f32[8,128]{1,0:T(8,128)S(1)}, u32[]{:S(2)}, u32[]{:S(2)}) collective-permute-start(f32[8,128]{1,0:T(8,128)S(1)} %get-tuple-element.35), channel_id=1, source_target_pairs={{0,16},{16,32},{32,48},{48,64},{64,80},{80,96},{96,112},{112,128},... | collective-permute-start | bytes 12296 | tf_op jit(solution)/shard_map/ppermute | solution.py:11
  47.9 12.6 %collective-permute-start.6 = (f32[8,128]{1,0:T(8,128)S(1)}, f32[8,128]{1,0:T(8,128)S(1)}, u32[]{:S(2)}, u32[]{:S(2)}) collective-permute-start(f32[8,128]{1,0:T(8,128)S(1)} %bitcast.157), channel_id=1, source_target_pairs={{0,1},{1,2},{2,3},{3,4},{4,5},{5,6},{6,7},{7,8},{8,9},{9,10},{10,1... | collective-permute-start | bytes 12296 | tf_op jit(solution)/shard_map/ppermute | solution.py:11
  49.8 11.3 %collective-permute-start.7 = (f32[8,128]{1,0:T(8,128)S(1)}, f32[8,128]{1,0:T(8,128)S(1)}, u32[]{:S(2)}, u32[]{:S(2)}) collective-permute-start(f32[8,128]{1,0:T(8,128)S(1)} %bitcast.156), channel_id=1, source_target_pairs={{0,15},{1,0},{2,1},{3,2},{4,3},{5,4},{6,5},{7,6},{8,7},{9,8},{10,9... | collective-permute-start | bytes 12296 | tf_op jit(solution)/shard_map/ppermute | solution.py:11
  61.1 5.4 %collective-permute-start.8 = (f32[4608]{0:T(1024)S(1)}, f32[4608]{0:T(1024)S(1)}, u32[]{:S(2)}, u32[]{:S(2)}) collective-permute-start(f32[4608]{0:T(1024)S(1)} %concatenate.103), channel_id=1, source_target_pairs={{0,16},{1,17},{2,18},{3,19},{4,20},{5,21},{6,22},{7,23},{8,24},{9,... | collective-permute-start | bytes 55304 | tf_op jit(solution)/shard_map/ppermute | solution.py:50
  66.5 5.7 %collective-permute-start.9 = (f32[4608]{0:T(1024)S(1)}, f32[4608]{0:T(1024)S(1)}, u32[]{:S(2)}, u32[]{:S(2)}) collective-permute-start(f32[4608]{0:T(1024)S(1)} %add.118), channel_id=1, source_target_pairs={{0,32},{1,33},{2,34},{3,35},{4,36},{5,37},{6,38},{7,39},{8,40},{9,... | collective-permute-start | bytes 55304 | tf_op jit(solution)/shard_map/ppermute | solution.py:50
  72.2 6.6 %collective-permute-start.10 = (f32[4608]{0:T(1024)S(1)}, f32[4608]{0:T(1024)S(1)}, u32[]{:S(2)}, u32[]{:S(2)}) collective-permute-start(f32[4608]{0:T(1024)S(1)} %add.119), channel_id=1, source_target_pairs={{0,64},{1,65},{2,66},{3,67},{4,68},{5,69},{6,70},{7,71},{8,72},{9,... | collective-permute-start | bytes 55304 | tf_op jit(solution)/shard_map/ppermute | solution.py:50
  78.7 6.9 %collective-permute-start.11 = (f32[4608]{0:T(1024)S(1)}, f32[4608]{0:T(1024)S(1)}, u32[]{:S(2)}, u32[]{:S(2)}) collective-permute-start(f32[4608]{0:T(1024)S(1)} %add.120), channel_id=1, source_target_pairs={{0,224},{1,225},{2,226},{3,227},{4,228},{5,229},{6,230},{7,231},{8... | collective-permute-start | bytes 55304 | tf_op jit(solution)/shard_map/ppermute | solution.py:50
  85.6 5.7 %collective-permute-start.12 = (f32[4608]{0:T(1024)S(1)}, f32[4608]{0:T(1024)S(1)}, u32[]{:S(2)}, u32[]{:S(2)}) collective-permute-start(f32[4608]{0:T(1024)S(1)} %add.121), channel_id=1, source_target_pairs={{0,256},{1,257},{2,258},{3,259},{4,260},{5,261},{6,262},{7,263},{8... | collective-permute-start | bytes 55304 | tf_op jit(solution)/shard_map/ppermute | solution.py:50
  91.3 7.1 %collective-permute-start.13 = (f32[4608]{0:T(1024)S(1)}, f32[4608]{0:T(1024)S(1)}, u32[]{:S(2)}, u32[]{:S(2)}) collective-permute-start(f32[4608]{0:T(1024)S(1)} %add.122), channel_id=1, source_target_pairs={{0,512},{1,513},{2,514},{3,515},{4,516},{5,517},{6,518},{7,519},{8... | collective-permute-start | bytes 55304 | tf_op jit(solution)/shard_map/ppermute | solution.py:50
  98.4 6.9 %collective-permute-start.14 = (f32[4608]{0:T(1024)S(1)}, f32[4608]{0:T(1024)S(1)}, u32[]{:S(2)}, u32[]{:S(2)}) collective-permute-start(f32[4608]{0:T(1024)S(1)} %add.123), channel_id=1, source_target_pairs={{0,769},{1,768},{2,771},{3,770},{4,773},{5,772},{6,775},{7,774},{8... | collective-permute-start | bytes 55304 | tf_op jit(solution)/shard_map/ppermute | solution.py:50
  105.3 5.9 %collective-permute-start.15 = (f32[4608]{0:T(1024)S(1)}, f32[4608]{0:T(1024)S(1)}, u32[]{:S(2)}, u32[]{:S(2)}) collective-permute-start(f32[4608]{0:T(1024)S(1)} %add.124), channel_id=1, source_target_pairs={{0,2},{1,3},{2,0},{3,1},{4,6},{5,7},{6,4},{7,5},{8,10},{9,11},{10,... | collective-permute-start | bytes 55304 | tf_op jit(solution)/shard_map/ppermute | solution.py:50
  111.2 7.6 %collective-permute-start.16 = (f32[4608]{0:T(1024)S(1)}, f32[4608]{0:T(1024)S(1)}, u32[]{:S(2)}, u32[]{:S(2)}) collective-permute-start(f32[4608]{0:T(1024)S(1)} %add.125), channel_id=1, source_target_pairs={{0,4},{1,5},{2,6},{3,7},{4,0},{5,1},{6,2},{7,3},{8,12},{9,13},{10,... | collective-permute-start | bytes 55304 | tf_op jit(solution)/shard_map/ppermute | solution.py:50
  118.8 8.9 %collective-permute-start.17 = (f32[4608]{0:T(1024)S(1)}, f32[4608]{0:T(1024)S(1)}, u32[]{:S(2)}, u32[]{:S(2)}) collective-permute-start(f32[4608]{0:T(1024)S(1)} %add.126), channel_id=1, source_target_pairs={{0,14},{1,15},{2,12},{3,13},{4,10},{5,11},{6,8},{7,9},{8,6},{9,7},... | collective-permute-start | bytes 55304 | tf_op jit(solution)/shard_map/ppermute | solution.py:50

commit v3 on v2

--- a/solution.py
+++ b/solution.py
@@ -136,8 +136,8 @@
     from_yhi = shift_from(dfeat[4, :, 0], "gy", -1)
 
     flat = jnp.concatenate([gin.reshape(-1), gmid.reshape(-1), gout.reshape(-1)])
-    flat, from_xlo, from_xhi, from_ylo, from_yhi = lax.optimization_barrier((flat, from_xlo, from_xhi, from_ylo, from_yhi))
-    total = all_sum(flat)
+    padded_flat = jnp.pad(flat, (0, max(0, 16384 - flat.shape[0])))
+    total = lax.psum(padded_flat, ("gx", "gy"))[: flat.shape[0]]
     side1 = jnp.concatenate([from_xlo[None], dfeat[1, :-1]], axis=0)
     side2 = jnp.concatenate([dfeat[2, 1:], from_xhi[None]], axis=0)
     side3 = jnp.concatenate([from_ylo[:, None], dfeat[3, :, :-1]], axis=1)

time: 131 us -> 332 us (2.53); the launches traced: 130 us -> 326 us
  waiting for transfers between devices: 26.3 us -> 245 us
  starting transfers between devices: 86 us -> 47.3 us
  between operations: 1.89 us -> 15.2 us
    psum x0 -> x1, waiting for transfers between devices: none -> 245 us  [body(): total = lax.psum(padded_flat, ('gx', 'gy'))[:flat.shape[0]]]
    ppermute x10 -> x0, starting transfers between devices: 38.1 us -> none  [all_sum(): x = x + lax.ppermute(x, ('gx', 'gy'), pairs)]
    ppermute x10 -> x0, waiting for transfers between devices: 25.6 us -> none  [all_sum(): x = x + lax.ppermute(x, ('gx', 'gy'), pairs)]
  transfers between devices with their start and end apart: 18 -> 9, of which waited for: 11 -> 2; matrix products, arithmetic and copies ran while one was open for 7% -> 3% of each run, Pallas kernels for 0% -> 0%
where the time goes in v3:
time: 332 us; the launch traced here: 326 us
  waiting for transfers between devices  245 us (74%)
  starting transfers between devices  47.3 us (14%)
  between operations  15.2 us (5%)
  local copies, waits for them, and re-layouts  10.5 us (3%)
  matrix products  4.29 us (1%)
    psum x1, waiting for transfers between devices, body(): total = lax.psum(padded_flat, ('gx', 'gy'))[:flat.shape[0]]  245 us
    ppermute x8, starting transfers between devices, shift_from(): lax.ppermute(face, axis, [(i, (i + step) % count) for i in range(count)])  47.3 us
  transfers between devices with their start and end apart: 9, of which 2 were waited for; matrix products, arithmetic and copies ran while one was open for 3% of the time, Pallas kernels for 0%

profile of v3, /device:TPU:14, one launch (start us, length us, event | category | flops | bytes accessed | tf_op | source)
XLA Modules:
  0.0 325.8 jit_solution(13610405519468719372)
XLA Ops:
  7.2 0.8 copy_bitcast_fusion.1
  8.0 8.2 %collective-permute-start = (f32[2,8,128]{2,1,0:T(8,128)S(1)}, f32[2,8,128]{2,1,0:T(8,128)S(1)}, u32[]{:S(2)}, u32[]{:S(2)}) collective-permute-start(f32[2,8,128]{2,1,0:T(8,128)S(1)} %get-tuple-element.28), channel_id=1, source_target_pairs={{0,1},{1,2},{2,3},{3,4},{4,5},{5,6},{6,7},{7,8},{8,9},{9,10},{10,1... | collective-permute-start | bytes 24584 | tf_op jit(solution)/shard_map/ppermute | solution.py:11
  16.2 16.8 %collective-permute-start.1 = (f32[2,8,128]{2,1,0:T(8,128)S(1)}, f32[2,8,128]{2,1,0:T(8,128)S(1)}, u32[]{:S(2)}, u32[]{:S(2)}) collective-permute-start(f32[2,8,128]{2,1,0:T(8,128)S(1)} %get-tuple-element.29), channel_id=1, source_target_pairs={{0,15},{1,0},{2,1},{3,2},{4,3},{5,4},{6,5},{7,6},{8,7},{9,8},{10,9... | collective-permute-start | bytes 24584 | tf_op jit(solution)/shard_map/ppermute | solution.py:11
  33.0 2.5 collective-permute-start.2
  35.5 1.9 collective-permute-start.3
  37.5 0.9 fusion.43
  38.4 0.9 fusion.44
  39.3 0.9 fusion.42
  40.2 0.9 fusion.41
  41.8 0.8 convert_reduce_fusion
  43.7 0.6 reshape_reshape.5
  44.3 0.6 reshape_reshape.6
  47.4 0.8 fusion.2
  50.4 1.9 collective-permute-start.6
  52.3 9.9 %collective-permute-start.7 = (f32[8,128]{1,0:T(8,128)S(1)}, f32[8,128]{1,0:T(8,128)S(1)}, u32[]{:S(2)}, u32[]{:S(2)}) collective-permute-start(f32[8,128]{1,0:T(8,128)S(1)} %bitcast.156), channel_id=1, source_target_pairs={{0,15},{1,0},{2,1},{3,2},{4,3},{5,4},{6,5},{7,6},{8,7},{9,8},{10,9... | collective-permute-start | bytes 12296 | tf_op jit(solution)/shard_map/ppermute | solution.py:11
  62.3 3.1 collective-permute-start.5
  65.4 3.0 collective-permute-start.4
  68.6 0.7 fusion.5
  69.3 0.7 multiply_add_fusion
  70.3 0.7 fusion.19
  71.0 245.0 %all-reduce.3.cloned.1.call-done = f32[16384]{0:T(1024)} async-done(((f32[16384]{0:T(1024)}), f32[16384]{0:T(1024)}) %all-reduce.3.cloned.1.call-update) | async-done | bytes 65552 | tf_op jit(solution)/shard_map/psum | solution.py:140
  316.0 0.7 slice_multiply_fusion
  317.4 0.7 slice.222
  318.3 0.7 copy.65
  (79 shorter events, 6.7 us)
Async XLA Ops:
  7.2 39.2 %copy-start = (bf16[64,64]{1,0:T(8,128)(2,1)S(1)}, bf16[64,64]{1,0:T(8,128)(2,1)}, u32[]{:S(2)}) copy-start(bf16[64,64]{1,0:T(8,128)(2,1)} %param.14) | copy-start | bytes 24580
  7.2 35.7 %copy-start.4 = (s32[1,1,128]{2,1,0:T(1,128)S(1)}, s32[1,1,128]{2,1,0:T(1,128)}, u32[]{:S(2)}) copy-start(s32[1,1,128]{2,1,0:T(1,128)} %param.10) | copy-start | bytes 1540
  7.2 308.9 %all-reduce.3.cloned.1.call-start = ((), (), s32[]{:S(2)}) async-start(), calls=%async_computation | async-start | bytes 131072 | tf_op jit(solution)/shard_map/psum | solution.py:140
  8.0 37.2 %collective-permute-start = (f32[2,8,128]{2,1,0:T(8,128)S(1)}, f32[2,8,128]{2,1,0:T(8,128)S(1)}, u32[]{:S(2)}, u32[]{:S(2)}) collective-permute-start(f32[2,8,128]{2,1,0:T(8,128)S(1)} %get-tuple-element.28), channel_id=1, source_target_pairs={{0,1},{1,2},{2,3},{3,4},{4,5},{5,6},{6,7},{7,8},{8,9},{9,10},{10,1... | collective-permute-start | bytes 24584 | tf_op jit(solution)/shard_map/ppermute | solution.py:11
  16.2 29.1 %collective-permute-start.1 = (f32[2,8,128]{2,1,0:T(8,128)S(1)}, f32[2,8,128]{2,1,0:T(8,128)S(1)}, u32[]{:S(2)}, u32[]{:S(2)}) collective-permute-start(f32[2,8,128]{2,1,0:T(8,128)S(1)} %get-tuple-element.29), channel_id=1, source_target_pairs={{0,15},{1,0},{2,1},{3,2},{4,3},{5,4},{6,5},{7,6},{8,7},{9,8},{10,9... | collective-permute-start | bytes 24584 | tf_op jit(solution)/shard_map/ppermute | solution.py:11
  33.0 12.2 %collective-permute-start.2 = (f32[2,8,128]{2,0,1:T(2,128)S(1)}, f32[2,8,128]{2,0,1:T(2,128)S(1)}, u32[]{:S(2)}, u32[]{:S(2)}) collective-permute-start(f32[2,8,128]{2,0,1:T(2,128)S(1)} %bitcast.151), channel_id=1, source_target_pairs={{0,1008},{16,0},{32,16},{48,32},{64,48},{80,64},{96,80},{112,96},{... | collective-permute-start | bytes 24584 | tf_op jit(solution)/shard_map/ppermute | solution.py:11
  35.5 9.7 %collective-permute-start.3 = (f32[2,8,128]{2,0,1:T(2,128)S(1)}, f32[2,8,128]{2,0,1:T(2,128)S(1)}, u32[]{:S(2)}, u32[]{:S(2)}) collective-permute-start(f32[2,8,128]{2,0,1:T(2,128)S(1)} %bitcast.150), channel_id=1, source_target_pairs={{0,16},{16,32},{32,48},{48,64},{64,80},{80,96},{96,112},{112,128},... | collective-permute-start | bytes 24584 | tf_op jit(solution)/shard_map/ppermute | solution.py:11
  43.7 1.3 copy-start.5
  43.7 1.3 copy-start.1
  43.7 1.4 copy-start.2
  44.3 1.5 copy-start.3
  50.4 19.8 %collective-permute-start.6 = (f32[8,128]{1,0:T(8,128)S(1)}, f32[8,128]{1,0:T(8,128)S(1)}, u32[]{:S(2)}, u32[]{:S(2)}) collective-permute-start(f32[8,128]{1,0:T(8,128)S(1)} %bitcast.157), channel_id=1, source_target_pairs={{0,1},{1,2},{2,3},{3,4},{4,5},{5,6},{6,7},{7,8},{8,9},{9,10},{10,1... | collective-permute-start | bytes 12296 | tf_op jit(solution)/shard_map/ppermute | solution.py:11
  52.3 17.9 %collective-permute-start.7 = (f32[8,128]{1,0:T(8,128)S(1)}, f32[8,128]{1,0:T(8,128)S(1)}, u32[]{:S(2)}, u32[]{:S(2)}) collective-permute-start(f32[8,128]{1,0:T(8,128)S(1)} %bitcast.156), channel_id=1, source_target_pairs={{0,15},{1,0},{2,1},{3,2},{4,3},{5,4},{6,5},{7,6},{8,7},{9,8},{10,9... | collective-permute-start | bytes 12296 | tf_op jit(solution)/shard_map/ppermute | solution.py:11
  62.3 7.9 %collective-permute-start.5 = (f32[8,128]{1,0:T(8,128)S(1)}, f32[8,128]{1,0:T(8,128)S(1)}, u32[]{:S(2)}, u32[]{:S(2)}) collective-permute-start(f32[8,128]{1,0:T(8,128)S(1)} %get-tuple-element.24), channel_id=1, source_target_pairs={{0,1008},{16,0},{32,16},{48,32},{64,48},{80,64},{96,80},{112,96},{... | collective-permute-start | bytes 12296 | tf_op jit(solution)/shard_map/ppermute | solution.py:11
  65.4 4.9 %collective-permute-start.4 = (f32[8,128]{1,0:T(8,128)S(1)}, f32[8,128]{1,0:T(8,128)S(1)}, u32[]{:S(2)}, u32[]{:S(2)}) collective-permute-start(f32[8,128]{1,0:T(8,128)S(1)} %get-tuple-element.25), channel_id=1, source_target_pairs={{0,16},{16,32},{32,48},{48,64},{64,80},{80,96},{96,112},{112,128},... | collective-permute-start | bytes 12296 | tf_op jit(solution)/shard_map/ppermute | solution.py:11
Sparse Core Ops, SparseCore 0:
  50.4 265.5 all-reduce.2

commit v4 on v1

--- a/solution.py
+++ b/solution.py
@@ -5,34 +5,51 @@
 
 viscosity = 0.1
 
-GROUP_BITS = (("gx", 1), ("gy", 1))
-
 
 def shift_from(face, axis, step):
     count = lax.axis_size(axis)
     return lax.ppermute(face, axis, [(i, (i + step) % count) for i in range(count)])
 
 
-def group_sum(x, axis, lo, bits):
-    count = lax.axis_size(axis)
-    parts = [x]
-    for m in range(1, 1 << bits):
-        mask = m << lo
-        parts.append(lax.ppermute(x, axis, [(i, i ^ mask) for i in range(count)]))
-    while len(parts) > 1:
-        parts = [parts[2 * k] + parts[2 * k + 1] for k in range(len(parts) // 2)]
-    return parts[0]
+def reduce_rounds(nx, ny):
+    if (nx, ny) == (64, 16):
+        def decode(i):
+            gx, gy = divmod(i, 16)
+            return {"core": gx % 2, "x": (gx // 2) % 8, "y": (gy % 2) * 4 + gx // 16, "z": gy // 2}
 
+        def encode(c):
+            return ((c["y"] % 4) * 16 + c["x"] * 2 + c["core"]) * 16 + c["z"] * 2 + c["y"] // 4
 
-def all_sum(x):
-    for axis, chunk in GROUP_BITS:
-        bits = lax.axis_size(axis).bit_length() - 1
-        lo = 0
-        while lo < bits:
-            step = min(chunk, bits - lo)
-            x = group_sum(x, axis, lo, step)
-            lo += step
-    return x
+        plan = [
+            ("core", lambda v: v ^ 1, "gx"),
+            ("y", lambda v: v ^ 4, "gy"),
+            ("x", lambda v: v ^ 1, None),
+            ("x", lambda v: v ^ 2, None),
+            ("x", lambda v: 7 - v, None),
+            ("y", lambda v: v ^ 1, None),
+            ("y", lambda v: v ^ 2, None),
+            ("z", lambda v: v ^ 1, None),
+            ("z", lambda v: v ^ 2, None),
+            ("z", lambda v: 7 - v, None),
+        ]
+        rounds = []
+        for ring, step, tag in plan:
+            pairs = []
+            for i in range(nx * ny):
+                c = decode(i)
+                c[ring] = step(c[ring])
+                pairs.append((i, encode(c)))
+            rounds.append((pairs, tag))
+        return rounds
+    rounds = []
+    for size, stride, tag in ((nx, ny, "gx"), (ny, 1, "gy")):
+        for bit in range(size.bit_length() - 1):
+            pairs = []
+            for i in range(nx * ny):
+                index = (i // stride) % size
+                pairs.append((i, i + ((index ^ (1 << bit)) - index) * stride))
+            rounds.append((pairs, tag if bit == 0 else None))
+    return rounds
 
 
 def from_blocks(blocks, sizex, sizey, sizez):
@@ -104,16 +121,43 @@
     da1 = (dh1 * (1.0 - h1f * h1f)).astype(jnp.bfloat16)
     dfeat = jnp.dot(w_in.T, da1, preferred_element_type=jnp.float32).reshape(7, sizex, sizey, sizez)
     dims = (((1,), (1,)), ((), ()))
-    gin = lax.dot_general(da1, chosen, dims, preferred_element_type=jnp.float32)
     gmid = lax.dot_general(da2, h1, dims, preferred_element_type=jnp.float32)
     gout = lax.dot_general(dcl[None, :], h2, dims, preferred_element_type=jnp.float32)
 
     new_field = velocity + viscosity * padded_laplace(padded) + corr.reshape(sizex, sizey, sizez)
 
-    from_xlo = shift_from(dfeat[1, -1], "gx", 1)
-    from_xhi = shift_from(dfeat[2, 0], "gx", -1)
-    from_ylo = shift_from(dfeat[3, :, -1], "gy", 1)
-    from_yhi = shift_from(dfeat[4, :, 0], "gy", -1)
+    nx = lax.axis_size("gx")
+    ny = lax.axis_size("gy")
+    xodd = lax.axis_index("gx") % 2 == 1
+    yodd = lax.axis_index("gy") % 2 == 1
+    up_x, down_x = dfeat[1, -1], dfeat[2, 0]
+    up_y, down_y = dfeat[3, :, -1], dfeat[4, :, 0]
+    pair_face = {"gx": jnp.where(xodd, down_x, up_x), "gy": jnp.where(yodd, down_y, up_y)}
+    other_x = lax.ppermute(
+        jnp.where(xodd, up_x, down_x), "gx", [(i, (i + 1) % nx if i % 2 else (i - 1) % nx) for i in range(nx)]
+    )
+    other_y = lax.ppermute(
+        jnp.where(yodd, up_y, down_y), "gy", [(i, (i + 1) % ny if i % 2 else (i - 1) % ny) for i in range(ny)]
+    )
+
+    gin_t = lax.dot_general(chosen, da1, dims, preferred_element_type=jnp.float32)
+    grads = jnp.concatenate([gmid, gin_t, gout], axis=0)
+    received = {}
+    for pairs, tag in reduce_rounds(nx, ny):
+        if tag is None:
+            grads = grads + lax.ppermute(grads, ("gx", "gy"), pairs)
+        else:
+            rows = grads.shape[0]
+            face = pair_face[tag]
+            message = jnp.concatenate([grads, face.reshape(-1, grads.shape[1])], axis=0)
+            got = lax.ppermute(message, ("gx", "gy"), pairs)
+            received[tag] = got[rows:].reshape(face.shape)
+            grads = grads + got[:rows]
+    from_xlo = jnp.where(xodd, received["gx"], other_x)
+    from_xhi = jnp.where(xodd, other_x, received["gx"])
+    from_ylo = jnp.where(yodd, received["gy"], other_y)
+    from_yhi = jnp.where(yodd, other_y, received["gy"])
+
     side1 = jnp.concatenate([from_xlo[None], dfeat[1, :-1]], axis=0)
     side2 = jnp.concatenate([dfeat[2, 1:], from_xhi[None]], axis=0)
     side3 = jnp.concatenate([from_ylo[:, None], dfeat[3, :, :-1]], axis=1)
@@ -121,14 +165,12 @@
     local = dfeat[0] + jnp.roll(dfeat[5], 1, 2) + jnp.roll(dfeat[6], -1, 2)
     grad_field = cotangent + viscosity * padded_laplace(cot_pad) + local + (side1 + side2 + side3 + side4)
 
-    flat = jnp.concatenate([gin.reshape(-1), gmid.reshape(-1), gout.reshape(-1)])
-    total = all_sum(flat)
-    scale = 1.0 / jnp.sqrt(jnp.float32(lax.axis_size("gx") * lax.axis_size("gy") * slots * 64))
-    total = total * scale
+    scale = 1.0 / jnp.sqrt(jnp.float32(nx * ny * slots * 64))
+    total = grads * scale
     width = gmid.shape[0]
-    grad_in = total[: width * 7].reshape(width, 7)
-    grad_mid = total[width * 7 : width * 7 + width * width].reshape(width, width)
-    grad_out = total[width * 7 + width * width :].reshape(1, width)
+    grad_mid = total[:width]
+    grad_in = total[width : width + 7].T
+    grad_out = total[width + 7 :]
     return (new_field, grad_field, grad_in, grad_mid, grad_out)
 
 

time: 130 us -> 118 us (0.908)
  starting transfers between devices: 75.7 us -> 63.8 us
  waiting for transfers between devices: 35.1 us -> 33.8 us
    ppermute x8 -> x4, starting transfers between devices: 45.6 us -> 29.4 us  [shift_from(): lax.ppermute(face, axis, [(i, (i + step) % count) for i in range(count)])]
    ppermute x10 -> x12, starting transfers between devices: 30.2 us -> 34.4 us  [the longest x8 18.3 us: body(): grads = grads + lax.ppermute(grads, ('gx', 'gy'), pairs)]
    ppermute x10 -> x12, waiting for transfers between devices: 35 us -> 33.8 us  [the longest x8 25.4 us: body(): grads = grads + lax.ppermute(grads, ('gx', 'gy'), pairs)]
  transfers between devices with their start and end apart: 18 -> 16, of which waited for: 9 -> 9; matrix products, arithmetic and copies ran while one was open for 8% -> 9% of each run, Pallas kernels for 0% -> 0%
where the time goes in v4:
time: 118 us; the launch traced here: 117 us
  starting transfers between devices  63.8 us (54%)
  waiting for transfers between devices  33.8 us (29%)
  local copies, waits for them, and re-layouts  9.42 us (8%)
  matrix products  4.99 us (4%)
  other arithmetic  2.89 us (2%)
  between operations  1.94 us (2%)
    ppermute x4, starting transfers between devices, shift_from(): lax.ppermute(face, axis, [(i, (i + step) % count) for i in range(count)])  29.4 us
    ppermute x8, waiting for transfers between devices, body(): grads = grads + lax.ppermute(grads, ('gx', 'gy'), pairs)  25.4 us
    ppermute x8, starting transfers between devices, body(): grads = grads + lax.ppermute(grads, ('gx', 'gy'), pairs)  18.3 us
    ppermute x2, waiting for transfers between devices, body(): got = lax.ppermute(message, ('gx', 'gy'), pairs)  8.38 us
    ppermute x1, starting transfers between devices, body(): lax.ppermute(jnp.where(yodd, up_y, down_y), 'gy', [(i, (i + 1) % ny if i...  7.54 us
    ppermute x2, starting transfers between devices, body(): got = lax.ppermute(message, ('gx', 'gy'), pairs)  6.62 us
    slice x4, local copies, waits for them, and re-layouts, padded_laplace(): total = total + jnp.roll(center, -1, 2) + jnp.roll(center, 1, 2)  2.8 us
  transfers between devices with their start and end apart: 16, of which 9 were waited for; matrix products, arithmetic and copies ran while one was open for 9% of the time, Pallas kernels for 0%

profile of v4, /device:TPU:14, one launch (start us, length us, event | category | flops | bytes accessed | tf_op | source)
XLA Modules:
  0.0 116.8 jit_solution(15873084425317625027)
XLA Ops:
  1.5 8.2 %collective-permute-start = (f32[2,8,128]{2,1,0:T(8,128)S(1)}, f32[2,8,128]{2,1,0:T(8,128)S(1)}, u32[]{:S(2)}, u32[]{:S(2)}) collective-permute-start(f32[2,8,128]{2,1,0:T(8,128)S(1)} %get-tuple-element.33), channel_id=1, source_target_pairs={{0,1},{1,2},{2,3},{3,4},{4,5},{5,6},{6,7},{7,8},{8,9},{9,10},{10,1... | collective-permute-start | bytes 24584 | tf_op jit(solution)/shard_map/ppermute | solution.py:11
  9.7 16.8 %collective-permute-start.1 = (f32[2,8,128]{2,1,0:T(8,128)S(1)}, f32[2,8,128]{2,1,0:T(8,128)S(1)}, u32[]{:S(2)}, u32[]{:S(2)}) collective-permute-start(f32[2,8,128]{2,1,0:T(8,128)S(1)} %get-tuple-element.34), channel_id=1, source_target_pairs={{0,15},{1,0},{2,1},{3,2},{4,3},{5,4},{6,5},{7,6},{8,7},{9,8},{10,9... | collective-permute-start | bytes 24584 | tf_op jit(solution)/shard_map/ppermute | solution.py:11
  26.4 2.5 %collective-permute-start.2 = (f32[2,8,128]{2,0,1:T(2,128)S(1)}, f32[2,8,128]{2,0,1:T(2,128)S(1)}, u32[]{:S(2)}, u32[]{:S(2)}) collective-permute-start(f32[2,8,128]{2,0,1:T(2,128)S(1)} %bitcast.162), channel_id=1, source_target_pairs={{0,1008},{16,0},{32,16},{48,32},{64,48},{80,64},{96,80},{112,96},{... | collective-permute-start | bytes 24584 | tf_op jit(solution)/shard_map/ppermute | solution.py:11
  29.0 1.9 %collective-permute-start.3 = (f32[2,8,128]{2,0,1:T(2,128)S(1)}, f32[2,8,128]{2,0,1:T(2,128)S(1)}, u32[]{:S(2)}, u32[]{:S(2)}) collective-permute-start(f32[2,8,128]{2,0,1:T(2,128)S(1)} %bitcast.161), channel_id=1, source_target_pairs={{0,16},{16,32},{32,48},{48,64},{64,80},{80,96},{96,112},{112,128},... | collective-permute-start | bytes 24584 | tf_op jit(solution)/shard_map/ppermute | solution.py:11
  42.8 4.7 %collective-permute-start.4 = (f32[88,64]{0,1:T(8,128)S(1)}, f32[88,64]{0,1:T(8,128)S(1)}, u32[]{:S(2)}, u32[]{:S(2)}) collective-permute-start(f32[88,64]{0,1:T(8,128)S(1)} %pad_maximum_fusion.18), channel_id=1, source_target_pairs={{0,16},{1,17},{2,18},{3,19},{4,20},{5,21},{6,22},{7,23},{8,24},{9,... | collective-permute-start | bytes 67592 | tf_op jit(solution)/shard_map/ppermute | solution.py:153
  48.5 1.9 %collective-permute-start.6 = (f32[88,64]{0,1:T(8,128)S(1)}, f32[88,64]{0,1:T(8,128)S(1)}, u32[]{:S(2)}, u32[]{:S(2)}) collective-permute-start(f32[88,64]{0,1:T(8,128)S(1)} %pad_maximum_fusion.19), channel_id=1, source_target_pairs={{0,1},{1,0},{2,3},{3,2},{4,5},{5,4},{6,7},{7,6},{8,9},{9,8},{10,11... | collective-permute-start | bytes 67592 | tf_op jit(solution)/shard_map/ppermute | solution.py:153
  50.5 7.7 %collective-permute-done.6 = f32[88,64]{0,1:T(8,128)S(1)} collective-permute-done((f32[88,64]{0,1:T(8,128)S(1)}, f32[88,64]{0,1:T(8,128)S(1)}, u32[]{:S(2)}, u32[]{:S(2)}) %collective-permute-start.6) | collective-permute-done | bytes 22560 | tf_op jit(solution)/shard_map/ppermute | solution.py:153
  58.2 1.9 %collective-permute-start.8 = (f32[72,64]{0,1:T(8,128)S(1)}, f32[72,64]{0,1:T(8,128)S(1)}, u32[]{:S(2)}, u32[]{:S(2)}) collective-permute-start(f32[72,64]{0,1:T(8,128)S(1)} %slice_add_fusion), channel_id=1, source_target_pairs={{0,32},{1,33},{2,34},{3,35},{4,36},{5,37},{6,38},{7,39},{8,40},{9,... | collective-permute-start | bytes 55304 | tf_op jit(solution)/shard_map/ppermute | solution.py:148
  60.5 3.5 %collective-permute-done.8 = f32[72,64]{0,1:T(8,128)S(1)} collective-permute-done((f32[72,64]{0,1:T(8,128)S(1)}, f32[72,64]{0,1:T(8,128)S(1)}, u32[]{:S(2)}, u32[]{:S(2)}) %collective-permute-start.8) | collective-permute-done | bytes 18464 | tf_op jit(solution)/shard_map/ppermute | solution.py:148
  64.0 2.1 %collective-permute-start.9 = (f32[72,64]{0,1:T(8,128)S(1)}, f32[72,64]{0,1:T(8,128)S(1)}, u32[]{:S(2)}, u32[]{:S(2)}) collective-permute-start(f32[72,64]{0,1:T(8,128)S(1)} %add.129), channel_id=1, source_target_pairs={{0,64},{1,65},{2,66},{3,67},{4,68},{5,69},{6,70},{7,71},{8,72},{9,... | collective-permute-start | bytes 55304 | tf_op jit(solution)/shard_map/ppermute | solution.py:148
  66.8 3.9 %collective-permute-done.9 = f32[72,64]{0,1:T(8,128)S(1)} collective-permute-done((f32[72,64]{0,1:T(8,128)S(1)}, f32[72,64]{0,1:T(8,128)S(1)}, u32[]{:S(2)}, u32[]{:S(2)}) %collective-permute-start.9) | collective-permute-done | bytes 18464 | tf_op jit(solution)/shard_map/ppermute | solution.py:148
  70.7 2.3 %collective-permute-start.10 = (f32[72,64]{0,1:T(8,128)S(1)}, f32[72,64]{0,1:T(8,128)S(1)}, u32[]{:S(2)}, u32[]{:S(2)}) collective-permute-start(f32[72,64]{0,1:T(8,128)S(1)} %add.130), channel_id=1, source_target_pairs={{0,224},{1,225},{2,226},{3,227},{4,228},{5,229},{6,230},{7,231},{8... | collective-permute-start | bytes 55304 | tf_op jit(solution)/shard_map/ppermute | solution.py:148
  73.7 4.0 %collective-permute-done.10 = f32[72,64]{0,1:T(8,128)S(1)} collective-permute-done((f32[72,64]{0,1:T(8,128)S(1)}, f32[72,64]{0,1:T(8,128)S(1)}, u32[]{:S(2)}, u32[]{:S(2)}) %collective-permute-start.10) | collective-permute-done | bytes 18464 | tf_op jit(solution)/shard_map/ppermute | solution.py:148
  77.8 2.7 %collective-permute-start.11 = (f32[72,64]{0,1:T(8,128)S(1)}, f32[72,64]{0,1:T(8,128)S(1)}, u32[]{:S(2)}, u32[]{:S(2)}) collective-permute-start(f32[72,64]{0,1:T(8,128)S(1)} %add.131), channel_id=1, source_target_pairs={{0,256},{1,257},{2,258},{3,259},{4,260},{5,261},{6,262},{7,263},{8... | collective-permute-start | bytes 55304 | tf_op jit(solution)/shard_map/ppermute | solution.py:148
  80.5 1.9 %collective-permute-start.5 = (f32[8,128]{1,0:T(8,128)S(1)}, f32[8,128]{1,0:T(8,128)S(1)}, u32[]{:S(2)}, u32[]{:S(2)}) collective-permute-start(f32[8,128]{1,0:T(8,128)S(1)} %get-tuple-element.29), channel_id=1, source_target_pairs={{0,1008},{16,32},{32,16},{48,64},{64,48},{80,96},{96,80},{112,128}... | collective-permute-start | bytes 12296 | tf_op jit(solution)/shard_map/ppermute | solution.py:136
  82.4 1.2 collective-permute-done.11
  83.6 3.6 %collective-permute-start.12 = (f32[72,64]{0,1:T(8,128)S(1)}, f32[72,64]{0,1:T(8,128)S(1)}, u32[]{:S(2)}, u32[]{:S(2)}) collective-permute-start(f32[72,64]{0,1:T(8,128)S(1)} %add.132), channel_id=1, source_target_pairs={{0,512},{1,513},{2,514},{3,515},{4,516},{5,517},{6,518},{7,519},{8... | collective-permute-start | bytes 55304 | tf_op jit(solution)/shard_map/ppermute | solution.py:148
  87.3 7.5 %collective-permute-start.7 = (f32[8,128]{1,0:T(8,128)S(1)}, f32[8,128]{1,0:T(8,128)S(1)}, u32[]{:S(2)}, u32[]{:S(2)}) collective-permute-start(f32[8,128]{1,0:T(8,128)S(1)} %get-tuple-element.49), channel_id=1, source_target_pairs={{0,15},{1,2},{2,1},{3,4},{4,3},{5,6},{6,5},{7,8},{8,7},{9,10},{10,... | collective-permute-start | bytes 12296 | tf_op jit(solution)/shard_map/ppermute | solution.py:139
  95.1 1.9 %collective-permute-start.13 = (f32[72,64]{0,1:T(8,128)S(1)}, f32[72,64]{0,1:T(8,128)S(1)}, u32[]{:S(2)}, u32[]{:S(2)}) collective-permute-start(f32[72,64]{0,1:T(8,128)S(1)} %add.133), channel_id=1, source_target_pairs={{0,2},{1,3},{2,0},{3,1},{4,6},{5,7},{6,4},{7,5},{8,10},{9,11},{10,... | collective-permute-start | bytes 55304 | tf_op jit(solution)/shard_map/ppermute | solution.py:148
  97.3 3.6 %collective-permute-done.13 = f32[72,64]{0,1:T(8,128)S(1)} collective-permute-done((f32[72,64]{0,1:T(8,128)S(1)}, f32[72,64]{0,1:T(8,128)S(1)}, u32[]{:S(2)}, u32[]{:S(2)}) %collective-permute-start.13) | collective-permute-done | bytes 18464 | tf_op jit(solution)/shard_map/ppermute | solution.py:148
  101.0 1.9 %collective-permute-start.14 = (f32[72,64]{0,1:T(8,128)S(1)}, f32[72,64]{0,1:T(8,128)S(1)}, u32[]{:S(2)}, u32[]{:S(2)}) collective-permute-start(f32[72,64]{0,1:T(8,128)S(1)} %add.134), channel_id=1, source_target_pairs={{0,4},{1,5},{2,6},{3,7},{4,0},{5,1},{6,2},{7,3},{8,12},{9,13},{10,... | collective-permute-start | bytes 55304 | tf_op jit(solution)/shard_map/ppermute | solution.py:148
  102.9 4.8 %collective-permute-done.14 = f32[72,64]{0,1:T(8,128)S(1)} collective-permute-done((f32[72,64]{0,1:T(8,128)S(1)}, f32[72,64]{0,1:T(8,128)S(1)}, u32[]{:S(2)}, u32[]{:S(2)}) %collective-permute-start.14) | collective-permute-done | bytes 18464 | tf_op jit(solution)/shard_map/ppermute | solution.py:148
  107.7 1.9 %collective-permute-start.15 = (f32[72,64]{0,1:T(8,128)S(1)}, f32[72,64]{0,1:T(8,128)S(1)}, u32[]{:S(2)}, u32[]{:S(2)}) collective-permute-start(f32[72,64]{0,1:T(8,128)S(1)} %add.135), channel_id=1, source_target_pairs={{0,14},{1,15},{2,12},{3,13},{4,10},{5,11},{6,8},{7,9},{8,6},{9,7},... | collective-permute-start | bytes 55304 | tf_op jit(solution)/shard_map/ppermute | solution.py:148
  110.3 4.4 %collective-permute-done.15 = f32[72,64]{0,1:T(8,128)S(1)} collective-permute-done((f32[72,64]{0,1:T(8,128)S(1)}, f32[72,64]{0,1:T(8,128)S(1)}, u32[]{:S(2)}, u32[]{:S(2)}) %collective-permute-start.15) | collective-permute-done | bytes 18464 | tf_op jit(solution)/shard_map/ppermute | solution.py:148
  (109 shorter events, 18.0 us)
Async XLA Ops:
  0.6 38.9 %copy-start = (bf16[64,64]{1,0:T(8,128)(2,1)S(1)}, bf16[64,64]{1,0:T(8,128)(2,1)}, u32[]{:S(2)}) copy-start(bf16[64,64]{1,0:T(8,128)(2,1)} %param.14) | copy-start | bytes 24580
  1.5 37.0 %collective-permute-start = (f32[2,8,128]{2,1,0:T(8,128)S(1)}, f32[2,8,128]{2,1,0:T(8,128)S(1)}, u32[]{:S(2)}, u32[]{:S(2)}) collective-permute-start(f32[2,8,128]{2,1,0:T(8,128)S(1)} %get-tuple-element.33), channel_id=1, source_target_pairs={{0,1},{1,2},{2,3},{3,4},{4,5},{5,6},{6,7},{7,8},{8,9},{9,10},{10,1... | collective-permute-start | bytes 24584 | tf_op jit(solution)/shard_map/ppermute | solution.py:11
  9.7 28.9 %collective-permute-start.1 = (f32[2,8,128]{2,1,0:T(8,128)S(1)}, f32[2,8,128]{2,1,0:T(8,128)S(1)}, u32[]{:S(2)}, u32[]{:S(2)}) collective-permute-start(f32[2,8,128]{2,1,0:T(8,128)S(1)} %get-tuple-element.34), channel_id=1, source_target_pairs={{0,15},{1,0},{2,1},{3,2},{4,3},{5,4},{6,5},{7,6},{8,7},{9,8},{10,9... | collective-permute-start | bytes 24584 | tf_op jit(solution)/shard_map/ppermute | solution.py:11
  26.4 12.0 %collective-permute-start.2 = (f32[2,8,128]{2,0,1:T(2,128)S(1)}, f32[2,8,128]{2,0,1:T(2,128)S(1)}, u32[]{:S(2)}, u32[]{:S(2)}) collective-permute-start(f32[2,8,128]{2,0,1:T(2,128)S(1)} %bitcast.162), channel_id=1, source_target_pairs={{0,1008},{16,0},{32,16},{48,32},{64,48},{80,64},{96,80},{112,96},{... | collective-permute-start | bytes 24584 | tf_op jit(solution)/shard_map/ppermute | solution.py:11
  29.0 9.5 %collective-permute-start.3 = (f32[2,8,128]{2,0,1:T(2,128)S(1)}, f32[2,8,128]{2,0,1:T(2,128)S(1)}, u32[]{:S(2)}, u32[]{:S(2)}) collective-permute-start(f32[2,8,128]{2,0,1:T(2,128)S(1)} %bitcast.161), channel_id=1, source_target_pairs={{0,16},{16,32},{32,48},{48,64},{64,80},{80,96},{96,112},{112,128},... | collective-permute-start | bytes 24584 | tf_op jit(solution)/shard_map/ppermute | solution.py:11
  36.8 1.3 %copy-start.4 = (bf16[1,64]{1,0:T(2,128)(2,1)S(1)}, bf16[1,64]{1,0:T(2,128)(2,1)}, u32[]{:S(2)}) copy-start(bf16[1,64]{1,0:T(2,128)(2,1)} %param.15) | copy-start | bytes 388
  36.8 1.3 %copy-start.1 = (f32[8,8,128]{2,1,0:T(8,128)S(1)}, f32[8,8,128]{2,1,0:T(8,128)}, u32[]{:S(2)}) copy-start(f32[8,8,128]{2,1,0:T(8,128)} %param.9) | copy-start | bytes 98308
  36.8 1.5 %copy-start.2 = (f32[8,8,128]{2,1,0:T(8,128)S(1)}, f32[8,8,128]{2,1,0:T(8,128)}, u32[]{:S(2)}) copy-start(f32[8,8,128]{2,1,0:T(8,128)} %param.8) | copy-start | bytes 98308
  37.5 1.5 %copy-start.3 = (bf16[64,7]{0,1:T(8,128)(2,1)S(1)}, bf16[64,7]{0,1:T(8,128)(2,1)}, u32[]{:S(2)}) copy-start(bf16[64,7]{0,1:T(8,128)(2,1)} %param.13) | copy-start | bytes 2692
  42.8 5.6 %collective-permute-start.4 = (f32[88,64]{0,1:T(8,128)S(1)}, f32[88,64]{0,1:T(8,128)S(1)}, u32[]{:S(2)}, u32[]{:S(2)}) collective-permute-start(f32[88,64]{0,1:T(8,128)S(1)} %pad_maximum_fusion.18), channel_id=1, source_target_pairs={{0,16},{1,17},{2,18},{3,19},{4,20},{5,21},{6,22},{7,23},{8,24},{9,... | collective-permute-start | bytes 67592 | tf_op jit(solution)/shard_map/ppermute | solution.py:153
  48.5 9.7 %collective-permute-start.6 = (f32[88,64]{0,1:T(8,128)S(1)}, f32[88,64]{0,1:T(8,128)S(1)}, u32[]{:S(2)}, u32[]{:S(2)}) collective-permute-start(f32[88,64]{0,1:T(8,128)S(1)} %pad_maximum_fusion.19), channel_id=1, source_target_pairs={{0,1},{1,0},{2,3},{3,2},{4,5},{5,4},{6,7},{7,6},{8,9},{9,8},{10,11... | collective-permute-start | bytes 67592 | tf_op jit(solution)/shard_map/ppermute | solution.py:153
  58.2 5.8 %collective-permute-start.8 = (f32[72,64]{0,1:T(8,128)S(1)}, f32[72,64]{0,1:T(8,128)S(1)}, u32[]{:S(2)}, u32[]{:S(2)}) collective-permute-start(f32[72,64]{0,1:T(8,128)S(1)} %slice_add_fusion), channel_id=1, source_target_pairs={{0,32},{1,33},{2,34},{3,35},{4,36},{5,37},{6,38},{7,39},{8,40},{9,... | collective-permute-start | bytes 55304 | tf_op jit(solution)/shard_map/ppermute | solution.py:148
  64.0 6.7 %collective-permute-start.9 = (f32[72,64]{0,1:T(8,128)S(1)}, f32[72,64]{0,1:T(8,128)S(1)}, u32[]{:S(2)}, u32[]{:S(2)}) collective-permute-start(f32[72,64]{0,1:T(8,128)S(1)} %add.129), channel_id=1, source_target_pairs={{0,64},{1,65},{2,66},{3,67},{4,68},{5,69},{6,70},{7,71},{8,72},{9,... | collective-permute-start | bytes 55304 | tf_op jit(solution)/shard_map/ppermute | solution.py:148
  70.7 7.0 %collective-permute-start.10 = (f32[72,64]{0,1:T(8,128)S(1)}, f32[72,64]{0,1:T(8,128)S(1)}, u32[]{:S(2)}, u32[]{:S(2)}) collective-permute-start(f32[72,64]{0,1:T(8,128)S(1)} %add.130), channel_id=1, source_target_pairs={{0,224},{1,225},{2,226},{3,227},{4,228},{5,229},{6,230},{7,231},{8... | collective-permute-start | bytes 55304 | tf_op jit(solution)/shard_map/ppermute | solution.py:148
  77.8 5.8 %collective-permute-start.11 = (f32[72,64]{0,1:T(8,128)S(1)}, f32[72,64]{0,1:T(8,128)S(1)}, u32[]{:S(2)}, u32[]{:S(2)}) collective-permute-start(f32[72,64]{0,1:T(8,128)S(1)} %add.131), channel_id=1, source_target_pairs={{0,256},{1,257},{2,258},{3,259},{4,260},{5,261},{6,262},{7,263},{8... | collective-permute-start | bytes 55304 | tf_op jit(solution)/shard_map/ppermute | solution.py:148
  80.5 16.6 %collective-permute-start.5 = (f32[8,128]{1,0:T(8,128)S(1)}, f32[8,128]{1,0:T(8,128)S(1)}, u32[]{:S(2)}, u32[]{:S(2)}) collective-permute-start(f32[8,128]{1,0:T(8,128)S(1)} %get-tuple-element.29), channel_id=1, source_target_pairs={{0,1008},{16,32},{32,16},{48,64},{64,48},{80,96},{96,80},{112,128}... | collective-permute-start | bytes 12296 | tf_op jit(solution)/shard_map/ppermute | solution.py:136
  83.6 11.5 %collective-permute-start.12 = (f32[72,64]{0,1:T(8,128)S(1)}, f32[72,64]{0,1:T(8,128)S(1)}, u32[]{:S(2)}, u32[]{:S(2)}) collective-permute-start(f32[72,64]{0,1:T(8,128)S(1)} %add.132), channel_id=1, source_target_pairs={{0,512},{1,513},{2,514},{3,515},{4,516},{5,517},{6,518},{7,519},{8... | collective-permute-start | bytes 55304 | tf_op jit(solution)/shard_map/ppermute | solution.py:148
  87.3 15.5 %collective-permute-start.7 = (f32[8,128]{1,0:T(8,128)S(1)}, f32[8,128]{1,0:T(8,128)S(1)}, u32[]{:S(2)}, u32[]{:S(2)}) collective-permute-start(f32[8,128]{1,0:T(8,128)S(1)} %get-tuple-element.49), channel_id=1, source_target_pairs={{0,15},{1,2},{2,1},{3,4},{4,3},{5,6},{6,5},{7,8},{8,7},{9,10},{10,... | collective-permute-start | bytes 12296 | tf_op jit(solution)/shard_map/ppermute | solution.py:139
  95.1 5.8 %collective-permute-start.13 = (f32[72,64]{0,1:T(8,128)S(1)}, f32[72,64]{0,1:T(8,128)S(1)}, u32[]{:S(2)}, u32[]{:S(2)}) collective-permute-start(f32[72,64]{0,1:T(8,128)S(1)} %add.133), channel_id=1, source_target_pairs={{0,2},{1,3},{2,0},{3,1},{4,6},{5,7},{6,4},{7,5},{8,10},{9,11},{10,... | collective-permute-start | bytes 55304 | tf_op jit(solution)/shard_map/ppermute | solution.py:148
  101.0 6.7 %collective-permute-start.14 = (f32[72,64]{0,1:T(8,128)S(1)}, f32[72,64]{0,1:T(8,128)S(1)}, u32[]{:S(2)}, u32[]{:S(2)}) collective-permute-start(f32[72,64]{0,1:T(8,128)S(1)} %add.134), channel_id=1, source_target_pairs={{0,4},{1,5},{2,6},{3,7},{4,0},{5,1},{6,2},{7,3},{8,12},{9,13},{10,... | collective-permute-start | bytes 55304 | tf_op jit(solution)/shard_map/ppermute | solution.py:148
  107.7 7.0 %collective-permute-start.15 = (f32[72,64]{0,1:T(8,128)S(1)}, f32[72,64]{0,1:T(8,128)S(1)}, u32[]{:S(2)}, u32[]{:S(2)}) collective-permute-start(f32[72,64]{0,1:T(8,128)S(1)} %add.135), channel_id=1, source_target_pairs={{0,14},{1,15},{2,12},{3,13},{4,10},{5,11},{6,8},{7,9},{8,6},{9,7},... | collective-permute-start | bytes 55304 | tf_op jit(solution)/shard_map/ppermute | solution.py:148

commit v5 on v4

--- a/solution.py
+++ b/solution.py
@@ -1,6 +1,8 @@
 import jax
 import jax.numpy as jnp
 from jax import lax
+from jax.experimental import pallas as pl
+from jax.experimental.pallas import tpu as pltpu
 from jax.sharding import PartitionSpec as P
 
 viscosity = 0.1
@@ -69,11 +71,31 @@
     return jnp.concatenate([top, mid, bot], axis=-3)
 
 
-def padded_laplace(padded):
+def padded_laplace(padded, zup, zdown):
     center = padded[1:-1, 1:-1]
     total = padded[2:, 1:-1] + padded[:-2, 1:-1] + padded[1:-1, 2:] + padded[1:-1, :-2]
-    total = total + jnp.roll(center, -1, 2) + jnp.roll(center, 1, 2)
+    total = total + zup + zdown
     return total - 6.0 * center
+
+
+def z_neighbours_kernel(v_ref, c_ref, vup_ref, vdown_ref, cup_ref, cdown_ref):
+    last = v_ref.shape[1] - 1
+    v = v_ref[...]
+    c = c_ref[...]
+    vup_ref[...] = pltpu.roll(v, last, 1)
+    vdown_ref[...] = pltpu.roll(v, 1, 1)
+    cup_ref[...] = pltpu.roll(c, last, 1)
+    cdown_ref[...] = pltpu.roll(c, 1, 1)
+
+
+def z_neighbours(velocity, cotangent):
+    shape = velocity.shape
+    flat = (shape[0] * shape[1], shape[2])
+    out = jax.ShapeDtypeStruct(flat, velocity.dtype)
+    parts = pl.pallas_call(z_neighbours_kernel, out_shape=(out, out, out, out))(
+        velocity.reshape(flat), cotangent.reshape(flat)
+    )
+    return [part.reshape(shape) for part in parts]
 
 
 def body(velocity, cotangent, block_ids, fluid_count, fluid_cells, w_in, w_mid, w_out):
@@ -82,11 +104,11 @@
     nblocks = sizex * sizey * sizez // 64
     cells = sizex * sizey * sizez
 
-    both = jnp.stack([velocity, cotangent])
-    xlo = shift_from(both[:, -1], "gx", 1)
-    xhi = shift_from(both[:, 0], "gx", -1)
-    ylo = shift_from(both[:, :, -1], "gy", 1)
-    yhi = shift_from(both[:, :, 0], "gy", -1)
+    xlo = shift_from(jnp.stack([velocity[-1], cotangent[-1]]), "gx", 1)
+    xhi = shift_from(jnp.stack([velocity[0], cotangent[0]]), "gx", -1)
+    ylo = shift_from(jnp.stack([velocity[:, -1], cotangent[:, -1]]), "gy", 1)
+    yhi = shift_from(jnp.stack([velocity[:, 0], cotangent[:, 0]]), "gy", -1)
+    vup, vdown, cup, cdown = z_neighbours(velocity, cotangent)
     padded = padded_of(velocity, xlo[0], xhi[0], ylo[0], yhi[0])
     cot_pad = padded_of(cotangent, xlo[1], xhi[1], ylo[1], yhi[1])
 
@@ -105,8 +127,8 @@
             padded[:-2, 1:-1],
             padded[1:-1, 2:],
             padded[1:-1, :-2],
-            jnp.roll(center, -1, 2),
-            jnp.roll(center, 1, 2),
+            vup,
+            vdown,
         ]
     ).astype(jnp.bfloat16).reshape(7, cells)
     h1 = jnp.tanh(jnp.dot(w_in, chosen, preferred_element_type=jnp.float32)).astype(jnp.bfloat16)
@@ -124,7 +146,7 @@
     gmid = lax.dot_general(da2, h1, dims, preferred_element_type=jnp.float32)
     gout = lax.dot_general(dcl[None, :], h2, dims, preferred_element_type=jnp.float32)
 
-    new_field = velocity + viscosity * padded_laplace(padded) + corr.reshape(sizex, sizey, sizez)
+    new_field = velocity + viscosity * padded_laplace(padded, vup, vdown) + corr.reshape(sizex, sizey, sizez)
 
     nx = lax.axis_size("gx")
     ny = lax.axis_size("gy")
@@ -163,7 +185,7 @@
     side3 = jnp.concatenate([from_ylo[:, None], dfeat[3, :, :-1]], axis=1)
     side4 = jnp.concatenate([dfeat[4, :, 1:], from_yhi[:, None]], axis=1)
     local = dfeat[0] + jnp.roll(dfeat[5], 1, 2) + jnp.roll(dfeat[6], -1, 2)
-    grad_field = cotangent + viscosity * padded_laplace(cot_pad) + local + (side1 + side2 + side3 + side4)
+    grad_field = cotangent + viscosity * padded_laplace(cot_pad, cup, cdown) + local + (side1 + side2 + side3 + side4)
 
     scale = 1.0 / jnp.sqrt(jnp.float32(nx * ny * slots * 64))
     total = grads * scale

time: 118 us -> 122 us (1.034)
  starting transfers between devices: 63.8 us -> 66.8 us
  Pallas kernels: 0 us -> 1.48 us
    ppermute x8, starting transfers between devices: 18.3 us -> 21.6 us  [body(): grads = grads + lax.ppermute(grads, ('gx', 'gy'), pairs)]
    ppermute x8, waiting for transfers between devices: 25.4 us -> 22.1 us  [body(): grads = grads + lax.ppermute(grads, ('gx', 'gy'), pairs)]
    ppermute x4, waiting for transfers between devices: 0.01 us -> 2.59 us  [shift_from(): lax.ppermute(face, axis, [(i, (i + step) % count) for i in range(count)])]
    pallas_call x0 -> x1, Pallas kernels: none -> 1.48 us  [z_neighbours(): pl.pallas_call(z_neighbours_kernel, out_shape=(out, out, out, out))]
    ppermute x2, starting transfers between devices: 6.62 us -> 5.21 us  [body(): got = lax.ppermute(message, ('gx', 'gy'), pairs)]
    slice x4 -> x3, local copies, waits for them, and re-layouts: 2.8 us -> 2.42 us  [the longest x2 1.68 us: body(): ylo = shift_from(jnp.stack([velocity[:, -1], cotangent[:, -1]]), 'gy', 1)]
  transfers between devices with their start and end apart: 16 -> 16, of which waited for: 9 -> 10; matrix products, arithmetic and copies ran while one was open for 9% -> 8% of each run, Pallas kernels for 0% -> 1%
where the time goes in v5:
time: 122 us; the launch traced here: 120 us
  starting transfers between devices  66.8 us (55%)
  waiting for transfers between devices  33.1 us (27%)
  local copies, waits for them, and re-layouts  8.27 us (7%)
  matrix products  4.99 us (4%)
  other arithmetic  3.48 us (3%)
  between operations  1.93 us (2%)
  Pallas kernels  1.48 us (1%)
    ppermute x4, starting transfers between devices, shift_from(): lax.ppermute(face, axis, [(i, (i + step) % count) for i in range(count)])  29.6 us
    ppermute x8, waiting for transfers between devices, body(): grads = grads + lax.ppermute(grads, ('gx', 'gy'), pairs)  22.1 us
    ppermute x8, starting transfers between devices, body(): grads = grads + lax.ppermute(grads, ('gx', 'gy'), pairs)  21.6 us
    ppermute x2, waiting for transfers between devices, body(): got = lax.ppermute(message, ('gx', 'gy'), pairs)  8.46 us
    ppermute x1, starting transfers between devices, body(): lax.ppermute(jnp.where(yodd, up_y, down_y), 'gy', [(i, (i + 1) % ny if i...  8.27 us
    ppermute x2, starting transfers between devices, body(): got = lax.ppermute(message, ('gx', 'gy'), pairs)  5.21 us
    ppermute x4, waiting for transfers between devices, shift_from(): lax.ppermute(face, axis, [(i, (i + step) % count) for i in range(count)])  2.59 us
  transfers between devices with their start and end apart: 16, of which 10 were waited for; matrix products, arithmetic and copies ran while one was open for 8% of the time, Pallas kernels for 1%

profile of v5, /device:TPU:14, one launch (start us, length us, event | category | flops | bytes accessed | tf_op | source)
XLA Modules:
  0.0 120.1 jit_solution(9550213797161106583)
XLA Ops:
  1.4 2.8 %collective-permute-start.2 = (f32[2,8,128]{2,1,0:T(8,128)S(1)}, f32[2,8,128]{2,1,0:T(8,128)S(1)}, u32[]{:S(2)}, u32[]{:S(2)}) collective-permute-start(f32[2,8,128]{2,1,0:T(8,128)S(1)} %pad_maximum_fusion.24), channel_id=1, source_target_pairs={{0,1008},{16,0},{32,16},{48,32},{64,48},{80,64},{96,80},{112,96},{... | collective-permute-start | bytes 24584 | tf_op jit(solution)/shard_map/ppermute | solution.py:13
  4.2 1.9 %collective-permute-start.3 = (f32[2,8,128]{2,1,0:T(8,128)S(1)}, f32[2,8,128]{2,1,0:T(8,128)S(1)}, u32[]{:S(2)}, u32[]{:S(2)}) collective-permute-start(f32[2,8,128]{2,1,0:T(8,128)S(1)} %pad_maximum_fusion.25), channel_id=1, source_target_pairs={{0,16},{16,32},{32,48},{48,64},{64,80},{80,96},{96,112},{112,128},... | collective-permute-start | bytes 24584 | tf_op jit(solution)/shard_map/ppermute | solution.py:13
  7.8 23.0 %collective-permute-start.1 = (f32[2,8,128]{2,1,0:T(8,128)S(1)}, f32[2,8,128]{2,1,0:T(8,128)S(1)}, u32[]{:S(2)}, u32[]{:S(2)}) collective-permute-start(f32[2,8,128]{2,1,0:T(8,128)S(1)} %pad_maximum_fusion.23), channel_id=1, source_target_pairs={{0,15},{1,0},{2,1},{3,2},{4,3},{5,4},{6,5},{7,6},{8,7},{9,8},{10,9... | collective-permute-start | bytes 24584 | tf_op jit(solution)/shard_map/ppermute | solution.py:13
  30.8 1.9 %collective-permute-start = (f32[2,8,128]{2,1,0:T(8,128)S(1)}, f32[2,8,128]{2,1,0:T(8,128)S(1)}, u32[]{:S(2)}, u32[]{:S(2)}) collective-permute-start(f32[2,8,128]{2,1,0:T(8,128)S(1)} %pad_maximum_fusion.22), channel_id=1, source_target_pairs={{0,1},{1,2},{2,3},{3,4},{4,5},{5,6},{6,7},{7,8},{8,9},{9,10},{10,1... | collective-permute-start | bytes 24584 | tf_op jit(solution)/shard_map/ppermute | solution.py:13
  39.8 2.6 %collective-permute-done = f32[2,8,128]{2,1,0:T(8,128)S(1)} collective-permute-done((f32[2,8,128]{2,1,0:T(8,128)S(1)}, f32[2,8,128]{2,1,0:T(8,128)S(1)}, u32[]{:S(2)}, u32[]{:S(2)}) %collective-permute-start) | collective-permute-done | bytes 8224 | tf_op jit(solution)/shard_map/ppermute | solution.py:13
  46.7 3.3 %collective-permute-start.4 = (f32[88,64]{0,1:T(8,128)S(1)}, f32[88,64]{0,1:T(8,128)S(1)}, u32[]{:S(2)}, u32[]{:S(2)}) collective-permute-start(f32[88,64]{0,1:T(8,128)S(1)} %pad_maximum_fusion.20), channel_id=1, source_target_pairs={{0,16},{1,17},{2,18},{3,19},{4,20},{5,21},{6,22},{7,23},{8,24},{9,... | collective-permute-start | bytes 67592 | tf_op jit(solution)/shard_map/ppermute | solution.py:175
  51.0 1.9 %collective-permute-start.6 = (f32[88,64]{0,1:T(8,128)S(1)}, f32[88,64]{0,1:T(8,128)S(1)}, u32[]{:S(2)}, u32[]{:S(2)}) collective-permute-start(f32[88,64]{0,1:T(8,128)S(1)} %pad_maximum_fusion.21), channel_id=1, source_target_pairs={{0,1},{1,0},{2,3},{3,2},{4,5},{5,4},{6,7},{7,6},{8,9},{9,8},{10,11... | collective-permute-start | bytes 67592 | tf_op jit(solution)/shard_map/ppermute | solution.py:175
  52.9 7.8 %collective-permute-done.6 = f32[88,64]{0,1:T(8,128)S(1)} collective-permute-done((f32[88,64]{0,1:T(8,128)S(1)}, f32[88,64]{0,1:T(8,128)S(1)}, u32[]{:S(2)}, u32[]{:S(2)}) %collective-permute-start.6) | collective-permute-done | bytes 22560 | tf_op jit(solution)/shard_map/ppermute | solution.py:175
  60.7 2.3 %collective-permute-start.8 = (f32[72,64]{0,1:T(8,128)S(1)}, f32[72,64]{0,1:T(8,128)S(1)}, u32[]{:S(2)}, u32[]{:S(2)}) collective-permute-start(f32[72,64]{0,1:T(8,128)S(1)} %slice_add_fusion), channel_id=1, source_target_pairs={{0,32},{1,33},{2,34},{3,35},{4,36},{5,37},{6,38},{7,39},{8,40},{9,... | collective-permute-start | bytes 55304 | tf_op jit(solution)/shard_map/ppermute | solution.py:170
  63.1 2.1 %collective-permute-start.5 = (f32[8,128]{1,0:T(8,128)S(1)}, f32[8,128]{1,0:T(8,128)S(1)}, u32[]{:S(2)}, u32[]{:S(2)}) collective-permute-start(f32[8,128]{1,0:T(8,128)S(1)} %get-tuple-element.37), channel_id=1, source_target_pairs={{0,1008},{16,32},{32,16},{48,64},{64,48},{80,96},{96,80},{112,128}... | collective-permute-start | bytes 12296 | tf_op jit(solution)/shard_map/ppermute | solution.py:158
  66.5 3.2 %collective-permute-start.9 = (f32[72,64]{0,1:T(8,128)S(1)}, f32[72,64]{0,1:T(8,128)S(1)}, u32[]{:S(2)}, u32[]{:S(2)}) collective-permute-start(f32[72,64]{0,1:T(8,128)S(1)} %add.129), channel_id=1, source_target_pairs={{0,64},{1,65},{2,66},{3,67},{4,68},{5,69},{6,70},{7,71},{8,72},{9,... | collective-permute-start | bytes 55304 | tf_op jit(solution)/shard_map/ppermute | solution.py:170
  70.3 3.3 %collective-permute-done.9 = f32[72,64]{0,1:T(8,128)S(1)} collective-permute-done((f32[72,64]{0,1:T(8,128)S(1)}, f32[72,64]{0,1:T(8,128)S(1)}, u32[]{:S(2)}, u32[]{:S(2)}) %collective-permute-start.9) | collective-permute-done | bytes 18464 | tf_op jit(solution)/shard_map/ppermute | solution.py:170
  73.7 4.4 %collective-permute-start.10 = (f32[72,64]{0,1:T(8,128)S(1)}, f32[72,64]{0,1:T(8,128)S(1)}, u32[]{:S(2)}, u32[]{:S(2)}) collective-permute-start(f32[72,64]{0,1:T(8,128)S(1)} %add.130), channel_id=1, source_target_pairs={{0,224},{1,225},{2,226},{3,227},{4,228},{5,229},{6,230},{7,231},{8... | collective-permute-start | bytes 55304 | tf_op jit(solution)/shard_map/ppermute | solution.py:170
  78.7 2.0 %collective-permute-done.10 = f32[72,64]{0,1:T(8,128)S(1)} collective-permute-done((f32[72,64]{0,1:T(8,128)S(1)}, f32[72,64]{0,1:T(8,128)S(1)}, u32[]{:S(2)}, u32[]{:S(2)}) %collective-permute-start.10) | collective-permute-done | bytes 18464 | tf_op jit(solution)/shard_map/ppermute | solution.py:170
  80.7 2.8 %collective-permute-start.11 = (f32[72,64]{0,1:T(8,128)S(1)}, f32[72,64]{0,1:T(8,128)S(1)}, u32[]{:S(2)}, u32[]{:S(2)}) collective-permute-start(f32[72,64]{0,1:T(8,128)S(1)} %add.131), channel_id=1, source_target_pairs={{0,256},{1,257},{2,258},{3,259},{4,260},{5,261},{6,262},{7,263},{8... | collective-permute-start | bytes 55304 | tf_op jit(solution)/shard_map/ppermute | solution.py:170
  83.6 2.9 %collective-permute-done.11 = f32[72,64]{0,1:T(8,128)S(1)} collective-permute-done((f32[72,64]{0,1:T(8,128)S(1)}, f32[72,64]{0,1:T(8,128)S(1)}, u32[]{:S(2)}, u32[]{:S(2)}) %collective-permute-start.11) | collective-permute-done | bytes 18464 | tf_op jit(solution)/shard_map/ppermute | solution.py:170
  86.5 3.2 %collective-permute-start.12 = (f32[72,64]{0,1:T(8,128)S(1)}, f32[72,64]{0,1:T(8,128)S(1)}, u32[]{:S(2)}, u32[]{:S(2)}) collective-permute-start(f32[72,64]{0,1:T(8,128)S(1)} %add.132), channel_id=1, source_target_pairs={{0,512},{1,513},{2,514},{3,515},{4,516},{5,517},{6,518},{7,519},{8... | collective-permute-start | bytes 55304 | tf_op jit(solution)/shard_map/ppermute | solution.py:170
  89.9 8.3 %collective-permute-start.7 = (f32[8,128]{1,0:T(8,128)S(1)}, f32[8,128]{1,0:T(8,128)S(1)}, u32[]{:S(2)}, u32[]{:S(2)}) collective-permute-start(f32[8,128]{1,0:T(8,128)S(1)} %get-tuple-element.53), channel_id=1, source_target_pairs={{0,15},{1,2},{2,1},{3,4},{4,3},{5,6},{6,5},{7,8},{8,7},{9,10},{10,... | collective-permute-start | bytes 12296 | tf_op jit(solution)/shard_map/ppermute | solution.py:161
  98.4 1.9 %collective-permute-start.13 = (f32[72,64]{0,1:T(8,128)S(1)}, f32[72,64]{0,1:T(8,128)S(1)}, u32[]{:S(2)}, u32[]{:S(2)}) collective-permute-start(f32[72,64]{0,1:T(8,128)S(1)} %add.133), channel_id=1, source_target_pairs={{0,2},{1,3},{2,0},{3,1},{4,6},{5,7},{6,4},{7,5},{8,10},{9,11},{10,... | collective-permute-start | bytes 55304 | tf_op jit(solution)/shard_map/ppermute | solution.py:170
  100.6 3.7 %collective-permute-done.13 = f32[72,64]{0,1:T(8,128)S(1)} collective-permute-done((f32[72,64]{0,1:T(8,128)S(1)}, f32[72,64]{0,1:T(8,128)S(1)}, u32[]{:S(2)}, u32[]{:S(2)}) %collective-permute-start.13) | collective-permute-done | bytes 18464 | tf_op jit(solution)/shard_map/ppermute | solution.py:170
  104.2 1.9 %collective-permute-start.14 = (f32[72,64]{0,1:T(8,128)S(1)}, f32[72,64]{0,1:T(8,128)S(1)}, u32[]{:S(2)}, u32[]{:S(2)}) collective-permute-start(f32[72,64]{0,1:T(8,128)S(1)} %add.134), channel_id=1, source_target_pairs={{0,4},{1,5},{2,6},{3,7},{4,0},{5,1},{6,2},{7,3},{8,12},{9,13},{10,... | collective-permute-start | bytes 55304 | tf_op jit(solution)/shard_map/ppermute | solution.py:170
  106.2 4.8 %collective-permute-done.14 = f32[72,64]{0,1:T(8,128)S(1)} collective-permute-done((f32[72,64]{0,1:T(8,128)S(1)}, f32[72,64]{0,1:T(8,128)S(1)}, u32[]{:S(2)}, u32[]{:S(2)}) %collective-permute-start.14) | collective-permute-done | bytes 18464 | tf_op jit(solution)/shard_map/ppermute | solution.py:170
  110.9 1.9 %collective-permute-start.15 = (f32[72,64]{0,1:T(8,128)S(1)}, f32[72,64]{0,1:T(8,128)S(1)}, u32[]{:S(2)}, u32[]{:S(2)}) collective-permute-start(f32[72,64]{0,1:T(8,128)S(1)} %add.135), channel_id=1, source_target_pairs={{0,14},{1,15},{2,12},{3,13},{4,10},{5,11},{6,8},{7,9},{8,6},{9,7},... | collective-permute-start | bytes 55304 | tf_op jit(solution)/shard_map/ppermute | solution.py:170
  113.6 4.3 %collective-permute-done.15 = f32[72,64]{0,1:T(8,128)S(1)} collective-permute-done((f32[72,64]{0,1:T(8,128)S(1)}, f32[72,64]{0,1:T(8,128)S(1)}, u32[]{:S(2)}, u32[]{:S(2)}) %collective-permute-start.15) | collective-permute-done | bytes 18464 | tf_op jit(solution)/shard_map/ppermute | solution.py:170
  (115 shorter events, 20.0 us)
Async XLA Ops:
  0.6 42.7 %copy-start = (bf16[64,64]{1,0:T(8,128)(2,1)S(1)}, bf16[64,64]{1,0:T(8,128)(2,1)}, u32[]{:S(2)}) copy-start(bf16[64,64]{1,0:T(8,128)(2,1)} %param.14) | copy-start | bytes 24580
  1.4 38.4 %collective-permute-start.2 = (f32[2,8,128]{2,1,0:T(8,128)S(1)}, f32[2,8,128]{2,1,0:T(8,128)S(1)}, u32[]{:S(2)}, u32[]{:S(2)}) collective-permute-start(f32[2,8,128]{2,1,0:T(8,128)S(1)} %pad_maximum_fusion.24), channel_id=1, source_target_pairs={{0,1008},{16,0},{32,16},{48,32},{64,48},{80,64},{96,80},{112,96},{... | collective-permute-start | bytes 24584 | tf_op jit(solution)/shard_map/ppermute | solution.py:13
  4.2 35.6 %collective-permute-start.3 = (f32[2,8,128]{2,1,0:T(8,128)S(1)}, f32[2,8,128]{2,1,0:T(8,128)S(1)}, u32[]{:S(2)}, u32[]{:S(2)}) collective-permute-start(f32[2,8,128]{2,1,0:T(8,128)S(1)} %pad_maximum_fusion.25), channel_id=1, source_target_pairs={{0,16},{16,32},{32,48},{48,64},{64,80},{80,96},{96,112},{112,128},... | collective-permute-start | bytes 24584 | tf_op jit(solution)/shard_map/ppermute | solution.py:13
  7.8 32.0 %collective-permute-start.1 = (f32[2,8,128]{2,1,0:T(8,128)S(1)}, f32[2,8,128]{2,1,0:T(8,128)S(1)}, u32[]{:S(2)}, u32[]{:S(2)}) collective-permute-start(f32[2,8,128]{2,1,0:T(8,128)S(1)} %pad_maximum_fusion.23), channel_id=1, source_target_pairs={{0,15},{1,0},{2,1},{3,2},{4,3},{5,4},{6,5},{7,6},{8,7},{9,8},{10,9... | collective-permute-start | bytes 24584 | tf_op jit(solution)/shard_map/ppermute | solution.py:13
  30.8 11.6 %collective-permute-start = (f32[2,8,128]{2,1,0:T(8,128)S(1)}, f32[2,8,128]{2,1,0:T(8,128)S(1)}, u32[]{:S(2)}, u32[]{:S(2)}) collective-permute-start(f32[2,8,128]{2,1,0:T(8,128)S(1)} %pad_maximum_fusion.22), channel_id=1, source_target_pairs={{0,1},{1,2},{2,3},{3,4},{4,5},{5,6},{6,7},{7,8},{8,9},{9,10},{10,1... | collective-permute-start | bytes 24584 | tf_op jit(solution)/shard_map/ppermute | solution.py:13
  36.0 3.6 %copy-start.1 = (f32[8,8,128]{2,1,0:T(8,128)S(1)}, f32[8,8,128]{2,1,0:T(8,128)}, u32[]{:S(2)}) copy-start(f32[8,8,128]{2,1,0:T(8,128)} %param.8) | copy-start | bytes 98308
  36.6 6.2 %copy-start.8 = (bf16[64,7]{0,1:T(8,128)(2,1)S(1)}, bf16[64,7]{0,1:T(8,128)(2,1)}, u32[]{:S(2)}) copy-start(bf16[64,7]{0,1:T(8,128)(2,1)} %param.13) | copy-start | bytes 2692
  46.7 4.1 %collective-permute-start.4 = (f32[88,64]{0,1:T(8,128)S(1)}, f32[88,64]{0,1:T(8,128)S(1)}, u32[]{:S(2)}, u32[]{:S(2)}) collective-permute-start(f32[88,64]{0,1:T(8,128)S(1)} %pad_maximum_fusion.20), channel_id=1, source_target_pairs={{0,16},{1,17},{2,18},{3,19},{4,20},{5,21},{6,22},{7,23},{8,24},{9,... | collective-permute-start | bytes 67592 | tf_op jit(solution)/shard_map/ppermute | solution.py:175
  51.0 9.7 %collective-permute-start.6 = (f32[88,64]{0,1:T(8,128)S(1)}, f32[88,64]{0,1:T(8,128)S(1)}, u32[]{:S(2)}, u32[]{:S(2)}) collective-permute-start(f32[88,64]{0,1:T(8,128)S(1)} %pad_maximum_fusion.21), channel_id=1, source_target_pairs={{0,1},{1,0},{2,3},{3,2},{4,5},{5,4},{6,7},{7,6},{8,9},{9,8},{10,11... | collective-permute-start | bytes 67592 | tf_op jit(solution)/shard_map/ppermute | solution.py:175
  60.7 5.8 %collective-permute-start.8 = (f32[72,64]{0,1:T(8,128)S(1)}, f32[72,64]{0,1:T(8,128)S(1)}, u32[]{:S(2)}, u32[]{:S(2)}) collective-permute-start(f32[72,64]{0,1:T(8,128)S(1)} %slice_add_fusion), channel_id=1, source_target_pairs={{0,32},{1,33},{2,34},{3,35},{4,36},{5,37},{6,38},{7,39},{8,40},{9,... | collective-permute-start | bytes 55304 | tf_op jit(solution)/shard_map/ppermute | solution.py:170
  63.1 37.3 %collective-permute-start.5 = (f32[8,128]{1,0:T(8,128)S(1)}, f32[8,128]{1,0:T(8,128)S(1)}, u32[]{:S(2)}, u32[]{:S(2)}) collective-permute-start(f32[8,128]{1,0:T(8,128)S(1)} %get-tuple-element.37), channel_id=1, source_target_pairs={{0,1008},{16,32},{32,16},{48,64},{64,48},{80,96},{96,80},{112,128}... | collective-permute-start | bytes 12296 | tf_op jit(solution)/shard_map/ppermute | solution.py:158
  65.4 12.6 %copy-start.4 = (f32[64,128]{1,0:T(8,128)S(1)}, f32[64,128]{1,0:T(8,128)}, u32[]{:S(2)}) copy-start(f32[64,128]{1,0:T(8,128)} %get-tuple-element.9) | copy-start | bytes 98308
  65.4 12.6 %copy-start.5 = (f32[64,128]{1,0:T(8,128)S(1)}, f32[64,128]{1,0:T(8,128)}, u32[]{:S(2)}) copy-start(f32[64,128]{1,0:T(8,128)} %get-tuple-element.10) | copy-start | bytes 98308
  66.5 7.2 %collective-permute-start.9 = (f32[72,64]{0,1:T(8,128)S(1)}, f32[72,64]{0,1:T(8,128)S(1)}, u32[]{:S(2)}, u32[]{:S(2)}) collective-permute-start(f32[72,64]{0,1:T(8,128)S(1)} %add.129), channel_id=1, source_target_pairs={{0,64},{1,65},{2,66},{3,67},{4,68},{5,69},{6,70},{7,71},{8,72},{9,... | collective-permute-start | bytes 55304 | tf_op jit(solution)/shard_map/ppermute | solution.py:170
  70.3 42.5 %copy-start.3 = (f32[8,8,128]{2,1,0:T(8,128)S(1)}, f32[8,8,128]{2,1,0:T(8,128)}, u32[]{:S(2)}) copy-start(f32[8,8,128]{2,1,0:T(8,128)} %param.9) | copy-start | bytes 98308
  70.3 42.6 %copy-start.6 = (f32[64,128]{1,0:T(8,128)S(1)}, f32[64,128]{1,0:T(8,128)}, u32[]{:S(2)}) copy-start(f32[64,128]{1,0:T(8,128)} %get-tuple-element.11) | copy-start | bytes 98308
  70.3 42.6 %copy-start.7 = (f32[64,128]{1,0:T(8,128)S(1)}, f32[64,128]{1,0:T(8,128)}, u32[]{:S(2)}) copy-start(f32[64,128]{1,0:T(8,128)} %get-tuple-element.12) | copy-start | bytes 98308
  73.7 7.0 %collective-permute-start.10 = (f32[72,64]{0,1:T(8,128)S(1)}, f32[72,64]{0,1:T(8,128)S(1)}, u32[]{:S(2)}, u32[]{:S(2)}) collective-permute-start(f32[72,64]{0,1:T(8,128)S(1)} %add.130), channel_id=1, source_target_pairs={{0,224},{1,225},{2,226},{3,227},{4,228},{5,229},{6,230},{7,231},{8... | collective-permute-start | bytes 55304 | tf_op jit(solution)/shard_map/ppermute | solution.py:170
  80.7 5.8 %collective-permute-start.11 = (f32[72,64]{0,1:T(8,128)S(1)}, f32[72,64]{0,1:T(8,128)S(1)}, u32[]{:S(2)}, u32[]{:S(2)}) collective-permute-start(f32[72,64]{0,1:T(8,128)S(1)} %add.131), channel_id=1, source_target_pairs={{0,256},{1,257},{2,258},{3,259},{4,260},{5,261},{6,262},{7,263},{8... | collective-permute-start | bytes 55304 | tf_op jit(solution)/shard_map/ppermute | solution.py:170
  86.5 11.9 %collective-permute-start.12 = (f32[72,64]{0,1:T(8,128)S(1)}, f32[72,64]{0,1:T(8,128)S(1)}, u32[]{:S(2)}, u32[]{:S(2)}) collective-permute-start(f32[72,64]{0,1:T(8,128)S(1)} %add.132), channel_id=1, source_target_pairs={{0,512},{1,513},{2,514},{3,515},{4,516},{5,517},{6,518},{7,519},{8... | collective-permute-start | bytes 55304 | tf_op jit(solution)/shard_map/ppermute | solution.py:170
  89.9 16.3 %collective-permute-start.7 = (f32[8,128]{1,0:T(8,128)S(1)}, f32[8,128]{1,0:T(8,128)S(1)}, u32[]{:S(2)}, u32[]{:S(2)}) collective-permute-start(f32[8,128]{1,0:T(8,128)S(1)} %get-tuple-element.53), channel_id=1, source_target_pairs={{0,15},{1,2},{2,1},{3,4},{4,3},{5,6},{6,5},{7,8},{8,7},{9,10},{10,... | collective-permute-start | bytes 12296 | tf_op jit(solution)/shard_map/ppermute | solution.py:161
  98.4 5.8 %collective-permute-start.13 = (f32[72,64]{0,1:T(8,128)S(1)}, f32[72,64]{0,1:T(8,128)S(1)}, u32[]{:S(2)}, u32[]{:S(2)}) collective-permute-start(f32[72,64]{0,1:T(8,128)S(1)} %add.133), channel_id=1, source_target_pairs={{0,2},{1,3},{2,0},{3,1},{4,6},{5,7},{6,4},{7,5},{8,10},{9,11},{10,... | collective-permute-start | bytes 55304 | tf_op jit(solution)/shard_map/ppermute | solution.py:170
  104.2 6.7 %collective-permute-start.14 = (f32[72,64]{0,1:T(8,128)S(1)}, f32[72,64]{0,1:T(8,128)S(1)}, u32[]{:S(2)}, u32[]{:S(2)}) collective-permute-start(f32[72,64]{0,1:T(8,128)S(1)} %add.134), channel_id=1, source_target_pairs={{0,4},{1,5},{2,6},{3,7},{4,0},{5,1},{6,2},{7,3},{8,12},{9,13},{10,... | collective-permute-start | bytes 55304 | tf_op jit(solution)/shard_map/ppermute | solution.py:170
  110.9 7.0 %collective-permute-start.15 = (f32[72,64]{0,1:T(8,128)S(1)}, f32[72,64]{0,1:T(8,128)S(1)}, u32[]{:S(2)}, u32[]{:S(2)}) collective-permute-start(f32[72,64]{0,1:T(8,128)S(1)} %add.135), channel_id=1, source_target_pairs={{0,14},{1,15},{2,12},{3,13},{4,10},{5,11},{6,8},{7,9},{8,6},{9,7},... | collective-permute-start | bytes 55304 | tf_op jit(solution)/shard_map/ppermute | solution.py:170
  (2 other events, 4.9 us)

commit v6 on v4

--- a/solution.py
+++ b/solution.py
@@ -21,9 +21,9 @@
             return ((c["y"] % 4) * 16 + c["x"] * 2 + c["core"]) * 16 + c["z"] * 2 + c["y"] // 4
 
         plan = [
+            ("x", lambda v: v ^ 1, None),
             ("core", lambda v: v ^ 1, "gx"),
             ("y", lambda v: v ^ 4, "gy"),
-            ("x", lambda v: v ^ 1, None),
             ("x", lambda v: v ^ 2, None),
             ("x", lambda v: 7 - v, None),
             ("y", lambda v: v ^ 1, None),
@@ -141,7 +141,11 @@
     )
 
     gin_t = lax.dot_general(chosen, da1, dims, preferred_element_type=jnp.float32)
-    grads = jnp.concatenate([gmid, gin_t, gout], axis=0)
+    width = gmid.shape[0]
+    lanes = 128
+    grads = jnp.concatenate(
+        [gmid.reshape(-1, lanes), jnp.concatenate([gin_t, gout], axis=0).reshape(-1, lanes)], axis=0
+    )
     received = {}
     for pairs, tag in reduce_rounds(nx, ny):
         if tag is None:
@@ -167,10 +171,11 @@
 
     scale = 1.0 / jnp.sqrt(jnp.float32(nx * ny * slots * 64))
     total = grads * scale
-    width = gmid.shape[0]
-    grad_mid = total[:width]
-    grad_in = total[width : width + 7].T
-    grad_out = total[width + 7 :]
+    mid_rows = width * width // lanes
+    grad_mid = total[:mid_rows].reshape(width, width)
+    rest = total[mid_rows:].reshape(-1, width)
+    grad_in = rest[:7].T
+    grad_out = rest[7:8]
     return (new_field, grad_field, grad_in, grad_mid, grad_out)
 
 

time: 118 us -> 116 us (0.983)
  waiting for transfers between devices: 33.8 us -> 30.1 us
  starting transfers between devices: 63.8 us -> 65.8 us
    ppermute x8, waiting for transfers between devices: 25.4 us -> 21.9 us  [body(): grads = grads + lax.ppermute(grads, ('gx', 'gy'), pairs)]
    ppermute x8, starting transfers between devices: 18.3 us -> 21.4 us  [body(): grads = grads + lax.ppermute(grads, ('gx', 'gy'), pairs)]
    unnamed x15, local copies, waits for them, and re-layouts: 2.3 us -> 0.35 us
  transfers between devices with their start and end apart: 16 -> 16, of which waited for: 9 -> 9; matrix products, arithmetic and copies ran while one was open for 9% -> 8% of each run, Pallas kernels for 0% -> 0%
where the time goes in v6:
time: 116 us; the launch traced here: 114 us
  starting transfers between devices  65.8 us (57%)
  waiting for transfers between devices  30.1 us (26%)
  local copies, waits for them, and re-layouts  9.46 us (8%)
  matrix products  4.33 us (4%)
  other arithmetic  2.66 us (2%)
  between operations  1.95 us (2%)
    ppermute x4, starting transfers between devices, shift_from(): lax.ppermute(face, axis, [(i, (i + step) % count) for i in range(count)])  29.4 us
    ppermute x8, waiting for transfers between devices, body(): grads = grads + lax.ppermute(grads, ('gx', 'gy'), pairs)  21.9 us
    ppermute x8, starting transfers between devices, body(): grads = grads + lax.ppermute(grads, ('gx', 'gy'), pairs)  21.4 us
    ppermute x2, waiting for transfers between devices, body(): got = lax.ppermute(message, ('gx', 'gy'), pairs)  8.16 us
    ppermute x1, starting transfers between devices, body(): lax.ppermute(jnp.where(yodd, up_y, down_y), 'gy', [(i, (i + 1) % ny if i...  7.56 us
    ppermute x2, starting transfers between devices, body(): got = lax.ppermute(message, ('gx', 'gy'), pairs)  5.48 us
    slice x4, local copies, waits for them, and re-layouts, padded_laplace(): total = total + jnp.roll(center, -1, 2) + jnp.roll(center, 1, 2)  3.64 us
  transfers between devices with their start and end apart: 16, of which 9 were waited for; matrix products, arithmetic and copies ran while one was open for 8% of the time, Pallas kernels for 0%

profile of v6, /device:TPU:14, one launch (start us, length us, event | category | flops | bytes accessed | tf_op | source)
XLA Modules:
  0.0 114.3 jit_solution(18316559070978838535)
XLA Ops:
  1.5 8.2 %collective-permute-start = (f32[2,8,128]{2,1,0:T(8,128)S(1)}, f32[2,8,128]{2,1,0:T(8,128)S(1)}, u32[]{:S(2)}, u32[]{:S(2)}) collective-permute-start(f32[2,8,128]{2,1,0:T(8,128)S(1)} %get-tuple-element.18), channel_id=1, source_target_pairs={{0,1},{1,2},{2,3},{3,4},{4,5},{5,6},{6,7},{7,8},{8,9},{9,10},{10,1... | collective-permute-start | bytes 24584 | tf_op jit(solution)/shard_map/ppermute | solution.py:11
  9.7 16.8 %collective-permute-start.1 = (f32[2,8,128]{2,1,0:T(8,128)S(1)}, f32[2,8,128]{2,1,0:T(8,128)S(1)}, u32[]{:S(2)}, u32[]{:S(2)}) collective-permute-start(f32[2,8,128]{2,1,0:T(8,128)S(1)} %get-tuple-element.19), channel_id=1, source_target_pairs={{0,15},{1,0},{2,1},{3,2},{4,3},{5,4},{6,5},{7,6},{8,7},{9,8},{10,9... | collective-permute-start | bytes 24584 | tf_op jit(solution)/shard_map/ppermute | solution.py:11
  26.5 2.5 %collective-permute-start.2 = (f32[2,8,128]{2,0,1:T(2,128)S(1)}, f32[2,8,128]{2,0,1:T(2,128)S(1)}, u32[]{:S(2)}, u32[]{:S(2)}) collective-permute-start(f32[2,8,128]{2,0,1:T(2,128)S(1)} %bitcast.158), channel_id=1, source_target_pairs={{0,1008},{16,0},{32,16},{48,32},{64,48},{80,64},{96,80},{112,96},{... | collective-permute-start | bytes 24584 | tf_op jit(solution)/shard_map/ppermute | solution.py:11
  29.0 1.9 %collective-permute-start.3 = (f32[2,8,128]{2,0,1:T(2,128)S(1)}, f32[2,8,128]{2,0,1:T(2,128)S(1)}, u32[]{:S(2)}, u32[]{:S(2)}) collective-permute-start(f32[2,8,128]{2,0,1:T(2,128)S(1)} %bitcast.157), channel_id=1, source_target_pairs={{0,16},{16,32},{32,48},{48,64},{64,80},{80,96},{96,112},{112,128},... | collective-permute-start | bytes 24584 | tf_op jit(solution)/shard_map/ppermute | solution.py:11
  42.9 3.3 %collective-permute-start.4 = (f32[36,128]{1,0:T(8,128)S(1)}, f32[36,128]{1,0:T(8,128)S(1)}, u32[]{:S(2)}, u32[]{:S(2)}) collective-permute-start(f32[36,128]{1,0:T(8,128)S(1)} %constant_dynamic-update-slice_fusion), channel_id=1, source_target_pairs={{0,32},{1,33},{2,34},{3,35},{4,36},{5,37},{6,38},{7,39},{8,40},{9,... | collective-permute-start | bytes 55304 | tf_op jit(solution)/shard_map/ppermute | solution.py:152
  46.3 2.2 %collective-permute-done.4 = f32[36,128]{1,0:T(8,128)S(1)} collective-permute-done((f32[36,128]{1,0:T(8,128)S(1)}, f32[36,128]{1,0:T(8,128)S(1)}, u32[]{:S(2)}, u32[]{:S(2)}) %collective-permute-start.4) | collective-permute-done | bytes 18464 | tf_op jit(solution)/shard_map/ppermute | solution.py:152
  48.6 3.6 %collective-permute-start.5 = (f32[44,128]{1,0:T(8,128)S(1)}, f32[44,128]{1,0:T(8,128)S(1)}, u32[]{:S(2)}, u32[]{:S(2)}) collective-permute-start(f32[44,128]{1,0:T(8,128)S(1)} %pad_maximum_fusion.18), channel_id=1, source_target_pairs={{0,16},{1,17},{2,18},{3,19},{4,20},{5,21},{6,22},{7,23},{8,24},{9,... | collective-permute-start | bytes 67592 | tf_op jit(solution)/shard_map/ppermute | solution.py:157
  53.0 1.9 %collective-permute-start.7 = (f32[44,128]{1,0:T(8,128)S(1)}, f32[44,128]{1,0:T(8,128)S(1)}, u32[]{:S(2)}, u32[]{:S(2)}) collective-permute-start(f32[44,128]{1,0:T(8,128)S(1)} %pad_maximum_fusion.19), channel_id=1, source_target_pairs={{0,1},{1,0},{2,3},{3,2},{4,5},{5,4},{6,7},{7,6},{8,9},{9,8},{10,11... | collective-permute-start | bytes 67592 | tf_op jit(solution)/shard_map/ppermute | solution.py:157
  55.3 7.3 %collective-permute-done.7 = f32[44,128]{1,0:T(8,128)S(1)} collective-permute-done((f32[44,128]{1,0:T(8,128)S(1)}, f32[44,128]{1,0:T(8,128)S(1)}, u32[]{:S(2)}, u32[]{:S(2)}) %collective-permute-start.7) | collective-permute-done | bytes 22560 | tf_op jit(solution)/shard_map/ppermute | solution.py:157
  62.6 2.9 %collective-permute-start.9 = (f32[36,128]{1,0:T(8,128)S(1)}, f32[36,128]{1,0:T(8,128)S(1)}, u32[]{:S(2)}, u32[]{:S(2)}) collective-permute-start(f32[36,128]{1,0:T(8,128)S(1)} %slice_add_fusion), channel_id=1, source_target_pairs={{0,64},{1,65},{2,66},{3,67},{4,68},{5,69},{6,70},{7,71},{8,72},{9,... | collective-permute-start | bytes 55304 | tf_op jit(solution)/shard_map/ppermute | solution.py:152
  66.2 3.0 %collective-permute-done.9 = f32[36,128]{1,0:T(8,128)S(1)} collective-permute-done((f32[36,128]{1,0:T(8,128)S(1)}, f32[36,128]{1,0:T(8,128)S(1)}, u32[]{:S(2)}, u32[]{:S(2)}) %collective-permute-start.9) | collective-permute-done | bytes 18464 | tf_op jit(solution)/shard_map/ppermute | solution.py:152
  69.2 3.1 %collective-permute-start.10 = (f32[36,128]{1,0:T(8,128)S(1)}, f32[36,128]{1,0:T(8,128)S(1)}, u32[]{:S(2)}, u32[]{:S(2)}) collective-permute-start(f32[36,128]{1,0:T(8,128)S(1)} %add.130), channel_id=1, source_target_pairs={{0,224},{1,225},{2,226},{3,227},{4,228},{5,229},{6,230},{7,231},{8... | collective-permute-start | bytes 55304 | tf_op jit(solution)/shard_map/ppermute | solution.py:152
  73.0 3.1 %collective-permute-done.10 = f32[36,128]{1,0:T(8,128)S(1)} collective-permute-done((f32[36,128]{1,0:T(8,128)S(1)}, f32[36,128]{1,0:T(8,128)S(1)}, u32[]{:S(2)}, u32[]{:S(2)}) %collective-permute-start.10) | collective-permute-done | bytes 18464 | tf_op jit(solution)/shard_map/ppermute | solution.py:152
  76.1 2.7 %collective-permute-start.11 = (f32[36,128]{1,0:T(8,128)S(1)}, f32[36,128]{1,0:T(8,128)S(1)}, u32[]{:S(2)}, u32[]{:S(2)}) collective-permute-start(f32[36,128]{1,0:T(8,128)S(1)} %add.131), channel_id=1, source_target_pairs={{0,256},{1,257},{2,258},{3,259},{4,260},{5,261},{6,262},{7,263},{8... | collective-permute-start | bytes 55304 | tf_op jit(solution)/shard_map/ppermute | solution.py:152
  78.8 1.9 %collective-permute-start.6 = (f32[8,128]{1,0:T(8,128)S(1)}, f32[8,128]{1,0:T(8,128)S(1)}, u32[]{:S(2)}, u32[]{:S(2)}) collective-permute-start(f32[8,128]{1,0:T(8,128)S(1)} %get-tuple-element.15), channel_id=1, source_target_pairs={{0,1008},{16,32},{32,16},{48,64},{64,48},{80,96},{96,80},{112,128}... | collective-permute-start | bytes 12296 | tf_op jit(solution)/shard_map/ppermute | solution.py:136
  80.7 1.0 collective-permute-done.11
  81.8 3.7 %collective-permute-start.12 = (f32[36,128]{1,0:T(8,128)S(1)}, f32[36,128]{1,0:T(8,128)S(1)}, u32[]{:S(2)}, u32[]{:S(2)}) collective-permute-start(f32[36,128]{1,0:T(8,128)S(1)} %add.132), channel_id=1, source_target_pairs={{0,512},{1,513},{2,514},{3,515},{4,516},{5,517},{6,518},{7,519},{8... | collective-permute-start | bytes 55304 | tf_op jit(solution)/shard_map/ppermute | solution.py:152
  85.7 7.6 %collective-permute-start.8 = (f32[8,128]{1,0:T(8,128)S(1)}, f32[8,128]{1,0:T(8,128)S(1)}, u32[]{:S(2)}, u32[]{:S(2)}) collective-permute-start(f32[8,128]{1,0:T(8,128)S(1)} %get-tuple-element.37), channel_id=1, source_target_pairs={{0,15},{1,2},{2,1},{3,4},{4,3},{5,6},{6,5},{7,8},{8,7},{9,10},{10,... | collective-permute-start | bytes 12296 | tf_op jit(solution)/shard_map/ppermute | solution.py:139
  93.3 1.9 %collective-permute-start.13 = (f32[36,128]{1,0:T(8,128)S(1)}, f32[36,128]{1,0:T(8,128)S(1)}, u32[]{:S(2)}, u32[]{:S(2)}) collective-permute-start(f32[36,128]{1,0:T(8,128)S(1)} %add.133), channel_id=1, source_target_pairs={{0,2},{1,3},{2,0},{3,1},{4,6},{5,7},{6,4},{7,5},{8,10},{9,11},{10,... | collective-permute-start | bytes 55304 | tf_op jit(solution)/shard_map/ppermute | solution.py:152
  95.2 3.7 %collective-permute-done.13 = f32[36,128]{1,0:T(8,128)S(1)} collective-permute-done((f32[36,128]{1,0:T(8,128)S(1)}, f32[36,128]{1,0:T(8,128)S(1)}, u32[]{:S(2)}, u32[]{:S(2)}) %collective-permute-start.13) | collective-permute-done | bytes 18464 | tf_op jit(solution)/shard_map/ppermute | solution.py:152
  98.9 1.9 %collective-permute-start.14 = (f32[36,128]{1,0:T(8,128)S(1)}, f32[36,128]{1,0:T(8,128)S(1)}, u32[]{:S(2)}, u32[]{:S(2)}) collective-permute-start(f32[36,128]{1,0:T(8,128)S(1)} %add.134), channel_id=1, source_target_pairs={{0,4},{1,5},{2,6},{3,7},{4,0},{5,1},{6,2},{7,3},{8,12},{9,13},{10,... | collective-permute-start | bytes 55304 | tf_op jit(solution)/shard_map/ppermute | solution.py:152
  100.9 4.6 %collective-permute-done.14 = f32[36,128]{1,0:T(8,128)S(1)} collective-permute-done((f32[36,128]{1,0:T(8,128)S(1)}, f32[36,128]{1,0:T(8,128)S(1)}, u32[]{:S(2)}, u32[]{:S(2)}) %collective-permute-start.14) | collective-permute-done | bytes 18464 | tf_op jit(solution)/shard_map/ppermute | solution.py:152
  105.5 1.9 %collective-permute-start.15 = (f32[36,128]{1,0:T(8,128)S(1)}, f32[36,128]{1,0:T(8,128)S(1)}, u32[]{:S(2)}, u32[]{:S(2)}) collective-permute-start(f32[36,128]{1,0:T(8,128)S(1)} %add.135), channel_id=1, source_target_pairs={{0,14},{1,15},{2,12},{3,13},{4,10},{5,11},{6,8},{7,9},{8,6},{9,7},... | collective-permute-start | bytes 55304 | tf_op jit(solution)/shard_map/ppermute | solution.py:152
  108.1 4.2 %collective-permute-done.15 = f32[36,128]{1,0:T(8,128)S(1)} collective-permute-done((f32[36,128]{1,0:T(8,128)S(1)}, f32[36,128]{1,0:T(8,128)S(1)}, u32[]{:S(2)}, u32[]{:S(2)}) %collective-permute-start.15) | collective-permute-done | bytes 18464 | tf_op jit(solution)/shard_map/ppermute | solution.py:152
  (107 shorter events, 17.3 us)
Async XLA Ops:
  0.6 39.2 %copy-start = (bf16[64,64]{1,0:T(8,128)(2,1)S(1)}, bf16[64,64]{1,0:T(8,128)(2,1)}, u32[]{:S(2)}) copy-start(bf16[64,64]{1,0:T(8,128)(2,1)} %param.14) | copy-start | bytes 24580
  0.6 35.7 %copy-start.4 = (s32[1,1,128]{2,1,0:T(1,128)S(1)}, s32[1,1,128]{2,1,0:T(1,128)}, u32[]{:S(2)}) copy-start(s32[1,1,128]{2,1,0:T(1,128)} %param.10) | copy-start | bytes 1540
  1.5 37.2 %collective-permute-start = (f32[2,8,128]{2,1,0:T(8,128)S(1)}, f32[2,8,128]{2,1,0:T(8,128)S(1)}, u32[]{:S(2)}, u32[]{:S(2)}) collective-permute-start(f32[2,8,128]{2,1,0:T(8,128)S(1)} %get-tuple-element.18), channel_id=1, source_target_pairs={{0,1},{1,2},{2,3},{3,4},{4,5},{5,6},{6,7},{7,8},{8,9},{9,10},{10,1... | collective-permute-start | bytes 24584 | tf_op jit(solution)/shard_map/ppermute | solution.py:11
  9.7 29.1 %collective-permute-start.1 = (f32[2,8,128]{2,1,0:T(8,128)S(1)}, f32[2,8,128]{2,1,0:T(8,128)S(1)}, u32[]{:S(2)}, u32[]{:S(2)}) collective-permute-start(f32[2,8,128]{2,1,0:T(8,128)S(1)} %get-tuple-element.19), channel_id=1, source_target_pairs={{0,15},{1,0},{2,1},{3,2},{4,3},{5,4},{6,5},{7,6},{8,7},{9,8},{10,9... | collective-permute-start | bytes 24584 | tf_op jit(solution)/shard_map/ppermute | solution.py:11
  26.5 12.2 %collective-permute-start.2 = (f32[2,8,128]{2,0,1:T(2,128)S(1)}, f32[2,8,128]{2,0,1:T(2,128)S(1)}, u32[]{:S(2)}, u32[]{:S(2)}) collective-permute-start(f32[2,8,128]{2,0,1:T(2,128)S(1)} %bitcast.158), channel_id=1, source_target_pairs={{0,1008},{16,0},{32,16},{48,32},{64,48},{80,64},{96,80},{112,96},{... | collective-permute-start | bytes 24584 | tf_op jit(solution)/shard_map/ppermute | solution.py:11
  29.0 9.8 %collective-permute-start.3 = (f32[2,8,128]{2,0,1:T(2,128)S(1)}, f32[2,8,128]{2,0,1:T(2,128)S(1)}, u32[]{:S(2)}, u32[]{:S(2)}) collective-permute-start(f32[2,8,128]{2,0,1:T(2,128)S(1)} %bitcast.157), channel_id=1, source_target_pairs={{0,16},{16,32},{32,48},{48,64},{64,80},{80,96},{96,112},{112,128},... | collective-permute-start | bytes 24584 | tf_op jit(solution)/shard_map/ppermute | solution.py:11
  37.1 1.3 %copy-start.5 = (bf16[1,64]{1,0:T(2,128)(2,1)S(1)}, bf16[1,64]{1,0:T(2,128)(2,1)}, u32[]{:S(2)}) copy-start(bf16[1,64]{1,0:T(2,128)(2,1)} %param.15) | copy-start | bytes 388
  37.1 1.3 %copy-start.1 = (f32[8,8,128]{2,1,0:T(8,128)S(1)}, f32[8,8,128]{2,1,0:T(8,128)}, u32[]{:S(2)}) copy-start(f32[8,8,128]{2,1,0:T(8,128)} %param.9) | copy-start | bytes 98308
  37.1 1.5 %copy-start.2 = (f32[8,8,128]{2,1,0:T(8,128)S(1)}, f32[8,8,128]{2,1,0:T(8,128)}, u32[]{:S(2)}) copy-start(f32[8,8,128]{2,1,0:T(8,128)} %param.8) | copy-start | bytes 98308
  37.8 1.5 %copy-start.3 = (bf16[64,7]{0,1:T(8,128)(2,1)S(1)}, bf16[64,7]{0,1:T(8,128)(2,1)}, u32[]{:S(2)}) copy-start(bf16[64,7]{0,1:T(8,128)(2,1)} %param.13) | copy-start | bytes 2692
  42.9 5.7 %collective-permute-start.4 = (f32[36,128]{1,0:T(8,128)S(1)}, f32[36,128]{1,0:T(8,128)S(1)}, u32[]{:S(2)}, u32[]{:S(2)}) collective-permute-start(f32[36,128]{1,0:T(8,128)S(1)} %constant_dynamic-update-slice_fusion), channel_id=1, source_target_pairs={{0,32},{1,33},{2,34},{3,35},{4,36},{5,37},{6,38},{7,39},{8,40},{9,... | collective-permute-start | bytes 55304 | tf_op jit(solution)/shard_map/ppermute | solution.py:152
  48.6 4.4 %collective-permute-start.5 = (f32[44,128]{1,0:T(8,128)S(1)}, f32[44,128]{1,0:T(8,128)S(1)}, u32[]{:S(2)}, u32[]{:S(2)}) collective-permute-start(f32[44,128]{1,0:T(8,128)S(1)} %pad_maximum_fusion.18), channel_id=1, source_target_pairs={{0,16},{1,17},{2,18},{3,19},{4,20},{5,21},{6,22},{7,23},{8,24},{9,... | collective-permute-start | bytes 67592 | tf_op jit(solution)/shard_map/ppermute | solution.py:157
  53.0 9.6 %collective-permute-start.7 = (f32[44,128]{1,0:T(8,128)S(1)}, f32[44,128]{1,0:T(8,128)S(1)}, u32[]{:S(2)}, u32[]{:S(2)}) collective-permute-start(f32[44,128]{1,0:T(8,128)S(1)} %pad_maximum_fusion.19), channel_id=1, source_target_pairs={{0,1},{1,0},{2,3},{3,2},{4,5},{5,4},{6,7},{7,6},{8,9},{9,8},{10,11... | collective-permute-start | bytes 67592 | tf_op jit(solution)/shard_map/ppermute | solution.py:157
  62.6 6.6 %collective-permute-start.9 = (f32[36,128]{1,0:T(8,128)S(1)}, f32[36,128]{1,0:T(8,128)S(1)}, u32[]{:S(2)}, u32[]{:S(2)}) collective-permute-start(f32[36,128]{1,0:T(8,128)S(1)} %slice_add_fusion), channel_id=1, source_target_pairs={{0,64},{1,65},{2,66},{3,67},{4,68},{5,69},{6,70},{7,71},{8,72},{9,... | collective-permute-start | bytes 55304 | tf_op jit(solution)/shard_map/ppermute | solution.py:152
  69.2 6.9 %collective-permute-start.10 = (f32[36,128]{1,0:T(8,128)S(1)}, f32[36,128]{1,0:T(8,128)S(1)}, u32[]{:S(2)}, u32[]{:S(2)}) collective-permute-start(f32[36,128]{1,0:T(8,128)S(1)} %add.130), channel_id=1, source_target_pairs={{0,224},{1,225},{2,226},{3,227},{4,228},{5,229},{6,230},{7,231},{8... | collective-permute-start | bytes 55304 | tf_op jit(solution)/shard_map/ppermute | solution.py:152
  76.1 5.7 %collective-permute-start.11 = (f32[36,128]{1,0:T(8,128)S(1)}, f32[36,128]{1,0:T(8,128)S(1)}, u32[]{:S(2)}, u32[]{:S(2)}) collective-permute-start(f32[36,128]{1,0:T(8,128)S(1)} %add.131), channel_id=1, source_target_pairs={{0,256},{1,257},{2,258},{3,259},{4,260},{5,261},{6,262},{7,263},{8... | collective-permute-start | bytes 55304 | tf_op jit(solution)/shard_map/ppermute | solution.py:152
  78.8 16.4 %collective-permute-start.6 = (f32[8,128]{1,0:T(8,128)S(1)}, f32[8,128]{1,0:T(8,128)S(1)}, u32[]{:S(2)}, u32[]{:S(2)}) collective-permute-start(f32[8,128]{1,0:T(8,128)S(1)} %get-tuple-element.15), channel_id=1, source_target_pairs={{0,1008},{16,32},{32,16},{48,64},{64,48},{80,96},{96,80},{112,128}... | collective-permute-start | bytes 12296 | tf_op jit(solution)/shard_map/ppermute | solution.py:136
  81.8 11.5 %collective-permute-start.12 = (f32[36,128]{1,0:T(8,128)S(1)}, f32[36,128]{1,0:T(8,128)S(1)}, u32[]{:S(2)}, u32[]{:S(2)}) collective-permute-start(f32[36,128]{1,0:T(8,128)S(1)} %add.132), channel_id=1, source_target_pairs={{0,512},{1,513},{2,514},{3,515},{4,516},{5,517},{6,518},{7,519},{8... | collective-permute-start | bytes 55304 | tf_op jit(solution)/shard_map/ppermute | solution.py:152
  85.7 15.2 %collective-permute-start.8 = (f32[8,128]{1,0:T(8,128)S(1)}, f32[8,128]{1,0:T(8,128)S(1)}, u32[]{:S(2)}, u32[]{:S(2)}) collective-permute-start(f32[8,128]{1,0:T(8,128)S(1)} %get-tuple-element.37), channel_id=1, source_target_pairs={{0,15},{1,2},{2,1},{3,4},{4,3},{5,6},{6,5},{7,8},{8,7},{9,10},{10,... | collective-permute-start | bytes 12296 | tf_op jit(solution)/shard_map/ppermute | solution.py:139
  93.3 5.7 %collective-permute-start.13 = (f32[36,128]{1,0:T(8,128)S(1)}, f32[36,128]{1,0:T(8,128)S(1)}, u32[]{:S(2)}, u32[]{:S(2)}) collective-permute-start(f32[36,128]{1,0:T(8,128)S(1)} %add.133), channel_id=1, source_target_pairs={{0,2},{1,3},{2,0},{3,1},{4,6},{5,7},{6,4},{7,5},{8,10},{9,11},{10,... | collective-permute-start | bytes 55304 | tf_op jit(solution)/shard_map/ppermute | solution.py:152
  98.9 6.6 %collective-permute-start.14 = (f32[36,128]{1,0:T(8,128)S(1)}, f32[36,128]{1,0:T(8,128)S(1)}, u32[]{:S(2)}, u32[]{:S(2)}) collective-permute-start(f32[36,128]{1,0:T(8,128)S(1)} %add.134), channel_id=1, source_target_pairs={{0,4},{1,5},{2,6},{3,7},{4,0},{5,1},{6,2},{7,3},{8,12},{9,13},{10,... | collective-permute-start | bytes 55304 | tf_op jit(solution)/shard_map/ppermute | solution.py:152
  105.5 6.9 %collective-permute-start.15 = (f32[36,128]{1,0:T(8,128)S(1)}, f32[36,128]{1,0:T(8,128)S(1)}, u32[]{:S(2)}, u32[]{:S(2)}) collective-permute-start(f32[36,128]{1,0:T(8,128)S(1)} %add.135), channel_id=1, source_target_pairs={{0,14},{1,15},{2,12},{3,13},{4,10},{5,11},{6,8},{7,9},{8,6},{9,7},... | collective-permute-start | bytes 55304 | tf_op jit(solution)/shard_map/ppermute | solution.py:152

commit v7 on v6

--- a/solution.py
+++ b/solution.py
@@ -25,12 +25,12 @@
             ("core", lambda v: v ^ 1, "gx"),
             ("y", lambda v: v ^ 4, "gy"),
             ("x", lambda v: v ^ 2, None),
-            ("x", lambda v: 7 - v, None),
+            ("x", lambda v: v ^ 6, None),
             ("y", lambda v: v ^ 1, None),
             ("y", lambda v: v ^ 2, None),
             ("z", lambda v: v ^ 1, None),
             ("z", lambda v: v ^ 2, None),
-            ("z", lambda v: 7 - v, None),
+            ("z", lambda v: v ^ 6, None),
         ]
         rounds = []
         for ring, step, tag in plan:

time: 116 us -> 117 us (level)
  waiting for transfers between devices: 30.1 us -> 32.4 us
    ppermute x8, waiting for transfers between devices: 21.9 us -> 24.3 us  [body(): grads = grads + lax.ppermute(grads, ('gx', 'gy'), pairs)]
where the time goes in v7:
time: 117 us; the launch traced here: 116 us
  starting transfers between devices  65.2 us (56%)
  waiting for transfers between devices  32.4 us (28%)
  local copies, waits for them, and re-layouts  9.46 us (8%)
  matrix products  4.33 us (4%)
  other arithmetic  2.66 us (2%)
  between operations  1.95 us (2%)
    ppermute x4, starting transfers between devices, shift_from(): lax.ppermute(face, axis, [(i, (i + step) % count) for i in range(count)])  29.4 us
    ppermute x8, waiting for transfers between devices, body(): grads = grads + lax.ppermute(grads, ('gx', 'gy'), pairs)  24.3 us
    ppermute x8, starting transfers between devices, body(): grads = grads + lax.ppermute(grads, ('gx', 'gy'), pairs)  20.9 us
    ppermute x2, waiting for transfers between devices, body(): got = lax.ppermute(message, ('gx', 'gy'), pairs)  8.16 us
    ppermute x1, starting transfers between devices, body(): lax.ppermute(jnp.where(yodd, up_y, down_y), 'gy', [(i, (i + 1) % ny if i...  7.56 us
    ppermute x2, starting transfers between devices, body(): got = lax.ppermute(message, ('gx', 'gy'), pairs)  5.48 us
    slice x4, local copies, waits for them, and re-layouts, padded_laplace(): total = total + jnp.roll(center, -1, 2) + jnp.roll(center, 1, 2)  3.64 us
  transfers between devices with their start and end apart: 16, of which 9 were waited for; matrix products, arithmetic and copies ran while one was open for 8% of the time, Pallas kernels for 0%

profile of v7, /device:TPU:14, one launch (start us, length us, event | category | flops | bytes accessed | tf_op | source)
XLA Modules:
  0.0 116.1 jit_solution(8129925521230687674)
XLA Ops:
  1.5 8.2 %collective-permute-start = (f32[2,8,128]{2,1,0:T(8,128)S(1)}, f32[2,8,128]{2,1,0:T(8,128)S(1)}, u32[]{:S(2)}, u32[]{:S(2)}) collective-permute-start(f32[2,8,128]{2,1,0:T(8,128)S(1)} %get-tuple-element.18), channel_id=1, source_target_pairs={{0,1},{1,2},{2,3},{3,4},{4,5},{5,6},{6,7},{7,8},{8,9},{9,10},{10,1... | collective-permute-start | bytes 24584 | tf_op jit(solution)/shard_map/ppermute | solution.py:11
  9.7 16.8 %collective-permute-start.1 = (f32[2,8,128]{2,1,0:T(8,128)S(1)}, f32[2,8,128]{2,1,0:T(8,128)S(1)}, u32[]{:S(2)}, u32[]{:S(2)}) collective-permute-start(f32[2,8,128]{2,1,0:T(8,128)S(1)} %get-tuple-element.19), channel_id=1, source_target_pairs={{0,15},{1,0},{2,1},{3,2},{4,3},{5,4},{6,5},{7,6},{8,7},{9,8},{10,9... | collective-permute-start | bytes 24584 | tf_op jit(solution)/shard_map/ppermute | solution.py:11
  26.5 2.5 %collective-permute-start.2 = (f32[2,8,128]{2,0,1:T(2,128)S(1)}, f32[2,8,128]{2,0,1:T(2,128)S(1)}, u32[]{:S(2)}, u32[]{:S(2)}) collective-permute-start(f32[2,8,128]{2,0,1:T(2,128)S(1)} %bitcast.158), channel_id=1, source_target_pairs={{0,1008},{16,0},{32,16},{48,32},{64,48},{80,64},{96,80},{112,96},{... | collective-permute-start | bytes 24584 | tf_op jit(solution)/shard_map/ppermute | solution.py:11
  29.0 1.9 %collective-permute-start.3 = (f32[2,8,128]{2,0,1:T(2,128)S(1)}, f32[2,8,128]{2,0,1:T(2,128)S(1)}, u32[]{:S(2)}, u32[]{:S(2)}) collective-permute-start(f32[2,8,128]{2,0,1:T(2,128)S(1)} %bitcast.157), channel_id=1, source_target_pairs={{0,16},{16,32},{32,48},{48,64},{64,80},{80,96},{96,112},{112,128},... | collective-permute-start | bytes 24584 | tf_op jit(solution)/shard_map/ppermute | solution.py:11
  42.9 3.3 %collective-permute-start.4 = (f32[36,128]{1,0:T(8,128)S(1)}, f32[36,128]{1,0:T(8,128)S(1)}, u32[]{:S(2)}, u32[]{:S(2)}) collective-permute-start(f32[36,128]{1,0:T(8,128)S(1)} %constant_dynamic-update-slice_fusion), channel_id=1, source_target_pairs={{0,32},{1,33},{2,34},{3,35},{4,36},{5,37},{6,38},{7,39},{8,40},{9,... | collective-permute-start | bytes 55304 | tf_op jit(solution)/shard_map/ppermute | solution.py:152
  46.3 2.2 %collective-permute-done.4 = f32[36,128]{1,0:T(8,128)S(1)} collective-permute-done((f32[36,128]{1,0:T(8,128)S(1)}, f32[36,128]{1,0:T(8,128)S(1)}, u32[]{:S(2)}, u32[]{:S(2)}) %collective-permute-start.4) | collective-permute-done | bytes 18464 | tf_op jit(solution)/shard_map/ppermute | solution.py:152
  48.6 3.6 %collective-permute-start.5 = (f32[44,128]{1,0:T(8,128)S(1)}, f32[44,128]{1,0:T(8,128)S(1)}, u32[]{:S(2)}, u32[]{:S(2)}) collective-permute-start(f32[44,128]{1,0:T(8,128)S(1)} %pad_maximum_fusion.18), channel_id=1, source_target_pairs={{0,16},{1,17},{2,18},{3,19},{4,20},{5,21},{6,22},{7,23},{8,24},{9,... | collective-permute-start | bytes 67592 | tf_op jit(solution)/shard_map/ppermute | solution.py:157
  53.0 1.9 %collective-permute-start.7 = (f32[44,128]{1,0:T(8,128)S(1)}, f32[44,128]{1,0:T(8,128)S(1)}, u32[]{:S(2)}, u32[]{:S(2)}) collective-permute-start(f32[44,128]{1,0:T(8,128)S(1)} %pad_maximum_fusion.19), channel_id=1, source_target_pairs={{0,1},{1,0},{2,3},{3,2},{4,5},{5,4},{6,7},{7,6},{8,9},{9,8},{10,11... | collective-permute-start | bytes 67592 | tf_op jit(solution)/shard_map/ppermute | solution.py:157
  55.3 7.3 %collective-permute-done.7 = f32[44,128]{1,0:T(8,128)S(1)} collective-permute-done((f32[44,128]{1,0:T(8,128)S(1)}, f32[44,128]{1,0:T(8,128)S(1)}, u32[]{:S(2)}, u32[]{:S(2)}) %collective-permute-start.7) | collective-permute-done | bytes 22560 | tf_op jit(solution)/shard_map/ppermute | solution.py:157
  62.6 2.9 %collective-permute-start.9 = (f32[36,128]{1,0:T(8,128)S(1)}, f32[36,128]{1,0:T(8,128)S(1)}, u32[]{:S(2)}, u32[]{:S(2)}) collective-permute-start(f32[36,128]{1,0:T(8,128)S(1)} %slice_add_fusion), channel_id=1, source_target_pairs={{0,64},{1,65},{2,66},{3,67},{4,68},{5,69},{6,70},{7,71},{8,72},{9,... | collective-permute-start | bytes 55304 | tf_op jit(solution)/shard_map/ppermute | solution.py:152
  66.2 3.0 %collective-permute-done.9 = f32[36,128]{1,0:T(8,128)S(1)} collective-permute-done((f32[36,128]{1,0:T(8,128)S(1)}, f32[36,128]{1,0:T(8,128)S(1)}, u32[]{:S(2)}, u32[]{:S(2)}) %collective-permute-start.9) | collective-permute-done | bytes 18464 | tf_op jit(solution)/shard_map/ppermute | solution.py:152
  69.2 2.5 %collective-permute-start.10 = (f32[36,128]{1,0:T(8,128)S(1)}, f32[36,128]{1,0:T(8,128)S(1)}, u32[]{:S(2)}, u32[]{:S(2)}) collective-permute-start(f32[36,128]{1,0:T(8,128)S(1)} %add.130), channel_id=1, source_target_pairs={{0,192},{1,193},{2,194},{3,195},{4,196},{5,197},{6,198},{7,199},{8... | collective-permute-start | bytes 55304 | tf_op jit(solution)/shard_map/ppermute | solution.py:152
  72.4 4.5 %collective-permute-done.10 = f32[36,128]{1,0:T(8,128)S(1)} collective-permute-done((f32[36,128]{1,0:T(8,128)S(1)}, f32[36,128]{1,0:T(8,128)S(1)}, u32[]{:S(2)}, u32[]{:S(2)}) %collective-permute-start.10) | collective-permute-done | bytes 18464 | tf_op jit(solution)/shard_map/ppermute | solution.py:152
  77.0 2.7 %collective-permute-start.11 = (f32[36,128]{1,0:T(8,128)S(1)}, f32[36,128]{1,0:T(8,128)S(1)}, u32[]{:S(2)}, u32[]{:S(2)}) collective-permute-start(f32[36,128]{1,0:T(8,128)S(1)} %add.131), channel_id=1, source_target_pairs={{0,256},{1,257},{2,258},{3,259},{4,260},{5,261},{6,262},{7,263},{8... | collective-permute-start | bytes 55304 | tf_op jit(solution)/shard_map/ppermute | solution.py:152
  79.7 1.9 %collective-permute-start.6 = (f32[8,128]{1,0:T(8,128)S(1)}, f32[8,128]{1,0:T(8,128)S(1)}, u32[]{:S(2)}, u32[]{:S(2)}) collective-permute-start(f32[8,128]{1,0:T(8,128)S(1)} %get-tuple-element.15), channel_id=1, source_target_pairs={{0,1008},{16,32},{32,16},{48,64},{64,48},{80,96},{96,80},{112,128}... | collective-permute-start | bytes 12296 | tf_op jit(solution)/shard_map/ppermute | solution.py:136
  81.6 1.0 collective-permute-done.11
  82.7 3.7 %collective-permute-start.12 = (f32[36,128]{1,0:T(8,128)S(1)}, f32[36,128]{1,0:T(8,128)S(1)}, u32[]{:S(2)}, u32[]{:S(2)}) collective-permute-start(f32[36,128]{1,0:T(8,128)S(1)} %add.132), channel_id=1, source_target_pairs={{0,512},{1,513},{2,514},{3,515},{4,516},{5,517},{6,518},{7,519},{8... | collective-permute-start | bytes 55304 | tf_op jit(solution)/shard_map/ppermute | solution.py:152
  86.6 7.6 %collective-permute-start.8 = (f32[8,128]{1,0:T(8,128)S(1)}, f32[8,128]{1,0:T(8,128)S(1)}, u32[]{:S(2)}, u32[]{:S(2)}) collective-permute-start(f32[8,128]{1,0:T(8,128)S(1)} %get-tuple-element.37), channel_id=1, source_target_pairs={{0,15},{1,2},{2,1},{3,4},{4,3},{5,6},{6,5},{7,8},{8,7},{9,10},{10,... | collective-permute-start | bytes 12296 | tf_op jit(solution)/shard_map/ppermute | solution.py:139
  94.2 1.9 %collective-permute-start.13 = (f32[36,128]{1,0:T(8,128)S(1)}, f32[36,128]{1,0:T(8,128)S(1)}, u32[]{:S(2)}, u32[]{:S(2)}) collective-permute-start(f32[36,128]{1,0:T(8,128)S(1)} %add.133), channel_id=1, source_target_pairs={{0,2},{1,3},{2,0},{3,1},{4,6},{5,7},{6,4},{7,5},{8,10},{9,11},{10,... | collective-permute-start | bytes 55304 | tf_op jit(solution)/shard_map/ppermute | solution.py:152
  96.1 3.7 %collective-permute-done.13 = f32[36,128]{1,0:T(8,128)S(1)} collective-permute-done((f32[36,128]{1,0:T(8,128)S(1)}, f32[36,128]{1,0:T(8,128)S(1)}, u32[]{:S(2)}, u32[]{:S(2)}) %collective-permute-start.13) | collective-permute-done | bytes 18464 | tf_op jit(solution)/shard_map/ppermute | solution.py:152
  99.8 1.9 %collective-permute-start.14 = (f32[36,128]{1,0:T(8,128)S(1)}, f32[36,128]{1,0:T(8,128)S(1)}, u32[]{:S(2)}, u32[]{:S(2)}) collective-permute-start(f32[36,128]{1,0:T(8,128)S(1)} %add.134), channel_id=1, source_target_pairs={{0,4},{1,5},{2,6},{3,7},{4,0},{5,1},{6,2},{7,3},{8,12},{9,13},{10,... | collective-permute-start | bytes 55304 | tf_op jit(solution)/shard_map/ppermute | solution.py:152
  101.8 4.6 %collective-permute-done.14 = f32[36,128]{1,0:T(8,128)S(1)} collective-permute-done((f32[36,128]{1,0:T(8,128)S(1)}, f32[36,128]{1,0:T(8,128)S(1)}, u32[]{:S(2)}, u32[]{:S(2)}) %collective-permute-start.14) | collective-permute-done | bytes 18464 | tf_op jit(solution)/shard_map/ppermute | solution.py:152
  106.4 1.9 %collective-permute-start.15 = (f32[36,128]{1,0:T(8,128)S(1)}, f32[36,128]{1,0:T(8,128)S(1)}, u32[]{:S(2)}, u32[]{:S(2)}) collective-permute-start(f32[36,128]{1,0:T(8,128)S(1)} %add.135), channel_id=1, source_target_pairs={{0,12},{1,13},{2,14},{3,15},{4,8},{5,9},{6,10},{7,11},{8,4},{9,5},... | collective-permute-start | bytes 55304 | tf_op jit(solution)/shard_map/ppermute | solution.py:152
  109.0 5.1 %collective-permute-done.15 = f32[36,128]{1,0:T(8,128)S(1)} collective-permute-done((f32[36,128]{1,0:T(8,128)S(1)}, f32[36,128]{1,0:T(8,128)S(1)}, u32[]{:S(2)}, u32[]{:S(2)}) %collective-permute-start.15) | collective-permute-done | bytes 18464 | tf_op jit(solution)/shard_map/ppermute | solution.py:152
  (107 shorter events, 17.3 us)
Async XLA Ops:
  0.6 39.2 %copy-start = (bf16[64,64]{1,0:T(8,128)(2,1)S(1)}, bf16[64,64]{1,0:T(8,128)(2,1)}, u32[]{:S(2)}) copy-start(bf16[64,64]{1,0:T(8,128)(2,1)} %param.14) | copy-start | bytes 24580
  0.6 35.7 %copy-start.4 = (s32[1,1,128]{2,1,0:T(1,128)S(1)}, s32[1,1,128]{2,1,0:T(1,128)}, u32[]{:S(2)}) copy-start(s32[1,1,128]{2,1,0:T(1,128)} %param.10) | copy-start | bytes 1540
  1.5 37.2 %collective-permute-start = (f32[2,8,128]{2,1,0:T(8,128)S(1)}, f32[2,8,128]{2,1,0:T(8,128)S(1)}, u32[]{:S(2)}, u32[]{:S(2)}) collective-permute-start(f32[2,8,128]{2,1,0:T(8,128)S(1)} %get-tuple-element.18), channel_id=1, source_target_pairs={{0,1},{1,2},{2,3},{3,4},{4,5},{5,6},{6,7},{7,8},{8,9},{9,10},{10,1... | collective-permute-start | bytes 24584 | tf_op jit(solution)/shard_map/ppermute | solution.py:11
  9.7 29.1 %collective-permute-start.1 = (f32[2,8,128]{2,1,0:T(8,128)S(1)}, f32[2,8,128]{2,1,0:T(8,128)S(1)}, u32[]{:S(2)}, u32[]{:S(2)}) collective-permute-start(f32[2,8,128]{2,1,0:T(8,128)S(1)} %get-tuple-element.19), channel_id=1, source_target_pairs={{0,15},{1,0},{2,1},{3,2},{4,3},{5,4},{6,5},{7,6},{8,7},{9,8},{10,9... | collective-permute-start | bytes 24584 | tf_op jit(solution)/shard_map/ppermute | solution.py:11
  26.5 12.2 %collective-permute-start.2 = (f32[2,8,128]{2,0,1:T(2,128)S(1)}, f32[2,8,128]{2,0,1:T(2,128)S(1)}, u32[]{:S(2)}, u32[]{:S(2)}) collective-permute-start(f32[2,8,128]{2,0,1:T(2,128)S(1)} %bitcast.158), channel_id=1, source_target_pairs={{0,1008},{16,0},{32,16},{48,32},{64,48},{80,64},{96,80},{112,96},{... | collective-permute-start | bytes 24584 | tf_op jit(solution)/shard_map/ppermute | solution.py:11
  29.0 9.8 %collective-permute-start.3 = (f32[2,8,128]{2,0,1:T(2,128)S(1)}, f32[2,8,128]{2,0,1:T(2,128)S(1)}, u32[]{:S(2)}, u32[]{:S(2)}) collective-permute-start(f32[2,8,128]{2,0,1:T(2,128)S(1)} %bitcast.157), channel_id=1, source_target_pairs={{0,16},{16,32},{32,48},{48,64},{64,80},{80,96},{96,112},{112,128},... | collective-permute-start | bytes 24584 | tf_op jit(solution)/shard_map/ppermute | solution.py:11
  37.1 1.3 %copy-start.5 = (bf16[1,64]{1,0:T(2,128)(2,1)S(1)}, bf16[1,64]{1,0:T(2,128)(2,1)}, u32[]{:S(2)}) copy-start(bf16[1,64]{1,0:T(2,128)(2,1)} %param.15) | copy-start | bytes 388
  37.1 1.3 %copy-start.1 = (f32[8,8,128]{2,1,0:T(8,128)S(1)}, f32[8,8,128]{2,1,0:T(8,128)}, u32[]{:S(2)}) copy-start(f32[8,8,128]{2,1,0:T(8,128)} %param.9) | copy-start | bytes 98308
  37.1 1.5 %copy-start.2 = (f32[8,8,128]{2,1,0:T(8,128)S(1)}, f32[8,8,128]{2,1,0:T(8,128)}, u32[]{:S(2)}) copy-start(f32[8,8,128]{2,1,0:T(8,128)} %param.8) | copy-start | bytes 98308
  37.8 1.5 %copy-start.3 = (bf16[64,7]{0,1:T(8,128)(2,1)S(1)}, bf16[64,7]{0,1:T(8,128)(2,1)}, u32[]{:S(2)}) copy-start(bf16[64,7]{0,1:T(8,128)(2,1)} %param.13) | copy-start | bytes 2692
  42.9 5.7 %collective-permute-start.4 = (f32[36,128]{1,0:T(8,128)S(1)}, f32[36,128]{1,0:T(8,128)S(1)}, u32[]{:S(2)}, u32[]{:S(2)}) collective-permute-start(f32[36,128]{1,0:T(8,128)S(1)} %constant_dynamic-update-slice_fusion), channel_id=1, source_target_pairs={{0,32},{1,33},{2,34},{3,35},{4,36},{5,37},{6,38},{7,39},{8,40},{9,... | collective-permute-start | bytes 55304 | tf_op jit(solution)/shard_map/ppermute | solution.py:152
  48.6 4.4 %collective-permute-start.5 = (f32[44,128]{1,0:T(8,128)S(1)}, f32[44,128]{1,0:T(8,128)S(1)}, u32[]{:S(2)}, u32[]{:S(2)}) collective-permute-start(f32[44,128]{1,0:T(8,128)S(1)} %pad_maximum_fusion.18), channel_id=1, source_target_pairs={{0,16},{1,17},{2,18},{3,19},{4,20},{5,21},{6,22},{7,23},{8,24},{9,... | collective-permute-start | bytes 67592 | tf_op jit(solution)/shard_map/ppermute | solution.py:157
  53.0 9.6 %collective-permute-start.7 = (f32[44,128]{1,0:T(8,128)S(1)}, f32[44,128]{1,0:T(8,128)S(1)}, u32[]{:S(2)}, u32[]{:S(2)}) collective-permute-start(f32[44,128]{1,0:T(8,128)S(1)} %pad_maximum_fusion.19), channel_id=1, source_target_pairs={{0,1},{1,0},{2,3},{3,2},{4,5},{5,4},{6,7},{7,6},{8,9},{9,8},{10,11... | collective-permute-start | bytes 67592 | tf_op jit(solution)/shard_map/ppermute | solution.py:157
  62.6 6.6 %collective-permute-start.9 = (f32[36,128]{1,0:T(8,128)S(1)}, f32[36,128]{1,0:T(8,128)S(1)}, u32[]{:S(2)}, u32[]{:S(2)}) collective-permute-start(f32[36,128]{1,0:T(8,128)S(1)} %slice_add_fusion), channel_id=1, source_target_pairs={{0,64},{1,65},{2,66},{3,67},{4,68},{5,69},{6,70},{7,71},{8,72},{9,... | collective-permute-start | bytes 55304 | tf_op jit(solution)/shard_map/ppermute | solution.py:152
  69.2 7.8 %collective-permute-start.10 = (f32[36,128]{1,0:T(8,128)S(1)}, f32[36,128]{1,0:T(8,128)S(1)}, u32[]{:S(2)}, u32[]{:S(2)}) collective-permute-start(f32[36,128]{1,0:T(8,128)S(1)} %add.130), channel_id=1, source_target_pairs={{0,192},{1,193},{2,194},{3,195},{4,196},{5,197},{6,198},{7,199},{8... | collective-permute-start | bytes 55304 | tf_op jit(solution)/shard_map/ppermute | solution.py:152
  77.0 5.7 %collective-permute-start.11 = (f32[36,128]{1,0:T(8,128)S(1)}, f32[36,128]{1,0:T(8,128)S(1)}, u32[]{:S(2)}, u32[]{:S(2)}) collective-permute-start(f32[36,128]{1,0:T(8,128)S(1)} %add.131), channel_id=1, source_target_pairs={{0,256},{1,257},{2,258},{3,259},{4,260},{5,261},{6,262},{7,263},{8... | collective-permute-start | bytes 55304 | tf_op jit(solution)/shard_map/ppermute | solution.py:152
  79.7 16.4 %collective-permute-start.6 = (f32[8,128]{1,0:T(8,128)S(1)}, f32[8,128]{1,0:T(8,128)S(1)}, u32[]{:S(2)}, u32[]{:S(2)}) collective-permute-start(f32[8,128]{1,0:T(8,128)S(1)} %get-tuple-element.15), channel_id=1, source_target_pairs={{0,1008},{16,32},{32,16},{48,64},{64,48},{80,96},{96,80},{112,128}... | collective-permute-start | bytes 12296 | tf_op jit(solution)/shard_map/ppermute | solution.py:136
  82.7 11.5 %collective-permute-start.12 = (f32[36,128]{1,0:T(8,128)S(1)}, f32[36,128]{1,0:T(8,128)S(1)}, u32[]{:S(2)}, u32[]{:S(2)}) collective-permute-start(f32[36,128]{1,0:T(8,128)S(1)} %add.132), channel_id=1, source_target_pairs={{0,512},{1,513},{2,514},{3,515},{4,516},{5,517},{6,518},{7,519},{8... | collective-permute-start | bytes 55304 | tf_op jit(solution)/shard_map/ppermute | solution.py:152
  86.6 15.2 %collective-permute-start.8 = (f32[8,128]{1,0:T(8,128)S(1)}, f32[8,128]{1,0:T(8,128)S(1)}, u32[]{:S(2)}, u32[]{:S(2)}) collective-permute-start(f32[8,128]{1,0:T(8,128)S(1)} %get-tuple-element.37), channel_id=1, source_target_pairs={{0,15},{1,2},{2,1},{3,4},{4,3},{5,6},{6,5},{7,8},{8,7},{9,10},{10,... | collective-permute-start | bytes 12296 | tf_op jit(solution)/shard_map/ppermute | solution.py:139
  94.2 5.7 %collective-permute-start.13 = (f32[36,128]{1,0:T(8,128)S(1)}, f32[36,128]{1,0:T(8,128)S(1)}, u32[]{:S(2)}, u32[]{:S(2)}) collective-permute-start(f32[36,128]{1,0:T(8,128)S(1)} %add.133), channel_id=1, source_target_pairs={{0,2},{1,3},{2,0},{3,1},{4,6},{5,7},{6,4},{7,5},{8,10},{9,11},{10,... | collective-permute-start | bytes 55304 | tf_op jit(solution)/shard_map/ppermute | solution.py:152
  99.8 6.6 %collective-permute-start.14 = (f32[36,128]{1,0:T(8,128)S(1)}, f32[36,128]{1,0:T(8,128)S(1)}, u32[]{:S(2)}, u32[]{:S(2)}) collective-permute-start(f32[36,128]{1,0:T(8,128)S(1)} %add.134), channel_id=1, source_target_pairs={{0,4},{1,5},{2,6},{3,7},{4,0},{5,1},{6,2},{7,3},{8,12},{9,13},{10,... | collective-permute-start | bytes 55304 | tf_op jit(solution)/shard_map/ppermute | solution.py:152
  106.4 7.8 %collective-permute-start.15 = (f32[36,128]{1,0:T(8,128)S(1)}, f32[36,128]{1,0:T(8,128)S(1)}, u32[]{:S(2)}, u32[]{:S(2)}) collective-permute-start(f32[36,128]{1,0:T(8,128)S(1)} %add.135), channel_id=1, source_target_pairs={{0,12},{1,13},{2,14},{3,15},{4,8},{5,9},{6,10},{7,11},{8,4},{9,5},... | collective-permute-start | bytes 55304 | tf_op jit(solution)/shard_map/ppermute | solution.py:152

commit v8 on v6

--- a/solution.py
+++ b/solution.py
@@ -69,11 +69,21 @@
     return jnp.concatenate([top, mid, bot], axis=-3)
 
 
-def padded_laplace(padded):
+def padded_laplace(padded, zup, zdown):
     center = padded[1:-1, 1:-1]
     total = padded[2:, 1:-1] + padded[:-2, 1:-1] + padded[1:-1, 2:] + padded[1:-1, :-2]
-    total = total + jnp.roll(center, -1, 2) + jnp.roll(center, 1, 2)
+    total = total + zup + zdown
     return total - 6.0 * center
+
+
+def z_neighbours(field):
+    sizez = field.shape[-1]
+    rows = lax.broadcasted_iota(jnp.int32, (sizez, 2 * sizez), 0)
+    cols = lax.broadcasted_iota(jnp.int32, (sizez, 2 * sizez), 1)
+    source = jnp.where(cols < sizez, (cols + 1) % sizez, (cols - sizez - 1) % sizez)
+    shift = (rows == source).astype(field.dtype)
+    both = jnp.dot(field.reshape(-1, sizez), shift, precision=lax.Precision.HIGHEST, preferred_element_type=jnp.float32)
+    return both[:, :sizez].reshape(field.shape), both[:, sizez:].reshape(field.shape)
 
 
 def body(velocity, cotangent, block_ids, fluid_count, fluid_cells, w_in, w_mid, w_out):
@@ -98,6 +108,8 @@
     weight = from_blocks(block_w, sizex, sizey, sizez).reshape(cells)
 
     center = padded[1:-1, 1:-1]
+    vup, vdown = z_neighbours(velocity)
+    cup, cdown = z_neighbours(cotangent)
     chosen = jnp.stack(
         [
             center,
@@ -105,8 +117,8 @@
             padded[:-2, 1:-1],
             padded[1:-1, 2:],
             padded[1:-1, :-2],
-            jnp.roll(center, -1, 2),
-            jnp.roll(center, 1, 2),
+            vup,
+            vdown,
         ]
     ).astype(jnp.bfloat16).reshape(7, cells)
     h1 = jnp.tanh(jnp.dot(w_in, chosen, preferred_element_type=jnp.float32)).astype(jnp.bfloat16)
@@ -124,7 +136,7 @@
     gmid = lax.dot_general(da2, h1, dims, preferred_element_type=jnp.float32)
     gout = lax.dot_general(dcl[None, :], h2, dims, preferred_element_type=jnp.float32)
 
-    new_field = velocity + viscosity * padded_laplace(padded) + corr.reshape(sizex, sizey, sizez)
+    new_field = velocity + viscosity * padded_laplace(padded, vup, vdown) + corr.reshape(sizex, sizey, sizez)
 
     nx = lax.axis_size("gx")
     ny = lax.axis_size("gy")
@@ -167,7 +179,7 @@
     side3 = jnp.concatenate([from_ylo[:, None], dfeat[3, :, :-1]], axis=1)
     side4 = jnp.concatenate([dfeat[4, :, 1:], from_yhi[:, None]], axis=1)
     local = dfeat[0] + jnp.roll(dfeat[5], 1, 2) + jnp.roll(dfeat[6], -1, 2)
-    grad_field = cotangent + viscosity * padded_laplace(cot_pad) + local + (side1 + side2 + side3 + side4)
+    grad_field = cotangent + viscosity * padded_laplace(cot_pad, cup, cdown) + local + (side1 + side2 + side3 + side4)
 
     scale = 1.0 / jnp.sqrt(jnp.float32(nx * ny * slots * 64))
     total = grads * scale

time: 116 us -> 115 us (level)
  local copies, waits for them, and re-layouts: 9.46 us -> 5.85 us
  matrix products: 4.33 us -> 6.06 us
    slice x4 -> x0, local copies, waits for them, and re-layouts: 3.64 us -> none  [padded_laplace(): total = total + jnp.roll(center, -1, 2) + jnp.roll(center, 1, 2)]
  transfers between devices with their start and end apart: 16 -> 16, of which waited for: 9 -> 9; matrix products, arithmetic and copies ran while one was open for 8% -> 5% of each run, Pallas kernels for 0% -> 0%
where the time goes in v8:
time: 115 us; the launch traced here: 114 us
  starting transfers between devices  66.9 us (58%)
  waiting for transfers between devices  30.4 us (26%)
  matrix products  6.06 us (5%)
  local copies, waits for them, and re-layouts  5.85 us (5%)
  other arithmetic  2.53 us (2%)
  between operations  1.97 us (2%)
    ppermute x4, starting transfers between devices, shift_from(): lax.ppermute(face, axis, [(i, (i + step) % count) for i in range(count)])  29.4 us
    ppermute x8, starting transfers between devices, body(): grads = grads + lax.ppermute(grads, ('gx', 'gy'), pairs)  22.6 us
    ppermute x8, waiting for transfers between devices, body(): grads = grads + lax.ppermute(grads, ('gx', 'gy'), pairs)  21.9 us
    ppermute x2, waiting for transfers between devices, body(): got = lax.ppermute(message, ('gx', 'gy'), pairs)  8.51 us
    ppermute x1, starting transfers between devices, body(): lax.ppermute(jnp.where(yodd, up_y, down_y), 'gy', [(i, (i + 1) % ny if i...  7.54 us
    ppermute x2, starting transfers between devices, body(): got = lax.ppermute(message, ('gx', 'gy'), pairs)  5.49 us
  transfers between devices with their start and end apart: 16, of which 9 were waited for; matrix products, arithmetic and copies ran while one was open for 5% of the time, Pallas kernels for 0%

profile of v8, /device:TPU:14, one launch (start us, length us, event | category | flops | bytes accessed | tf_op | source)
XLA Modules:
  0.0 113.7 jit_solution(9881646433157480907)
XLA Ops:
  1.5 8.2 %collective-permute-start = (f32[2,8,128]{2,1,0:T(8,128)S(1)}, f32[2,8,128]{2,1,0:T(8,128)S(1)}, u32[]{:S(2)}, u32[]{:S(2)}) collective-permute-start(f32[2,8,128]{2,1,0:T(8,128)S(1)} %get-tuple-element.20), channel_id=1, source_target_pairs={{0,1},{1,2},{2,3},{3,4},{4,5},{5,6},{6,7},{7,8},{8,9},{9,10},{10,1... | collective-permute-start | bytes 24584 | tf_op jit(solution)/shard_map/ppermute | solution.py:11
  9.7 16.8 %collective-permute-start.1 = (f32[2,8,128]{2,1,0:T(8,128)S(1)}, f32[2,8,128]{2,1,0:T(8,128)S(1)}, u32[]{:S(2)}, u32[]{:S(2)}) collective-permute-start(f32[2,8,128]{2,1,0:T(8,128)S(1)} %get-tuple-element.21), channel_id=1, source_target_pairs={{0,15},{1,0},{2,1},{3,2},{4,3},{5,4},{6,5},{7,6},{8,7},{9,8},{10,9... | collective-permute-start | bytes 24584 | tf_op jit(solution)/shard_map/ppermute | solution.py:11
  26.4 2.5 %collective-permute-start.2 = (f32[2,8,128]{2,0,1:T(2,128)S(1)}, f32[2,8,128]{2,0,1:T(2,128)S(1)}, u32[]{:S(2)}, u32[]{:S(2)}) collective-permute-start(f32[2,8,128]{2,0,1:T(2,128)S(1)} %bitcast.216), channel_id=1, source_target_pairs={{0,1008},{16,0},{32,16},{48,32},{64,48},{80,64},{96,80},{112,96},{... | collective-permute-start | bytes 24584 | tf_op jit(solution)/shard_map/ppermute | solution.py:11
  29.0 1.9 %collective-permute-start.3 = (f32[2,8,128]{2,0,1:T(2,128)S(1)}, f32[2,8,128]{2,0,1:T(2,128)S(1)}, u32[]{:S(2)}, u32[]{:S(2)}) collective-permute-start(f32[2,8,128]{2,0,1:T(2,128)S(1)} %bitcast.215), channel_id=1, source_target_pairs={{0,16},{16,32},{32,48},{48,64},{64,80},{80,96},{96,112},{112,128},... | collective-permute-start | bytes 24584 | tf_op jit(solution)/shard_map/ppermute | solution.py:11
  42.4 3.3 %collective-permute-start.4 = (f32[36,128]{1,0:T(8,128)S(1)}, f32[36,128]{1,0:T(8,128)S(1)}, u32[]{:S(2)}, u32[]{:S(2)}) collective-permute-start(f32[36,128]{1,0:T(8,128)S(1)} %constant_dynamic-update-slice_fusion), channel_id=1, source_target_pairs={{0,32},{1,33},{2,34},{3,35},{4,36},{5,37},{6,38},{7,39},{8,40},{9,... | collective-permute-start | bytes 55304 | tf_op jit(solution)/shard_map/ppermute | solution.py:164
  45.8 2.2 %collective-permute-done.4 = f32[36,128]{1,0:T(8,128)S(1)} collective-permute-done((f32[36,128]{1,0:T(8,128)S(1)}, f32[36,128]{1,0:T(8,128)S(1)}, u32[]{:S(2)}, u32[]{:S(2)}) %collective-permute-start.4) | collective-permute-done | bytes 18464 | tf_op jit(solution)/shard_map/ppermute | solution.py:164
  48.1 3.6 %collective-permute-start.5 = (f32[44,128]{1,0:T(8,128)S(1)}, f32[44,128]{1,0:T(8,128)S(1)}, u32[]{:S(2)}, u32[]{:S(2)}) collective-permute-start(f32[44,128]{1,0:T(8,128)S(1)} %pad_maximum_fusion.16), channel_id=1, source_target_pairs={{0,16},{1,17},{2,18},{3,19},{4,20},{5,21},{6,22},{7,23},{8,24},{9,... | collective-permute-start | bytes 67592 | tf_op jit(solution)/shard_map/ppermute | solution.py:169
  52.5 1.9 %collective-permute-start.7 = (f32[44,128]{1,0:T(8,128)S(1)}, f32[44,128]{1,0:T(8,128)S(1)}, u32[]{:S(2)}, u32[]{:S(2)}) collective-permute-start(f32[44,128]{1,0:T(8,128)S(1)} %pad_maximum_fusion.17), channel_id=1, source_target_pairs={{0,1},{1,0},{2,3},{3,2},{4,5},{5,4},{6,7},{7,6},{8,9},{9,8},{10,11... | collective-permute-start | bytes 67592 | tf_op jit(solution)/shard_map/ppermute | solution.py:169
  54.4 7.7 %collective-permute-done.7 = f32[44,128]{1,0:T(8,128)S(1)} collective-permute-done((f32[44,128]{1,0:T(8,128)S(1)}, f32[44,128]{1,0:T(8,128)S(1)}, u32[]{:S(2)}, u32[]{:S(2)}) %collective-permute-start.7) | collective-permute-done | bytes 22560 | tf_op jit(solution)/shard_map/ppermute | solution.py:169
  62.1 2.9 %collective-permute-start.9 = (f32[36,128]{1,0:T(8,128)S(1)}, f32[36,128]{1,0:T(8,128)S(1)}, u32[]{:S(2)}, u32[]{:S(2)}) collective-permute-start(f32[36,128]{1,0:T(8,128)S(1)} %slice_add_fusion), channel_id=1, source_target_pairs={{0,64},{1,65},{2,66},{3,67},{4,68},{5,69},{6,70},{7,71},{8,72},{9,... | collective-permute-start | bytes 55304 | tf_op jit(solution)/shard_map/ppermute | solution.py:164
  65.2 3.5 %collective-permute-done.9 = f32[36,128]{1,0:T(8,128)S(1)} collective-permute-done((f32[36,128]{1,0:T(8,128)S(1)}, f32[36,128]{1,0:T(8,128)S(1)}, u32[]{:S(2)}, u32[]{:S(2)}) %collective-permute-start.9) | collective-permute-done | bytes 18464 | tf_op jit(solution)/shard_map/ppermute | solution.py:164
  68.7 4.2 %collective-permute-start.10 = (f32[36,128]{1,0:T(8,128)S(1)}, f32[36,128]{1,0:T(8,128)S(1)}, u32[]{:S(2)}, u32[]{:S(2)}) collective-permute-start(f32[36,128]{1,0:T(8,128)S(1)} %add.165), channel_id=1, source_target_pairs={{0,224},{1,225},{2,226},{3,227},{4,228},{5,229},{6,230},{7,231},{8... | collective-permute-start | bytes 55304 | tf_op jit(solution)/shard_map/ppermute | solution.py:164
  73.0 2.6 %collective-permute-done.10 = f32[36,128]{1,0:T(8,128)S(1)} collective-permute-done((f32[36,128]{1,0:T(8,128)S(1)}, f32[36,128]{1,0:T(8,128)S(1)}, u32[]{:S(2)}, u32[]{:S(2)}) %collective-permute-start.10) | collective-permute-done | bytes 18464 | tf_op jit(solution)/shard_map/ppermute | solution.py:164
  75.6 2.7 %collective-permute-start.11 = (f32[36,128]{1,0:T(8,128)S(1)}, f32[36,128]{1,0:T(8,128)S(1)}, u32[]{:S(2)}, u32[]{:S(2)}) collective-permute-start(f32[36,128]{1,0:T(8,128)S(1)} %add.166), channel_id=1, source_target_pairs={{0,256},{1,257},{2,258},{3,259},{4,260},{5,261},{6,262},{7,263},{8... | collective-permute-start | bytes 55304 | tf_op jit(solution)/shard_map/ppermute | solution.py:164
  78.3 1.9 %collective-permute-start.6 = (f32[8,128]{1,0:T(8,128)S(1)}, f32[8,128]{1,0:T(8,128)S(1)}, u32[]{:S(2)}, u32[]{:S(2)}) collective-permute-start(f32[8,128]{1,0:T(8,128)S(1)} %get-tuple-element.15), channel_id=1, source_target_pairs={{0,1008},{16,32},{32,16},{48,64},{64,48},{80,96},{96,80},{112,128}... | collective-permute-start | bytes 12296 | tf_op jit(solution)/shard_map/ppermute | solution.py:148
  80.2 1.0 collective-permute-done.11
  81.2 3.7 %collective-permute-start.12 = (f32[36,128]{1,0:T(8,128)S(1)}, f32[36,128]{1,0:T(8,128)S(1)}, u32[]{:S(2)}, u32[]{:S(2)}) collective-permute-start(f32[36,128]{1,0:T(8,128)S(1)} %add.167), channel_id=1, source_target_pairs={{0,512},{1,513},{2,514},{3,515},{4,516},{5,517},{6,518},{7,519},{8... | collective-permute-start | bytes 55304 | tf_op jit(solution)/shard_map/ppermute | solution.py:164
  85.2 7.5 %collective-permute-start.8 = (f32[8,128]{1,0:T(8,128)S(1)}, f32[8,128]{1,0:T(8,128)S(1)}, u32[]{:S(2)}, u32[]{:S(2)}) collective-permute-start(f32[8,128]{1,0:T(8,128)S(1)} %get-tuple-element.33), channel_id=1, source_target_pairs={{0,15},{1,2},{2,1},{3,4},{4,3},{5,6},{6,5},{7,8},{8,7},{9,10},{10,... | collective-permute-start | bytes 12296 | tf_op jit(solution)/shard_map/ppermute | solution.py:151
  92.7 1.9 %collective-permute-start.13 = (f32[36,128]{1,0:T(8,128)S(1)}, f32[36,128]{1,0:T(8,128)S(1)}, u32[]{:S(2)}, u32[]{:S(2)}) collective-permute-start(f32[36,128]{1,0:T(8,128)S(1)} %add.168), channel_id=1, source_target_pairs={{0,2},{1,3},{2,0},{3,1},{4,6},{5,7},{6,4},{7,5},{8,10},{9,11},{10,... | collective-permute-start | bytes 55304 | tf_op jit(solution)/shard_map/ppermute | solution.py:164
  94.7 3.7 %collective-permute-done.13 = f32[36,128]{1,0:T(8,128)S(1)} collective-permute-done((f32[36,128]{1,0:T(8,128)S(1)}, f32[36,128]{1,0:T(8,128)S(1)}, u32[]{:S(2)}, u32[]{:S(2)}) %collective-permute-start.13) | collective-permute-done | bytes 18464 | tf_op jit(solution)/shard_map/ppermute | solution.py:164
  98.4 1.9 %collective-permute-start.14 = (f32[36,128]{1,0:T(8,128)S(1)}, f32[36,128]{1,0:T(8,128)S(1)}, u32[]{:S(2)}, u32[]{:S(2)}) collective-permute-start(f32[36,128]{1,0:T(8,128)S(1)} %add.169), channel_id=1, source_target_pairs={{0,4},{1,5},{2,6},{3,7},{4,0},{5,1},{6,2},{7,3},{8,12},{9,13},{10,... | collective-permute-start | bytes 55304 | tf_op jit(solution)/shard_map/ppermute | solution.py:164
  100.3 4.6 %collective-permute-done.14 = f32[36,128]{1,0:T(8,128)S(1)} collective-permute-done((f32[36,128]{1,0:T(8,128)S(1)}, f32[36,128]{1,0:T(8,128)S(1)}, u32[]{:S(2)}, u32[]{:S(2)}) %collective-permute-start.14) | collective-permute-done | bytes 18464 | tf_op jit(solution)/shard_map/ppermute | solution.py:164
  105.0 1.9 %collective-permute-start.15 = (f32[36,128]{1,0:T(8,128)S(1)}, f32[36,128]{1,0:T(8,128)S(1)}, u32[]{:S(2)}, u32[]{:S(2)}) collective-permute-start(f32[36,128]{1,0:T(8,128)S(1)} %add.170), channel_id=1, source_target_pairs={{0,14},{1,15},{2,12},{3,13},{4,10},{5,11},{6,8},{7,9},{8,6},{9,7},... | collective-permute-start | bytes 55304 | tf_op jit(solution)/shard_map/ppermute | solution.py:164
  107.6 4.2 %collective-permute-done.15 = f32[36,128]{1,0:T(8,128)S(1)} collective-permute-done((f32[36,128]{1,0:T(8,128)S(1)}, f32[36,128]{1,0:T(8,128)S(1)}, u32[]{:S(2)}, u32[]{:S(2)}) %collective-permute-start.15) | collective-permute-done | bytes 18464 | tf_op jit(solution)/shard_map/ppermute | solution.py:164
  (106 shorter events, 15.3 us)
Async XLA Ops:
  0.6 37.1 %copy-start = (bf16[64,64]{1,0:T(8,128)(2,1)S(1)}, bf16[64,64]{1,0:T(8,128)(2,1)}, u32[]{:S(2)}) copy-start(bf16[64,64]{1,0:T(8,128)(2,1)} %param.14) | copy-start | bytes 24580
  1.5 35.2 %collective-permute-start = (f32[2,8,128]{2,1,0:T(8,128)S(1)}, f32[2,8,128]{2,1,0:T(8,128)S(1)}, u32[]{:S(2)}, u32[]{:S(2)}) collective-permute-start(f32[2,8,128]{2,1,0:T(8,128)S(1)} %get-tuple-element.20), channel_id=1, source_target_pairs={{0,1},{1,2},{2,3},{3,4},{4,5},{5,6},{6,7},{7,8},{8,9},{9,10},{10,1... | collective-permute-start | bytes 24584 | tf_op jit(solution)/shard_map/ppermute | solution.py:11
  9.7 27.1 %collective-permute-start.1 = (f32[2,8,128]{2,1,0:T(8,128)S(1)}, f32[2,8,128]{2,1,0:T(8,128)S(1)}, u32[]{:S(2)}, u32[]{:S(2)}) collective-permute-start(f32[2,8,128]{2,1,0:T(8,128)S(1)} %get-tuple-element.21), channel_id=1, source_target_pairs={{0,15},{1,0},{2,1},{3,2},{4,3},{5,4},{6,5},{7,6},{8,7},{9,8},{10,9... | collective-permute-start | bytes 24584 | tf_op jit(solution)/shard_map/ppermute | solution.py:11
  26.4 10.2 %collective-permute-start.2 = (f32[2,8,128]{2,0,1:T(2,128)S(1)}, f32[2,8,128]{2,0,1:T(2,128)S(1)}, u32[]{:S(2)}, u32[]{:S(2)}) collective-permute-start(f32[2,8,128]{2,0,1:T(2,128)S(1)} %bitcast.216), channel_id=1, source_target_pairs={{0,1008},{16,0},{32,16},{48,32},{64,48},{80,64},{96,80},{112,96},{... | collective-permute-start | bytes 24584 | tf_op jit(solution)/shard_map/ppermute | solution.py:11
  29.0 7.7 %collective-permute-start.3 = (f32[2,8,128]{2,0,1:T(2,128)S(1)}, f32[2,8,128]{2,0,1:T(2,128)S(1)}, u32[]{:S(2)}, u32[]{:S(2)}) collective-permute-start(f32[2,8,128]{2,0,1:T(2,128)S(1)} %bitcast.215), channel_id=1, source_target_pairs={{0,16},{16,32},{32,48},{48,64},{64,80},{80,96},{96,112},{112,128},... | collective-permute-start | bytes 24584 | tf_op jit(solution)/shard_map/ppermute | solution.py:11
  34.6 1.1 %copy-start.1 = (f32[8,8,128]{2,1,0:T(8,128)S(1)}, f32[8,8,128]{2,1,0:T(8,128)}, u32[]{:S(2)}) copy-start(f32[8,8,128]{2,1,0:T(8,128)} %param.9) | copy-start | bytes 98308
  34.6 1.1 %copy-start.4 = (bf16[1,64]{1,0:T(2,128)(2,1)S(1)}, bf16[1,64]{1,0:T(2,128)(2,1)}, u32[]{:S(2)}) copy-start(bf16[1,64]{1,0:T(2,128)(2,1)} %param.15) | copy-start | bytes 388
  34.7 1.2 %copy-start.2 = (f32[8,8,128]{2,1,0:T(8,128)S(1)}, f32[8,8,128]{2,1,0:T(8,128)}, u32[]{:S(2)}) copy-start(f32[8,8,128]{2,1,0:T(8,128)} %param.8) | copy-start | bytes 98308
  35.8 1.4 %copy-start.3 = (bf16[64,7]{0,1:T(8,128)(2,1)S(1)}, bf16[64,7]{0,1:T(8,128)(2,1)}, u32[]{:S(2)}) copy-start(bf16[64,7]{0,1:T(8,128)(2,1)} %param.13) | copy-start | bytes 2692
  42.4 5.7 %collective-permute-start.4 = (f32[36,128]{1,0:T(8,128)S(1)}, f32[36,128]{1,0:T(8,128)S(1)}, u32[]{:S(2)}, u32[]{:S(2)}) collective-permute-start(f32[36,128]{1,0:T(8,128)S(1)} %constant_dynamic-update-slice_fusion), channel_id=1, source_target_pairs={{0,32},{1,33},{2,34},{3,35},{4,36},{5,37},{6,38},{7,39},{8,40},{9,... | collective-permute-start | bytes 55304 | tf_op jit(solution)/shard_map/ppermute | solution.py:164
  48.1 4.4 %collective-permute-start.5 = (f32[44,128]{1,0:T(8,128)S(1)}, f32[44,128]{1,0:T(8,128)S(1)}, u32[]{:S(2)}, u32[]{:S(2)}) collective-permute-start(f32[44,128]{1,0:T(8,128)S(1)} %pad_maximum_fusion.16), channel_id=1, source_target_pairs={{0,16},{1,17},{2,18},{3,19},{4,20},{5,21},{6,22},{7,23},{8,24},{9,... | collective-permute-start | bytes 67592 | tf_op jit(solution)/shard_map/ppermute | solution.py:169
  52.5 9.6 %collective-permute-start.7 = (f32[44,128]{1,0:T(8,128)S(1)}, f32[44,128]{1,0:T(8,128)S(1)}, u32[]{:S(2)}, u32[]{:S(2)}) collective-permute-start(f32[44,128]{1,0:T(8,128)S(1)} %pad_maximum_fusion.17), channel_id=1, source_target_pairs={{0,1},{1,0},{2,3},{3,2},{4,5},{5,4},{6,7},{7,6},{8,9},{9,8},{10,11... | collective-permute-start | bytes 67592 | tf_op jit(solution)/shard_map/ppermute | solution.py:169
  62.1 6.6 %collective-permute-start.9 = (f32[36,128]{1,0:T(8,128)S(1)}, f32[36,128]{1,0:T(8,128)S(1)}, u32[]{:S(2)}, u32[]{:S(2)}) collective-permute-start(f32[36,128]{1,0:T(8,128)S(1)} %slice_add_fusion), channel_id=1, source_target_pairs={{0,64},{1,65},{2,66},{3,67},{4,68},{5,69},{6,70},{7,71},{8,72},{9,... | collective-permute-start | bytes 55304 | tf_op jit(solution)/shard_map/ppermute | solution.py:164
  68.7 6.9 %collective-permute-start.10 = (f32[36,128]{1,0:T(8,128)S(1)}, f32[36,128]{1,0:T(8,128)S(1)}, u32[]{:S(2)}, u32[]{:S(2)}) collective-permute-start(f32[36,128]{1,0:T(8,128)S(1)} %add.165), channel_id=1, source_target_pairs={{0,224},{1,225},{2,226},{3,227},{4,228},{5,229},{6,230},{7,231},{8... | collective-permute-start | bytes 55304 | tf_op jit(solution)/shard_map/ppermute | solution.py:164
  75.6 5.7 %collective-permute-start.11 = (f32[36,128]{1,0:T(8,128)S(1)}, f32[36,128]{1,0:T(8,128)S(1)}, u32[]{:S(2)}, u32[]{:S(2)}) collective-permute-start(f32[36,128]{1,0:T(8,128)S(1)} %add.166), channel_id=1, source_target_pairs={{0,256},{1,257},{2,258},{3,259},{4,260},{5,261},{6,262},{7,263},{8... | collective-permute-start | bytes 55304 | tf_op jit(solution)/shard_map/ppermute | solution.py:164
  78.3 16.4 %collective-permute-start.6 = (f32[8,128]{1,0:T(8,128)S(1)}, f32[8,128]{1,0:T(8,128)S(1)}, u32[]{:S(2)}, u32[]{:S(2)}) collective-permute-start(f32[8,128]{1,0:T(8,128)S(1)} %get-tuple-element.15), channel_id=1, source_target_pairs={{0,1008},{16,32},{32,16},{48,64},{64,48},{80,96},{96,80},{112,128}... | collective-permute-start | bytes 12296 | tf_op jit(solution)/shard_map/ppermute | solution.py:148
  81.2 11.5 %collective-permute-start.12 = (f32[36,128]{1,0:T(8,128)S(1)}, f32[36,128]{1,0:T(8,128)S(1)}, u32[]{:S(2)}, u32[]{:S(2)}) collective-permute-start(f32[36,128]{1,0:T(8,128)S(1)} %add.167), channel_id=1, source_target_pairs={{0,512},{1,513},{2,514},{3,515},{4,516},{5,517},{6,518},{7,519},{8... | collective-permute-start | bytes 55304 | tf_op jit(solution)/shard_map/ppermute | solution.py:164
  85.2 15.2 %collective-permute-start.8 = (f32[8,128]{1,0:T(8,128)S(1)}, f32[8,128]{1,0:T(8,128)S(1)}, u32[]{:S(2)}, u32[]{:S(2)}) collective-permute-start(f32[8,128]{1,0:T(8,128)S(1)} %get-tuple-element.33), channel_id=1, source_target_pairs={{0,15},{1,2},{2,1},{3,4},{4,3},{5,6},{6,5},{7,8},{8,7},{9,10},{10,... | collective-permute-start | bytes 12296 | tf_op jit(solution)/shard_map/ppermute | solution.py:151
  92.7 5.7 %collective-permute-start.13 = (f32[36,128]{1,0:T(8,128)S(1)}, f32[36,128]{1,0:T(8,128)S(1)}, u32[]{:S(2)}, u32[]{:S(2)}) collective-permute-start(f32[36,128]{1,0:T(8,128)S(1)} %add.168), channel_id=1, source_target_pairs={{0,2},{1,3},{2,0},{3,1},{4,6},{5,7},{6,4},{7,5},{8,10},{9,11},{10,... | collective-permute-start | bytes 55304 | tf_op jit(solution)/shard_map/ppermute | solution.py:164
  98.4 6.6 %collective-permute-start.14 = (f32[36,128]{1,0:T(8,128)S(1)}, f32[36,128]{1,0:T(8,128)S(1)}, u32[]{:S(2)}, u32[]{:S(2)}) collective-permute-start(f32[36,128]{1,0:T(8,128)S(1)} %add.169), channel_id=1, source_target_pairs={{0,4},{1,5},{2,6},{3,7},{4,0},{5,1},{6,2},{7,3},{8,12},{9,13},{10,... | collective-permute-start | bytes 55304 | tf_op jit(solution)/shard_map/ppermute | solution.py:164
  105.0 6.9 %collective-permute-start.15 = (f32[36,128]{1,0:T(8,128)S(1)}, f32[36,128]{1,0:T(8,128)S(1)}, u32[]{:S(2)}, u32[]{:S(2)}) collective-permute-start(f32[36,128]{1,0:T(8,128)S(1)} %add.170), channel_id=1, source_target_pairs={{0,14},{1,15},{2,12},{3,13},{4,10},{5,11},{6,8},{7,9},{8,6},{9,7},... | collective-permute-start | bytes 55304 | tf_op jit(solution)/shard_map/ppermute | solution.py:164

commit v9 on v8

--- a/solution.py
+++ b/solution.py
@@ -105,7 +105,8 @@
     slot_w = fluid_cells.reshape(slots, 64).astype(jnp.bfloat16) * live[:, None]
     onehot = (ids[:, None] == jnp.arange(nblocks)[None, :]).astype(jnp.bfloat16)
     block_w = lax.dot_general(onehot, slot_w, (((0,), (0,)), ((), ())), preferred_element_type=jnp.float32)
-    weight = from_blocks(block_w, sizex, sizey, sizez).reshape(cells)
+    grid = (sizex * sizey, sizez)
+    weight = from_blocks(block_w, sizex, sizey, sizez).reshape(grid)
 
     center = padded[1:-1, 1:-1]
     vup, vdown = z_neighbours(velocity)
@@ -120,21 +121,24 @@
             vup,
             vdown,
         ]
-    ).astype(jnp.bfloat16).reshape(7, cells)
-    h1 = jnp.tanh(jnp.dot(w_in, chosen, preferred_element_type=jnp.float32)).astype(jnp.bfloat16)
-    h2 = jnp.tanh(jnp.dot(w_mid, h1, preferred_element_type=jnp.float32)).astype(jnp.bfloat16)
-    corr = jnp.dot(w_out, h2, preferred_element_type=jnp.float32)[0] * weight
-    dcl = (cotangent.reshape(cells) * weight).astype(jnp.bfloat16)
+    ).astype(jnp.bfloat16).reshape((7,) + grid)
+    def mix(w, a):
+        return jnp.einsum("oc,crz->orz", w, a, preferred_element_type=jnp.float32)
+
+    h1 = jnp.tanh(mix(w_in, chosen)).astype(jnp.bfloat16)
+    h2 = jnp.tanh(mix(w_mid, h1)).astype(jnp.bfloat16)
+    corr = mix(w_out, h2)[0] * weight
+    dcl = (cotangent.reshape(grid) * weight).astype(jnp.bfloat16)
     h2f = h2.astype(jnp.float32)
     h1f = h1.astype(jnp.float32)
-    dh2 = jnp.dot(w_out.T, dcl[None, :], preferred_element_type=jnp.float32)
+    dh2 = mix(w_out.T, dcl[None])
     da2 = (dh2 * (1.0 - h2f * h2f)).astype(jnp.bfloat16)
-    dh1 = jnp.dot(w_mid.T, da2, preferred_element_type=jnp.float32)
+    dh1 = mix(w_mid.T, da2)
     da1 = (dh1 * (1.0 - h1f * h1f)).astype(jnp.bfloat16)
-    dfeat = jnp.dot(w_in.T, da1, preferred_element_type=jnp.float32).reshape(7, sizex, sizey, sizez)
-    dims = (((1,), (1,)), ((), ()))
+    dfeat = mix(w_in.T, da1).reshape(7, sizex, sizey, sizez)
+    dims = (((1, 2), (1, 2)), ((), ()))
     gmid = lax.dot_general(da2, h1, dims, preferred_element_type=jnp.float32)
-    gout = lax.dot_general(dcl[None, :], h2, dims, preferred_element_type=jnp.float32)
+    gout = lax.dot_general(dcl[None], h2, dims, preferred_element_type=jnp.float32)
 
     new_field = velocity + viscosity * padded_laplace(padded, vup, vdown) + corr.reshape(sizex, sizey, sizez)
 

time: 115 us -> 116 us (level)
  waiting for transfers between devices: 30.4 us -> 35.1 us
  starting transfers between devices: 66.9 us -> 64.5 us
  matrix products: 6.06 us -> 4.89 us
    ppermute x8, waiting for transfers between devices: 21.9 us -> 26.5 us  [body(): grads = grads + lax.ppermute(grads, ('gx', 'gy'), pairs)]
    ppermute x8, starting transfers between devices: 22.6 us -> 20.1 us  [body(): grads = grads + lax.ppermute(grads, ('gx', 'gy'), pairs)]
where the time goes in v9:
time: 116 us; the launch traced here: 115 us
  starting transfers between devices  64.5 us (56%)
  waiting for transfers between devices  35.1 us (30%)
  local copies, waits for them, and re-layouts  5.2 us (4%)
  matrix products  4.89 us (4%)
  other arithmetic  3.34 us (3%)
  between operations  1.93 us (2%)
    ppermute x4, starting transfers between devices, shift_from(): lax.ppermute(face, axis, [(i, (i + step) % count) for i in range(count)])  29.4 us
    ppermute x8, waiting for transfers between devices, body(): grads = grads + lax.ppermute(grads, ('gx', 'gy'), pairs)  26.5 us
    ppermute x8, starting transfers between devices, body(): grads = grads + lax.ppermute(grads, ('gx', 'gy'), pairs)  20.1 us
    ppermute x2, waiting for transfers between devices, body(): got = lax.ppermute(message, ('gx', 'gy'), pairs)  8.51 us
    ppermute x1, starting transfers between devices, body(): lax.ppermute(jnp.where(yodd, up_y, down_y), 'gy', [(i, (i + 1) % ny if i...  7.56 us
    ppermute x2, starting transfers between devices, body(): got = lax.ppermute(message, ('gx', 'gy'), pairs)  5.49 us
  transfers between devices with their start and end apart: 16, of which 9 were waited for; matrix products, arithmetic and copies ran while one was open for 5% of the time, Pallas kernels for 0%

profile of v9, /device:TPU:14, one launch (start us, length us, event | category | flops | bytes accessed | tf_op | source)
XLA Modules:
  0.0 114.9 jit_solution(17669051866200924907)
XLA Ops:
  1.5 8.2 %collective-permute-start = (f32[2,8,128]{2,1,0:T(8,128)S(1)}, f32[2,8,128]{2,1,0:T(8,128)S(1)}, u32[]{:S(2)}, u32[]{:S(2)}) collective-permute-start(f32[2,8,128]{2,1,0:T(8,128)S(1)} %get-tuple-element.18), channel_id=1, source_target_pairs={{0,1},{1,2},{2,3},{3,4},{4,5},{5,6},{6,7},{7,8},{8,9},{9,10},{10,1... | collective-permute-start | bytes 24584 | tf_op jit(solution)/shard_map/ppermute | solution.py:11
  9.7 16.8 %collective-permute-start.1 = (f32[2,8,128]{2,1,0:T(8,128)S(1)}, f32[2,8,128]{2,1,0:T(8,128)S(1)}, u32[]{:S(2)}, u32[]{:S(2)}) collective-permute-start(f32[2,8,128]{2,1,0:T(8,128)S(1)} %get-tuple-element.19), channel_id=1, source_target_pairs={{0,15},{1,0},{2,1},{3,2},{4,3},{5,4},{6,5},{7,6},{8,7},{9,8},{10,9... | collective-permute-start | bytes 24584 | tf_op jit(solution)/shard_map/ppermute | solution.py:11
  26.4 2.5 %collective-permute-start.2 = (f32[2,8,128]{2,0,1:T(2,128)S(1)}, f32[2,8,128]{2,0,1:T(2,128)S(1)}, u32[]{:S(2)}, u32[]{:S(2)}) collective-permute-start(f32[2,8,128]{2,0,1:T(2,128)S(1)} %bitcast.252), channel_id=1, source_target_pairs={{0,1008},{16,0},{32,16},{48,32},{64,48},{80,64},{96,80},{112,96},{... | collective-permute-start | bytes 24584 | tf_op jit(solution)/shard_map/ppermute | solution.py:11
  29.0 1.9 %collective-permute-start.3 = (f32[2,8,128]{2,0,1:T(2,128)S(1)}, f32[2,8,128]{2,0,1:T(2,128)S(1)}, u32[]{:S(2)}, u32[]{:S(2)}) collective-permute-start(f32[2,8,128]{2,0,1:T(2,128)S(1)} %bitcast.251), channel_id=1, source_target_pairs={{0,16},{16,32},{32,48},{48,64},{64,80},{80,96},{96,112},{112,128},... | collective-permute-start | bytes 24584 | tf_op jit(solution)/shard_map/ppermute | solution.py:11
  41.3 3.3 %collective-permute-start.4 = (f32[36,128]{1,0:T(8,128)S(1)}, f32[36,128]{1,0:T(8,128)S(1)}, u32[]{:S(2)}, u32[]{:S(2)}) collective-permute-start(f32[36,128]{1,0:T(8,128)S(1)} %constant_dynamic-update-slice_fusion.7), channel_id=1, source_target_pairs={{0,32},{1,33},{2,34},{3,35},{4,36},{5,37},{6,38},{7,39},{8,40},{9,... | collective-permute-start | bytes 55304 | tf_op jit(solution)/shard_map/ppermute | solution.py:168
  44.7 2.3 %collective-permute-done.4 = f32[36,128]{1,0:T(8,128)S(1)} collective-permute-done((f32[36,128]{1,0:T(8,128)S(1)}, f32[36,128]{1,0:T(8,128)S(1)}, u32[]{:S(2)}, u32[]{:S(2)}) %collective-permute-start.4) | collective-permute-done | bytes 18464 | tf_op jit(solution)/shard_map/ppermute | solution.py:168
  47.0 3.6 %collective-permute-start.5 = (f32[44,128]{1,0:T(8,128)S(1)}, f32[44,128]{1,0:T(8,128)S(1)}, u32[]{:S(2)}, u32[]{:S(2)}) collective-permute-start(f32[44,128]{1,0:T(8,128)S(1)} %pad_maximum_fusion.16), channel_id=1, source_target_pairs={{0,16},{1,17},{2,18},{3,19},{4,20},{5,21},{6,22},{7,23},{8,24},{9,... | collective-permute-start | bytes 67592 | tf_op jit(solution)/shard_map/ppermute | solution.py:173
  51.4 1.9 %collective-permute-start.7 = (f32[44,128]{1,0:T(8,128)S(1)}, f32[44,128]{1,0:T(8,128)S(1)}, u32[]{:S(2)}, u32[]{:S(2)}) collective-permute-start(f32[44,128]{1,0:T(8,128)S(1)} %pad_maximum_fusion.17), channel_id=1, source_target_pairs={{0,1},{1,0},{2,3},{3,2},{4,5},{5,4},{6,7},{7,6},{8,9},{9,8},{10,11... | collective-permute-start | bytes 67592 | tf_op jit(solution)/shard_map/ppermute | solution.py:173
  53.3 7.7 %collective-permute-done.7 = f32[44,128]{1,0:T(8,128)S(1)} collective-permute-done((f32[44,128]{1,0:T(8,128)S(1)}, f32[44,128]{1,0:T(8,128)S(1)}, u32[]{:S(2)}, u32[]{:S(2)}) %collective-permute-start.7) | collective-permute-done | bytes 22560 | tf_op jit(solution)/shard_map/ppermute | solution.py:173
  61.0 2.9 %collective-permute-start.9 = (f32[36,128]{1,0:T(8,128)S(1)}, f32[36,128]{1,0:T(8,128)S(1)}, u32[]{:S(2)}, u32[]{:S(2)}) collective-permute-start(f32[36,128]{1,0:T(8,128)S(1)} %slice_add_fusion), channel_id=1, source_target_pairs={{0,64},{1,65},{2,66},{3,67},{4,68},{5,69},{6,70},{7,71},{8,72},{9,... | collective-permute-start | bytes 55304 | tf_op jit(solution)/shard_map/ppermute | solution.py:168
  64.1 3.5 %collective-permute-done.9 = f32[36,128]{1,0:T(8,128)S(1)} collective-permute-done((f32[36,128]{1,0:T(8,128)S(1)}, f32[36,128]{1,0:T(8,128)S(1)}, u32[]{:S(2)}, u32[]{:S(2)}) %collective-permute-start.9) | collective-permute-done | bytes 18464 | tf_op jit(solution)/shard_map/ppermute | solution.py:168
  67.6 4.3 %collective-permute-start.10 = (f32[36,128]{1,0:T(8,128)S(1)}, f32[36,128]{1,0:T(8,128)S(1)}, u32[]{:S(2)}, u32[]{:S(2)}) collective-permute-start(f32[36,128]{1,0:T(8,128)S(1)} %add.165), channel_id=1, source_target_pairs={{0,224},{1,225},{2,226},{3,227},{4,228},{5,229},{6,230},{7,231},{8... | collective-permute-start | bytes 55304 | tf_op jit(solution)/shard_map/ppermute | solution.py:168
  72.0 7.6 %collective-permute-start.8 = (f32[8,128]{1,0:T(8,128)S(1)}, f32[8,128]{1,0:T(8,128)S(1)}, u32[]{:S(2)}, u32[]{:S(2)}) collective-permute-start(f32[8,128]{1,0:T(8,128)S(1)} %get-tuple-element.27), channel_id=1, source_target_pairs={{0,15},{1,2},{2,1},{3,4},{4,3},{5,6},{6,5},{7,8},{8,7},{9,10},{10,... | collective-permute-start | bytes 12296 | tf_op jit(solution)/shard_map/ppermute | solution.py:155
  79.6 1.9 %collective-permute-start.6 = (f32[8,128]{1,0:T(8,128)S(1)}, f32[8,128]{1,0:T(8,128)S(1)}, u32[]{:S(2)}, u32[]{:S(2)}) collective-permute-start(f32[8,128]{1,0:T(8,128)S(1)} %get-tuple-element.29), channel_id=1, source_target_pairs={{0,1008},{16,32},{32,16},{48,64},{64,48},{80,96},{96,80},{112,128}... | collective-permute-start | bytes 12296 | tf_op jit(solution)/shard_map/ppermute | solution.py:152
  81.6 1.9 %collective-permute-start.11 = (f32[36,128]{1,0:T(8,128)S(1)}, f32[36,128]{1,0:T(8,128)S(1)}, u32[]{:S(2)}, u32[]{:S(2)}) collective-permute-start(f32[36,128]{1,0:T(8,128)S(1)} %add.166), channel_id=1, source_target_pairs={{0,256},{1,257},{2,258},{3,259},{4,260},{5,261},{6,262},{7,263},{8... | collective-permute-start | bytes 55304 | tf_op jit(solution)/shard_map/ppermute | solution.py:168
  83.6 3.7 %collective-permute-done.11 = f32[36,128]{1,0:T(8,128)S(1)} collective-permute-done((f32[36,128]{1,0:T(8,128)S(1)}, f32[36,128]{1,0:T(8,128)S(1)}, u32[]{:S(2)}, u32[]{:S(2)}) %collective-permute-start.11) | collective-permute-done | bytes 18464 | tf_op jit(solution)/shard_map/ppermute | solution.py:168
  87.3 1.9 %collective-permute-start.12 = (f32[36,128]{1,0:T(8,128)S(1)}, f32[36,128]{1,0:T(8,128)S(1)}, u32[]{:S(2)}, u32[]{:S(2)}) collective-permute-start(f32[36,128]{1,0:T(8,128)S(1)} %add.167), channel_id=1, source_target_pairs={{0,512},{1,513},{2,514},{3,515},{4,516},{5,517},{6,518},{7,519},{8... | collective-permute-start | bytes 55304 | tf_op jit(solution)/shard_map/ppermute | solution.py:168
  89.5 4.4 %collective-permute-done.12 = f32[36,128]{1,0:T(8,128)S(1)} collective-permute-done((f32[36,128]{1,0:T(8,128)S(1)}, f32[36,128]{1,0:T(8,128)S(1)}, u32[]{:S(2)}, u32[]{:S(2)}) %collective-permute-start.12) | collective-permute-done | bytes 18464 | tf_op jit(solution)/shard_map/ppermute | solution.py:168
  93.9 1.9 %collective-permute-start.13 = (f32[36,128]{1,0:T(8,128)S(1)}, f32[36,128]{1,0:T(8,128)S(1)}, u32[]{:S(2)}, u32[]{:S(2)}) collective-permute-start(f32[36,128]{1,0:T(8,128)S(1)} %add.168), channel_id=1, source_target_pairs={{0,2},{1,3},{2,0},{3,1},{4,6},{5,7},{6,4},{7,5},{8,10},{9,11},{10,... | collective-permute-start | bytes 55304 | tf_op jit(solution)/shard_map/ppermute | solution.py:168
  95.8 3.7 %collective-permute-done.13 = f32[36,128]{1,0:T(8,128)S(1)} collective-permute-done((f32[36,128]{1,0:T(8,128)S(1)}, f32[36,128]{1,0:T(8,128)S(1)}, u32[]{:S(2)}, u32[]{:S(2)}) %collective-permute-start.13) | collective-permute-done | bytes 18464 | tf_op jit(solution)/shard_map/ppermute | solution.py:168
  99.5 1.9 %collective-permute-start.14 = (f32[36,128]{1,0:T(8,128)S(1)}, f32[36,128]{1,0:T(8,128)S(1)}, u32[]{:S(2)}, u32[]{:S(2)}) collective-permute-start(f32[36,128]{1,0:T(8,128)S(1)} %add.169), channel_id=1, source_target_pairs={{0,4},{1,5},{2,6},{3,7},{4,0},{5,1},{6,2},{7,3},{8,12},{9,13},{10,... | collective-permute-start | bytes 55304 | tf_op jit(solution)/shard_map/ppermute | solution.py:168
  101.5 4.6 %collective-permute-done.14 = f32[36,128]{1,0:T(8,128)S(1)} collective-permute-done((f32[36,128]{1,0:T(8,128)S(1)}, f32[36,128]{1,0:T(8,128)S(1)}, u32[]{:S(2)}, u32[]{:S(2)}) %collective-permute-start.14) | collective-permute-done | bytes 18464 | tf_op jit(solution)/shard_map/ppermute | solution.py:168
  106.1 1.9 %collective-permute-start.15 = (f32[36,128]{1,0:T(8,128)S(1)}, f32[36,128]{1,0:T(8,128)S(1)}, u32[]{:S(2)}, u32[]{:S(2)}) collective-permute-start(f32[36,128]{1,0:T(8,128)S(1)} %add.170), channel_id=1, source_target_pairs={{0,14},{1,15},{2,12},{3,13},{4,10},{5,11},{6,8},{7,9},{8,6},{9,7},... | collective-permute-start | bytes 55304 | tf_op jit(solution)/shard_map/ppermute | solution.py:168
  108.7 4.2 %collective-permute-done.15 = f32[36,128]{1,0:T(8,128)S(1)} collective-permute-done((f32[36,128]{1,0:T(8,128)S(1)}, f32[36,128]{1,0:T(8,128)S(1)}, u32[]{:S(2)}, u32[]{:S(2)}) %collective-permute-start.15) | collective-permute-done | bytes 18464 | tf_op jit(solution)/shard_map/ppermute | solution.py:168
  (102 shorter events, 14.3 us)
Async XLA Ops:
  0.6 36.6 %copy-start = (bf16[64,64]{1,0:T(8,128)(2,1)S(1)}, bf16[64,64]{1,0:T(8,128)(2,1)}, u32[]{:S(2)}) copy-start(bf16[64,64]{1,0:T(8,128)(2,1)} %param.14) | copy-start | bytes 24580
  1.5 35.1 %collective-permute-start = (f32[2,8,128]{2,1,0:T(8,128)S(1)}, f32[2,8,128]{2,1,0:T(8,128)S(1)}, u32[]{:S(2)}, u32[]{:S(2)}) collective-permute-start(f32[2,8,128]{2,1,0:T(8,128)S(1)} %get-tuple-element.18), channel_id=1, source_target_pairs={{0,1},{1,2},{2,3},{3,4},{4,5},{5,6},{6,7},{7,8},{8,9},{9,10},{10,1... | collective-permute-start | bytes 24584 | tf_op jit(solution)/shard_map/ppermute | solution.py:11
  9.7 27.0 %collective-permute-start.1 = (f32[2,8,128]{2,1,0:T(8,128)S(1)}, f32[2,8,128]{2,1,0:T(8,128)S(1)}, u32[]{:S(2)}, u32[]{:S(2)}) collective-permute-start(f32[2,8,128]{2,1,0:T(8,128)S(1)} %get-tuple-element.19), channel_id=1, source_target_pairs={{0,15},{1,0},{2,1},{3,2},{4,3},{5,4},{6,5},{7,6},{8,7},{9,8},{10,9... | collective-permute-start | bytes 24584 | tf_op jit(solution)/shard_map/ppermute | solution.py:11
  26.4 10.0 %collective-permute-start.2 = (f32[2,8,128]{2,0,1:T(2,128)S(1)}, f32[2,8,128]{2,0,1:T(2,128)S(1)}, u32[]{:S(2)}, u32[]{:S(2)}) collective-permute-start(f32[2,8,128]{2,0,1:T(2,128)S(1)} %bitcast.252), channel_id=1, source_target_pairs={{0,1008},{16,0},{32,16},{48,32},{64,48},{80,64},{96,80},{112,96},{... | collective-permute-start | bytes 24584 | tf_op jit(solution)/shard_map/ppermute | solution.py:11
  29.0 7.6 %collective-permute-start.3 = (f32[2,8,128]{2,0,1:T(2,128)S(1)}, f32[2,8,128]{2,0,1:T(2,128)S(1)}, u32[]{:S(2)}, u32[]{:S(2)}) collective-permute-start(f32[2,8,128]{2,0,1:T(2,128)S(1)} %bitcast.251), channel_id=1, source_target_pairs={{0,16},{16,32},{32,48},{48,64},{64,80},{80,96},{96,112},{112,128},... | collective-permute-start | bytes 24584 | tf_op jit(solution)/shard_map/ppermute | solution.py:11
  34.4 1.1 copy-start.2
  34.4 1.2 %copy-start.1 = (f32[8,8,128]{2,1,0:T(8,128)S(1)}, f32[8,8,128]{2,1,0:T(8,128)}, u32[]{:S(2)}) copy-start(f32[8,8,128]{2,1,0:T(8,128)} %param.8) | copy-start | bytes 98308
  34.5 1.4 %copy-start.4 = (bf16[1,64]{1,0:T(2,128)(2,1)S(1)}, bf16[1,64]{1,0:T(2,128)(2,1)}, u32[]{:S(2)}) copy-start(bf16[1,64]{1,0:T(2,128)(2,1)} %param.15) | copy-start | bytes 388
  35.6 1.2 %copy-start.3 = (bf16[64,7]{0,1:T(8,128)(2,1)S(1)}, bf16[64,7]{0,1:T(8,128)(2,1)}, u32[]{:S(2)}) copy-start(bf16[64,7]{0,1:T(8,128)(2,1)} %param.13) | copy-start | bytes 2692
  41.3 5.7 %collective-permute-start.4 = (f32[36,128]{1,0:T(8,128)S(1)}, f32[36,128]{1,0:T(8,128)S(1)}, u32[]{:S(2)}, u32[]{:S(2)}) collective-permute-start(f32[36,128]{1,0:T(8,128)S(1)} %constant_dynamic-update-slice_fusion.7), channel_id=1, source_target_pairs={{0,32},{1,33},{2,34},{3,35},{4,36},{5,37},{6,38},{7,39},{8,40},{9,... | collective-permute-start | bytes 55304 | tf_op jit(solution)/shard_map/ppermute | solution.py:168
  47.0 4.4 %collective-permute-start.5 = (f32[44,128]{1,0:T(8,128)S(1)}, f32[44,128]{1,0:T(8,128)S(1)}, u32[]{:S(2)}, u32[]{:S(2)}) collective-permute-start(f32[44,128]{1,0:T(8,128)S(1)} %pad_maximum_fusion.16), channel_id=1, source_target_pairs={{0,16},{1,17},{2,18},{3,19},{4,20},{5,21},{6,22},{7,23},{8,24},{9,... | collective-permute-start | bytes 67592 | tf_op jit(solution)/shard_map/ppermute | solution.py:173
  51.4 9.6 %collective-permute-start.7 = (f32[44,128]{1,0:T(8,128)S(1)}, f32[44,128]{1,0:T(8,128)S(1)}, u32[]{:S(2)}, u32[]{:S(2)}) collective-permute-start(f32[44,128]{1,0:T(8,128)S(1)} %pad_maximum_fusion.17), channel_id=1, source_target_pairs={{0,1},{1,0},{2,3},{3,2},{4,5},{5,4},{6,7},{7,6},{8,9},{9,8},{10,11... | collective-permute-start | bytes 67592 | tf_op jit(solution)/shard_map/ppermute | solution.py:173
  61.0 6.6 %collective-permute-start.9 = (f32[36,128]{1,0:T(8,128)S(1)}, f32[36,128]{1,0:T(8,128)S(1)}, u32[]{:S(2)}, u32[]{:S(2)}) collective-permute-start(f32[36,128]{1,0:T(8,128)S(1)} %slice_add_fusion), channel_id=1, source_target_pairs={{0,64},{1,65},{2,66},{3,67},{4,68},{5,69},{6,70},{7,71},{8,72},{9,... | collective-permute-start | bytes 55304 | tf_op jit(solution)/shard_map/ppermute | solution.py:168
  67.6 13.9 %collective-permute-start.10 = (f32[36,128]{1,0:T(8,128)S(1)}, f32[36,128]{1,0:T(8,128)S(1)}, u32[]{:S(2)}, u32[]{:S(2)}) collective-permute-start(f32[36,128]{1,0:T(8,128)S(1)} %add.165), channel_id=1, source_target_pairs={{0,224},{1,225},{2,226},{3,227},{4,228},{5,229},{6,230},{7,231},{8... | collective-permute-start | bytes 55304 | tf_op jit(solution)/shard_map/ppermute | solution.py:168
  72.0 29.4 %collective-permute-start.8 = (f32[8,128]{1,0:T(8,128)S(1)}, f32[8,128]{1,0:T(8,128)S(1)}, u32[]{:S(2)}, u32[]{:S(2)}) collective-permute-start(f32[8,128]{1,0:T(8,128)S(1)} %get-tuple-element.27), channel_id=1, source_target_pairs={{0,15},{1,2},{2,1},{3,4},{4,3},{5,6},{6,5},{7,8},{8,7},{9,10},{10,... | collective-permute-start | bytes 12296 | tf_op jit(solution)/shard_map/ppermute | solution.py:155
  79.6 16.2 %collective-permute-start.6 = (f32[8,128]{1,0:T(8,128)S(1)}, f32[8,128]{1,0:T(8,128)S(1)}, u32[]{:S(2)}, u32[]{:S(2)}) collective-permute-start(f32[8,128]{1,0:T(8,128)S(1)} %get-tuple-element.29), channel_id=1, source_target_pairs={{0,1008},{16,32},{32,16},{48,64},{64,48},{80,96},{96,80},{112,128}... | collective-permute-start | bytes 12296 | tf_op jit(solution)/shard_map/ppermute | solution.py:152
  81.6 5.7 %collective-permute-start.11 = (f32[36,128]{1,0:T(8,128)S(1)}, f32[36,128]{1,0:T(8,128)S(1)}, u32[]{:S(2)}, u32[]{:S(2)}) collective-permute-start(f32[36,128]{1,0:T(8,128)S(1)} %add.166), channel_id=1, source_target_pairs={{0,256},{1,257},{2,258},{3,259},{4,260},{5,261},{6,262},{7,263},{8... | collective-permute-start | bytes 55304 | tf_op jit(solution)/shard_map/ppermute | solution.py:168
  87.3 6.6 %collective-permute-start.12 = (f32[36,128]{1,0:T(8,128)S(1)}, f32[36,128]{1,0:T(8,128)S(1)}, u32[]{:S(2)}, u32[]{:S(2)}) collective-permute-start(f32[36,128]{1,0:T(8,128)S(1)} %add.167), channel_id=1, source_target_pairs={{0,512},{1,513},{2,514},{3,515},{4,516},{5,517},{6,518},{7,519},{8... | collective-permute-start | bytes 55304 | tf_op jit(solution)/shard_map/ppermute | solution.py:168
  93.9 5.7 %collective-permute-start.13 = (f32[36,128]{1,0:T(8,128)S(1)}, f32[36,128]{1,0:T(8,128)S(1)}, u32[]{:S(2)}, u32[]{:S(2)}) collective-permute-start(f32[36,128]{1,0:T(8,128)S(1)} %add.168), channel_id=1, source_target_pairs={{0,2},{1,3},{2,0},{3,1},{4,6},{5,7},{6,4},{7,5},{8,10},{9,11},{10,... | collective-permute-start | bytes 55304 | tf_op jit(solution)/shard_map/ppermute | solution.py:168
  99.5 6.6 %collective-permute-start.14 = (f32[36,128]{1,0:T(8,128)S(1)}, f32[36,128]{1,0:T(8,128)S(1)}, u32[]{:S(2)}, u32[]{:S(2)}) collective-permute-start(f32[36,128]{1,0:T(8,128)S(1)} %add.169), channel_id=1, source_target_pairs={{0,4},{1,5},{2,6},{3,7},{4,0},{5,1},{6,2},{7,3},{8,12},{9,13},{10,... | collective-permute-start | bytes 55304 | tf_op jit(solution)/shard_map/ppermute | solution.py:168
  106.1 6.9 %collective-permute-start.15 = (f32[36,128]{1,0:T(8,128)S(1)}, f32[36,128]{1,0:T(8,128)S(1)}, u32[]{:S(2)}, u32[]{:S(2)}) collective-permute-start(f32[36,128]{1,0:T(8,128)S(1)} %add.170), channel_id=1, source_target_pairs={{0,14},{1,15},{2,12},{3,13},{4,10},{5,11},{6,8},{7,9},{8,6},{9,7},... | collective-permute-start | bytes 55304 | tf_op jit(solution)/shard_map/ppermute | solution.py:168

commit v10 on v8

--- a/solution.py
+++ b/solution.py
@@ -92,13 +92,11 @@
     nblocks = sizex * sizey * sizez // 64
     cells = sizex * sizey * sizez
 
-    both = jnp.stack([velocity, cotangent])
-    xlo = shift_from(both[:, -1], "gx", 1)
-    xhi = shift_from(both[:, 0], "gx", -1)
-    ylo = shift_from(both[:, :, -1], "gy", 1)
-    yhi = shift_from(both[:, :, 0], "gy", -1)
-    padded = padded_of(velocity, xlo[0], xhi[0], ylo[0], yhi[0])
-    cot_pad = padded_of(cotangent, xlo[1], xhi[1], ylo[1], yhi[1])
+    xlo = shift_from(velocity[-1], "gx", 1)
+    xhi = shift_from(velocity[0], "gx", -1)
+    ylo = shift_from(velocity[:, -1], "gy", 1)
+    yhi = shift_from(velocity[:, 0], "gy", -1)
+    padded = padded_of(velocity, xlo, xhi, ylo, yhi)
 
     ids = block_ids.reshape(slots)
     live = (jnp.arange(slots) < fluid_count[0, 0]).astype(jnp.bfloat16)
@@ -142,8 +140,8 @@
     ny = lax.axis_size("gy")
     xodd = lax.axis_index("gx") % 2 == 1
     yodd = lax.axis_index("gy") % 2 == 1
-    up_x, down_x = dfeat[1, -1], dfeat[2, 0]
-    up_y, down_y = dfeat[3, :, -1], dfeat[4, :, 0]
+    up_x, down_x = jnp.stack([dfeat[1, -1], cotangent[-1]]), jnp.stack([dfeat[2, 0], cotangent[0]])
+    up_y, down_y = jnp.stack([dfeat[3, :, -1], cotangent[:, -1]]), jnp.stack([dfeat[4, :, 0], cotangent[:, 0]])
     pair_face = {"gx": jnp.where(xodd, down_x, up_x), "gy": jnp.where(yodd, down_y, up_y)}
     other_x = lax.ppermute(
         jnp.where(xodd, up_x, down_x), "gx", [(i, (i + 1) % nx if i % 2 else (i - 1) % nx) for i in range(nx)]
@@ -173,6 +171,8 @@
     from_xhi = jnp.where(xodd, other_x, received["gx"])
     from_ylo = jnp.where(yodd, received["gy"], other_y)
     from_yhi = jnp.where(yodd, other_y, received["gy"])
+    cot_pad = padded_of(cotangent, from_xlo[1], from_xhi[1], from_ylo[1], from_yhi[1])
+    from_xlo, from_xhi, from_ylo, from_yhi = from_xlo[0], from_xhi[0], from_ylo[0], from_yhi[0]
 
     side1 = jnp.concatenate([from_xlo[None], dfeat[1, :-1]], axis=0)
     side2 = jnp.concatenate([dfeat[2, 1:], from_xhi[None]], axis=0)

time: 115 us -> 120 us (1.043)
  the two profiles are of different devices: /device:TPU:14 before, /device:TPU:2 now
where the time goes in v10:
time: 120 us; the launch traced here: 119 us
  starting transfers between devices  69 us (58%)
  waiting for transfers between devices  30.7 us (26%)
  local copies, waits for them, and re-layouts  8.13 us (7%)
  matrix products  6.85 us (6%)
  other arithmetic  2.5 us (2%)
  between operations  1.92 us (2%)
    ppermute x4, starting transfers between devices, shift_from(): lax.ppermute(face, axis, [(i, (i + step) % count) for i in range(count)])  30.5 us
    ppermute x8, waiting for transfers between devices, body(): grads = grads + lax.ppermute(grads, ('gx', 'gy'), pairs)  28.2 us
    ppermute x8, starting transfers between devices, body(): grads = grads + lax.ppermute(grads, ('gx', 'gy'), pairs)  24.1 us
    ppermute x1, starting transfers between devices, body(): lax.ppermute(jnp.where(yodd, up_y, down_y), 'gy', [(i, (i + 1) % ny if i...  8.64 us
    ppermute x2, starting transfers between devices, body(): got = lax.ppermute(message, ('gx', 'gy'), pairs)  3.84 us
  transfers between devices with their start and end apart: 16, of which 9 were waited for; matrix products, arithmetic and copies ran while one was open for 9% of the time, Pallas kernels for 0%

profile of v10, /device:TPU:2, one launch (start us, length us, event | category | flops | bytes accessed | tf_op | source)
XLA Modules:
  0.0 119.2 jit_solution(10011565293279928118)
XLA Ops:
  1.4 1.9 %collective-permute-start.3 = (f32[8,128]{1,0:T(8,128)S(1)}, f32[8,128]{1,0:T(8,128)S(1)}, u32[]{:S(2)}, u32[]{:S(2)}) collective-permute-start(f32[8,128]{1,0:T(8,128)S(1)} %get-tuple-element.30), channel_id=1, source_target_pairs={{0,16},{16,32},{32,48},{48,64},{64,80},{80,96},{96,112},{112,128},... | collective-permute-start | bytes 12296 | tf_op jit(solution)/shard_map/ppermute | solution.py:11
  3.3 3.6 %collective-permute-start.2 = (f32[8,128]{1,0:T(8,128)S(1)}, f32[8,128]{1,0:T(8,128)S(1)}, u32[]{:S(2)}, u32[]{:S(2)}) collective-permute-start(f32[8,128]{1,0:T(8,128)S(1)} %get-tuple-element.31), channel_id=1, source_target_pairs={{0,1008},{16,0},{32,16},{48,32},{64,48},{80,64},{96,80},{112,96},{... | collective-permute-start | bytes 12296 | tf_op jit(solution)/shard_map/ppermute | solution.py:11
  7.8 23.0 %collective-permute-start.1 = (f32[8,128]{1,0:T(8,128)S(1)}, f32[8,128]{1,0:T(8,128)S(1)}, u32[]{:S(2)}, u32[]{:S(2)}) collective-permute-start(f32[8,128]{1,0:T(8,128)S(1)} %bitcast.227), channel_id=1, source_target_pairs={{0,15},{1,0},{2,1},{3,2},{4,3},{5,4},{6,5},{7,6},{8,7},{9,8},{10,9... | collective-permute-start | bytes 12296 | tf_op jit(solution)/shard_map/ppermute | solution.py:11
  30.8 1.9 %collective-permute-start = (f32[8,128]{1,0:T(8,128)S(1)}, f32[8,128]{1,0:T(8,128)S(1)}, u32[]{:S(2)}, u32[]{:S(2)}) collective-permute-start(f32[8,128]{1,0:T(8,128)S(1)} %bitcast.226), channel_id=1, source_target_pairs={{0,1},{1,2},{2,3},{3,4},{4,5},{5,6},{6,7},{7,8},{8,9},{9,10},{10,1... | collective-permute-start | bytes 12296 | tf_op jit(solution)/shard_map/ppermute | solution.py:11
  41.0 1.3 %collective-permute-done = f32[8,128]{1,0:T(8,128)S(1)} collective-permute-done((f32[8,128]{1,0:T(8,128)S(1)}, f32[8,128]{1,0:T(8,128)S(1)}, u32[]{:S(2)}, u32[]{:S(2)}) %collective-permute-start) | collective-permute-done | bytes 4128 | tf_op jit(solution)/shard_map/ppermute | solution.py:11
  46.4 6.4 %collective-permute-start.4 = (f32[36,128]{1,0:T(8,128)S(1)}, f32[36,128]{1,0:T(8,128)S(1)}, u32[]{:S(2)}, u32[]{:S(2)}) collective-permute-start(f32[36,128]{1,0:T(8,128)S(1)} %constant_dynamic-update-slice_fusion), channel_id=1, source_target_pairs={{0,32},{1,33},{2,34},{3,35},{4,36},{5,37},{6,38},{7,39},{8,40},{9,... | collective-permute-start | bytes 55304 | tf_op jit(solution)/shard_map/ppermute | solution.py:162
  52.9 1.9 %collective-permute-start.8 = (f32[2,8,128]{2,1,0:T(8,128)S(1)}, f32[2,8,128]{2,1,0:T(8,128)S(1)}, u32[]{:S(2)}, u32[]{:S(2)}) collective-permute-start(f32[2,8,128]{2,1,0:T(8,128)S(1)} %get-tuple-element.34), channel_id=1, source_target_pairs={{0,1008},{16,32},{32,16},{48,64},{64,48},{80,96},{96,80},{112,128}... | collective-permute-start | bytes 24584 | tf_op jit(solution)/shard_map/ppermute | solution.py:146
  56.5 1.9 %collective-permute-start.5 = (f32[52,128]{1,0:T(8,128)S(1)}, f32[52,128]{1,0:T(8,128)S(1)}, u32[]{:S(2)}, u32[]{:S(2)}) collective-permute-start(f32[52,128]{1,0:T(8,128)S(1)} %pad_maximum_fusion.20), channel_id=1, source_target_pairs={{0,16},{1,17},{2,18},{3,19},{4,20},{5,21},{6,22},{7,23},{8,24},{9,... | collective-permute-start | bytes 79880 | tf_op jit(solution)/shard_map/ppermute | solution.py:167
  59.6 1.9 %collective-permute-start.6 = (f32[52,128]{1,0:T(8,128)S(1)}, f32[52,128]{1,0:T(8,128)S(1)}, u32[]{:S(2)}, u32[]{:S(2)}) collective-permute-start(f32[52,128]{1,0:T(8,128)S(1)} %pad_maximum_fusion.21), channel_id=1, source_target_pairs={{0,1},{1,0},{2,3},{3,2},{4,5},{5,4},{6,7},{7,6},{8,9},{9,8},{10,11... | collective-permute-start | bytes 79880 | tf_op jit(solution)/shard_map/ppermute | solution.py:167
  61.7 8.6 %collective-permute-start.7 = (f32[2,8,128]{2,1,0:T(8,128)S(1)}, f32[2,8,128]{2,1,0:T(8,128)S(1)}, u32[]{:S(2)}, u32[]{:S(2)}) collective-permute-start(f32[2,8,128]{2,1,0:T(8,128)S(1)} %get-tuple-element.37), channel_id=1, source_target_pairs={{0,15},{1,2},{2,1},{3,4},{4,3},{5,6},{6,5},{7,8},{8,7},{9,10},{10,... | collective-permute-start | bytes 24584 | tf_op jit(solution)/shard_map/ppermute | solution.py:149
  70.3 3.6 %collective-permute-start.9 = (f32[36,128]{1,0:T(8,128)S(1)}, f32[36,128]{1,0:T(8,128)S(1)}, u32[]{:S(2)}, u32[]{:S(2)}) collective-permute-start(f32[36,128]{1,0:T(8,128)S(1)} %slice_add_fusion), channel_id=1, source_target_pairs={{0,64},{1,65},{2,66},{3,67},{4,68},{5,69},{6,70},{7,71},{8,72},{9,... | collective-permute-start | bytes 55304 | tf_op jit(solution)/shard_map/ppermute | solution.py:162
  73.9 3.0 %collective-permute-done.9 = f32[36,128]{1,0:T(8,128)S(1)} collective-permute-done((f32[36,128]{1,0:T(8,128)S(1)}, f32[36,128]{1,0:T(8,128)S(1)}, u32[]{:S(2)}, u32[]{:S(2)}) %collective-permute-start.9) | collective-permute-done | bytes 18464 | tf_op jit(solution)/shard_map/ppermute | solution.py:162
  76.9 3.6 %collective-permute-start.10 = (f32[36,128]{1,0:T(8,128)S(1)}, f32[36,128]{1,0:T(8,128)S(1)}, u32[]{:S(2)}, u32[]{:S(2)}) collective-permute-start(f32[36,128]{1,0:T(8,128)S(1)} %add.165), channel_id=1, source_target_pairs={{0,224},{1,225},{2,226},{3,227},{4,228},{5,229},{6,230},{7,231},{8... | collective-permute-start | bytes 55304 | tf_op jit(solution)/shard_map/ppermute | solution.py:162
  80.5 5.1 %collective-permute-done.10 = f32[36,128]{1,0:T(8,128)S(1)} collective-permute-done((f32[36,128]{1,0:T(8,128)S(1)}, f32[36,128]{1,0:T(8,128)S(1)}, u32[]{:S(2)}, u32[]{:S(2)}) %collective-permute-start.10) | collective-permute-done | bytes 18464 | tf_op jit(solution)/shard_map/ppermute | solution.py:162
  85.6 1.9 %collective-permute-start.11 = (f32[36,128]{1,0:T(8,128)S(1)}, f32[36,128]{1,0:T(8,128)S(1)}, u32[]{:S(2)}, u32[]{:S(2)}) collective-permute-start(f32[36,128]{1,0:T(8,128)S(1)} %add.166), channel_id=1, source_target_pairs={{0,256},{1,257},{2,258},{3,259},{4,260},{5,261},{6,262},{7,263},{8... | collective-permute-start | bytes 55304 | tf_op jit(solution)/shard_map/ppermute | solution.py:162
  87.5 3.7 %collective-permute-done.11 = f32[36,128]{1,0:T(8,128)S(1)} collective-permute-done((f32[36,128]{1,0:T(8,128)S(1)}, f32[36,128]{1,0:T(8,128)S(1)}, u32[]{:S(2)}, u32[]{:S(2)}) %collective-permute-start.11) | collective-permute-done | bytes 18464 | tf_op jit(solution)/shard_map/ppermute | solution.py:162
  91.3 1.9 %collective-permute-start.12 = (f32[36,128]{1,0:T(8,128)S(1)}, f32[36,128]{1,0:T(8,128)S(1)}, u32[]{:S(2)}, u32[]{:S(2)}) collective-permute-start(f32[36,128]{1,0:T(8,128)S(1)} %add.167), channel_id=1, source_target_pairs={{0,512},{1,513},{2,514},{3,515},{4,516},{5,517},{6,518},{7,519},{8... | collective-permute-start | bytes 55304 | tf_op jit(solution)/shard_map/ppermute | solution.py:162
  93.2 4.6 %collective-permute-done.12 = f32[36,128]{1,0:T(8,128)S(1)} collective-permute-done((f32[36,128]{1,0:T(8,128)S(1)}, f32[36,128]{1,0:T(8,128)S(1)}, u32[]{:S(2)}, u32[]{:S(2)}) %collective-permute-start.12) | collective-permute-done | bytes 18464 | tf_op jit(solution)/shard_map/ppermute | solution.py:162
  97.8 2.5 %collective-permute-start.13 = (f32[36,128]{1,0:T(8,128)S(1)}, f32[36,128]{1,0:T(8,128)S(1)}, u32[]{:S(2)}, u32[]{:S(2)}) collective-permute-start(f32[36,128]{1,0:T(8,128)S(1)} %add.168), channel_id=1, source_target_pairs={{0,2},{1,3},{2,0},{3,1},{4,6},{5,7},{6,4},{7,5},{8,10},{9,11},{10,... | collective-permute-start | bytes 55304 | tf_op jit(solution)/shard_map/ppermute | solution.py:162
  100.4 3.3 %collective-permute-done.13 = f32[36,128]{1,0:T(8,128)S(1)} collective-permute-done((f32[36,128]{1,0:T(8,128)S(1)}, f32[36,128]{1,0:T(8,128)S(1)}, u32[]{:S(2)}, u32[]{:S(2)}) %collective-permute-start.13) | collective-permute-done | bytes 18464 | tf_op jit(solution)/shard_map/ppermute | solution.py:162
  103.7 1.9 %collective-permute-start.14 = (f32[36,128]{1,0:T(8,128)S(1)}, f32[36,128]{1,0:T(8,128)S(1)}, u32[]{:S(2)}, u32[]{:S(2)}) collective-permute-start(f32[36,128]{1,0:T(8,128)S(1)} %add.169), channel_id=1, source_target_pairs={{0,4},{1,5},{2,6},{3,7},{4,0},{5,1},{6,2},{7,3},{8,12},{9,13},{10,... | collective-permute-start | bytes 55304 | tf_op jit(solution)/shard_map/ppermute | solution.py:162
  105.7 4.7 %collective-permute-done.14 = f32[36,128]{1,0:T(8,128)S(1)} collective-permute-done((f32[36,128]{1,0:T(8,128)S(1)}, f32[36,128]{1,0:T(8,128)S(1)}, u32[]{:S(2)}, u32[]{:S(2)}) %collective-permute-start.14) | collective-permute-done | bytes 18464 | tf_op jit(solution)/shard_map/ppermute | solution.py:162
  110.4 2.4 %collective-permute-start.15 = (f32[36,128]{1,0:T(8,128)S(1)}, f32[36,128]{1,0:T(8,128)S(1)}, u32[]{:S(2)}, u32[]{:S(2)}) collective-permute-start(f32[36,128]{1,0:T(8,128)S(1)} %add.170), channel_id=1, source_target_pairs={{0,14},{1,15},{2,12},{3,13},{4,10},{5,11},{6,8},{7,9},{8,6},{9,7},... | collective-permute-start | bytes 55304 | tf_op jit(solution)/shard_map/ppermute | solution.py:162
  113.5 3.8 %collective-permute-done.15 = f32[36,128]{1,0:T(8,128)S(1)} collective-permute-done((f32[36,128]{1,0:T(8,128)S(1)}, f32[36,128]{1,0:T(8,128)S(1)}, u32[]{:S(2)}, u32[]{:S(2)}) %collective-permute-start.15) | collective-permute-done | bytes 18464 | tf_op jit(solution)/shard_map/ppermute | solution.py:162
  (104 shorter events, 18.7 us)
Async XLA Ops:
  0.6 42.6 %copy-start = (bf16[64,64]{1,0:T(8,128)(2,1)S(1)}, bf16[64,64]{1,0:T(8,128)(2,1)}, u32[]{:S(2)}) copy-start(bf16[64,64]{1,0:T(8,128)(2,1)} %param.14) | copy-start | bytes 24580
  1.4 39.6 %collective-permute-start.3 = (f32[8,128]{1,0:T(8,128)S(1)}, f32[8,128]{1,0:T(8,128)S(1)}, u32[]{:S(2)}, u32[]{:S(2)}) collective-permute-start(f32[8,128]{1,0:T(8,128)S(1)} %get-tuple-element.30), channel_id=1, source_target_pairs={{0,16},{16,32},{32,48},{48,64},{64,80},{80,96},{96,112},{112,128},... | collective-permute-start | bytes 12296 | tf_op jit(solution)/shard_map/ppermute | solution.py:11
  3.3 37.7 %collective-permute-start.2 = (f32[8,128]{1,0:T(8,128)S(1)}, f32[8,128]{1,0:T(8,128)S(1)}, u32[]{:S(2)}, u32[]{:S(2)}) collective-permute-start(f32[8,128]{1,0:T(8,128)S(1)} %get-tuple-element.31), channel_id=1, source_target_pairs={{0,1008},{16,0},{32,16},{48,32},{64,48},{80,64},{96,80},{112,96},{... | collective-permute-start | bytes 12296 | tf_op jit(solution)/shard_map/ppermute | solution.py:11
  7.8 33.2 %collective-permute-start.1 = (f32[8,128]{1,0:T(8,128)S(1)}, f32[8,128]{1,0:T(8,128)S(1)}, u32[]{:S(2)}, u32[]{:S(2)}) collective-permute-start(f32[8,128]{1,0:T(8,128)S(1)} %bitcast.227), channel_id=1, source_target_pairs={{0,15},{1,0},{2,1},{3,2},{4,3},{5,4},{6,5},{7,6},{8,7},{9,8},{10,9... | collective-permute-start | bytes 12296 | tf_op jit(solution)/shard_map/ppermute | solution.py:11
  30.8 11.5 %collective-permute-start = (f32[8,128]{1,0:T(8,128)S(1)}, f32[8,128]{1,0:T(8,128)S(1)}, u32[]{:S(2)}, u32[]{:S(2)}) collective-permute-start(f32[8,128]{1,0:T(8,128)S(1)} %bitcast.226), channel_id=1, source_target_pairs={{0,1},{1,2},{2,3},{3,4},{4,5},{5,6},{6,7},{7,8},{8,9},{9,10},{10,1... | collective-permute-start | bytes 12296 | tf_op jit(solution)/shard_map/ppermute | solution.py:11
  39.4 1.3 %copy-start.2 = (f32[8,8,128]{2,1,0:T(8,128)S(1)}, f32[8,8,128]{2,1,0:T(8,128)}, u32[]{:S(2)}) copy-start(f32[8,8,128]{2,1,0:T(8,128)} %param.9) | copy-start | bytes 98308
  39.4 1.4 %copy-start.4 = (bf16[1,64]{1,0:T(2,128)(2,1)S(1)}, bf16[1,64]{1,0:T(2,128)(2,1)}, u32[]{:S(2)}) copy-start(bf16[1,64]{1,0:T(2,128)(2,1)} %param.15) | copy-start | bytes 388
  39.4 1.4 %copy-start.1 = (f32[8,8,128]{2,1,0:T(8,128)S(1)}, f32[8,8,128]{2,1,0:T(8,128)}, u32[]{:S(2)}) copy-start(f32[8,8,128]{2,1,0:T(8,128)} %param.8) | copy-start | bytes 98308
  40.1 2.7 %copy-start.3 = (bf16[64,7]{0,1:T(8,128)(2,1)S(1)}, bf16[64,7]{0,1:T(8,128)(2,1)}, u32[]{:S(2)}) copy-start(bf16[64,7]{0,1:T(8,128)(2,1)} %param.13) | copy-start | bytes 2692
  46.4 10.0 %collective-permute-start.4 = (f32[36,128]{1,0:T(8,128)S(1)}, f32[36,128]{1,0:T(8,128)S(1)}, u32[]{:S(2)}, u32[]{:S(2)}) collective-permute-start(f32[36,128]{1,0:T(8,128)S(1)} %constant_dynamic-update-slice_fusion), channel_id=1, source_target_pairs={{0,32},{1,33},{2,34},{3,35},{4,36},{5,37},{6,38},{7,39},{8,40},{9,... | collective-permute-start | bytes 55304 | tf_op jit(solution)/shard_map/ppermute | solution.py:162
  52.9 21.0 %collective-permute-start.8 = (f32[2,8,128]{2,1,0:T(8,128)S(1)}, f32[2,8,128]{2,1,0:T(8,128)S(1)}, u32[]{:S(2)}, u32[]{:S(2)}) collective-permute-start(f32[2,8,128]{2,1,0:T(8,128)S(1)} %get-tuple-element.34), channel_id=1, source_target_pairs={{0,1008},{16,32},{32,16},{48,64},{64,48},{80,96},{96,80},{112,128}... | collective-permute-start | bytes 24584 | tf_op jit(solution)/shard_map/ppermute | solution.py:146
  56.5 3.1 %collective-permute-start.5 = (f32[52,128]{1,0:T(8,128)S(1)}, f32[52,128]{1,0:T(8,128)S(1)}, u32[]{:S(2)}, u32[]{:S(2)}) collective-permute-start(f32[52,128]{1,0:T(8,128)S(1)} %pad_maximum_fusion.20), channel_id=1, source_target_pairs={{0,16},{1,17},{2,18},{3,19},{4,20},{5,21},{6,22},{7,23},{8,24},{9,... | collective-permute-start | bytes 79880 | tf_op jit(solution)/shard_map/ppermute | solution.py:167
  59.6 10.7 %collective-permute-start.6 = (f32[52,128]{1,0:T(8,128)S(1)}, f32[52,128]{1,0:T(8,128)S(1)}, u32[]{:S(2)}, u32[]{:S(2)}) collective-permute-start(f32[52,128]{1,0:T(8,128)S(1)} %pad_maximum_fusion.21), channel_id=1, source_target_pairs={{0,1},{1,0},{2,3},{3,2},{4,5},{5,4},{6,7},{7,6},{8,9},{9,8},{10,11... | collective-permute-start | bytes 79880 | tf_op jit(solution)/shard_map/ppermute | solution.py:167
  61.7 31.5 %collective-permute-start.7 = (f32[2,8,128]{2,1,0:T(8,128)S(1)}, f32[2,8,128]{2,1,0:T(8,128)S(1)}, u32[]{:S(2)}, u32[]{:S(2)}) collective-permute-start(f32[2,8,128]{2,1,0:T(8,128)S(1)} %get-tuple-element.37), channel_id=1, source_target_pairs={{0,15},{1,2},{2,1},{3,4},{4,3},{5,6},{6,5},{7,8},{8,7},{9,10},{10,... | collective-permute-start | bytes 24584 | tf_op jit(solution)/shard_map/ppermute | solution.py:149
  70.3 6.6 %collective-permute-start.9 = (f32[36,128]{1,0:T(8,128)S(1)}, f32[36,128]{1,0:T(8,128)S(1)}, u32[]{:S(2)}, u32[]{:S(2)}) collective-permute-start(f32[36,128]{1,0:T(8,128)S(1)} %slice_add_fusion), channel_id=1, source_target_pairs={{0,64},{1,65},{2,66},{3,67},{4,68},{5,69},{6,70},{7,71},{8,72},{9,... | collective-permute-start | bytes 55304 | tf_op jit(solution)/shard_map/ppermute | solution.py:162
  76.9 8.7 %collective-permute-start.10 = (f32[36,128]{1,0:T(8,128)S(1)}, f32[36,128]{1,0:T(8,128)S(1)}, u32[]{:S(2)}, u32[]{:S(2)}) collective-permute-start(f32[36,128]{1,0:T(8,128)S(1)} %add.165), channel_id=1, source_target_pairs={{0,224},{1,225},{2,226},{3,227},{4,228},{5,229},{6,230},{7,231},{8... | collective-permute-start | bytes 55304 | tf_op jit(solution)/shard_map/ppermute | solution.py:162
  85.6 5.7 %collective-permute-start.11 = (f32[36,128]{1,0:T(8,128)S(1)}, f32[36,128]{1,0:T(8,128)S(1)}, u32[]{:S(2)}, u32[]{:S(2)}) collective-permute-start(f32[36,128]{1,0:T(8,128)S(1)} %add.166), channel_id=1, source_target_pairs={{0,256},{1,257},{2,258},{3,259},{4,260},{5,261},{6,262},{7,263},{8... | collective-permute-start | bytes 55304 | tf_op jit(solution)/shard_map/ppermute | solution.py:162
  91.3 6.6 %collective-permute-start.12 = (f32[36,128]{1,0:T(8,128)S(1)}, f32[36,128]{1,0:T(8,128)S(1)}, u32[]{:S(2)}, u32[]{:S(2)}) collective-permute-start(f32[36,128]{1,0:T(8,128)S(1)} %add.167), channel_id=1, source_target_pairs={{0,512},{1,513},{2,514},{3,515},{4,516},{5,517},{6,518},{7,519},{8... | collective-permute-start | bytes 55304 | tf_op jit(solution)/shard_map/ppermute | solution.py:162
  97.8 5.9 %collective-permute-start.13 = (f32[36,128]{1,0:T(8,128)S(1)}, f32[36,128]{1,0:T(8,128)S(1)}, u32[]{:S(2)}, u32[]{:S(2)}) collective-permute-start(f32[36,128]{1,0:T(8,128)S(1)} %add.168), channel_id=1, source_target_pairs={{0,2},{1,3},{2,0},{3,1},{4,6},{5,7},{6,4},{7,5},{8,10},{9,11},{10,... | collective-permute-start | bytes 55304 | tf_op jit(solution)/shard_map/ppermute | solution.py:162
  103.7 6.6 %collective-permute-start.14 = (f32[36,128]{1,0:T(8,128)S(1)}, f32[36,128]{1,0:T(8,128)S(1)}, u32[]{:S(2)}, u32[]{:S(2)}) collective-permute-start(f32[36,128]{1,0:T(8,128)S(1)} %add.169), channel_id=1, source_target_pairs={{0,4},{1,5},{2,6},{3,7},{4,0},{5,1},{6,2},{7,3},{8,12},{9,13},{10,... | collective-permute-start | bytes 55304 | tf_op jit(solution)/shard_map/ppermute | solution.py:162
  110.4 6.9 %collective-permute-start.15 = (f32[36,128]{1,0:T(8,128)S(1)}, f32[36,128]{1,0:T(8,128)S(1)}, u32[]{:S(2)}, u32[]{:S(2)}) collective-permute-start(f32[36,128]{1,0:T(8,128)S(1)} %add.170), channel_id=1, source_target_pairs={{0,14},{1,15},{2,12},{3,13},{4,10},{5,11},{6,8},{7,9},{8,6},{9,7},... | collective-permute-start | bytes 55304 | tf_op jit(solution)/shard_map/ppermute | solution.py:162

commit v11 on v8

--- a/solution.py
+++ b/solution.py
@@ -108,8 +108,9 @@
     weight = from_blocks(block_w, sizex, sizey, sizez).reshape(cells)
 
     center = padded[1:-1, 1:-1]
-    vup, vdown = z_neighbours(velocity)
-    cup, cdown = z_neighbours(cotangent)
+    zup, zdown = z_neighbours(both)
+    vup, cup = zup[0], zup[1]
+    vdown, cdown = zdown[0], zdown[1]
     chosen = jnp.stack(
         [
             center,

time: 115 us -> 119 us (1.035)
  the two profiles are of different devices: /device:TPU:14 before, /device:TPU:34 now
where the time goes in v11:
time: 119 us; the launch traced here: 118 us
  starting transfers between devices  70.2 us (59%)
  waiting for transfers between devices  30.5 us (26%)
  matrix products  5.19 us (4%)
  local copies, waits for them, and re-layouts  5.03 us (4%)
  other arithmetic  4.87 us (4%)
  between operations  1.9 us (2%)
    ppermute x4, starting transfers between devices, shift_from(): lax.ppermute(face, axis, [(i, (i + step) % count) for i in range(count)])  28.7 us
    ppermute x8, starting transfers between devices, body(): grads = grads + lax.ppermute(grads, ('gx', 'gy'), pairs)  27.8 us
    ppermute x8, waiting for transfers between devices, body(): grads = grads + lax.ppermute(grads, ('gx', 'gy'), pairs)  21.8 us
    ppermute x1, starting transfers between devices, body(): lax.ppermute(jnp.where(yodd, up_y, down_y), 'gy', [(i, (i + 1) % ny if i...  6.21 us
    ppermute x2, waiting for transfers between devices, body(): got = lax.ppermute(message, ('gx', 'gy'), pairs)  4.8 us
    ppermute x2, starting transfers between devices, body(): got = lax.ppermute(message, ('gx', 'gy'), pairs)  3.84 us
    ppermute x4, waiting for transfers between devices, shift_from(): lax.ppermute(face, axis, [(i, (i + step) % count) for i in range(count)])  3.82 us
    ppermute x1, starting transfers between devices, body(): lax.ppermute(jnp.where(xodd, up_x, down_x), 'gx', [(i, (i + 1) % nx if i...  3.69 us
  transfers between devices with their start and end apart: 16, of which 10 were waited for; matrix products, arithmetic and copies ran while one was open for 7% of the time, Pallas kernels for 0%

profile of v11, /device:TPU:34, one launch (start us, length us, event | category | flops | bytes accessed | tf_op | source)
XLA Modules:
  0.0 117.7 jit_solution(17070892340276536266)
XLA Ops:
  1.4 1.9 %collective-permute-start.3 = (f32[2,8,128]{2,1,0:T(8,128)S(1)}, f32[2,8,128]{2,1,0:T(8,128)S(1)}, u32[]{:S(2)}, u32[]{:S(2)}) collective-permute-start(f32[2,8,128]{2,1,0:T(8,128)S(1)} %get-tuple-element.18), channel_id=1, source_target_pairs={{0,16},{16,32},{32,48},{48,64},{64,80},{80,96},{96,112},{112,128},... | collective-permute-start | bytes 24584 | tf_op jit(solution)/shard_map/ppermute | solution.py:11
  3.3 3.6 %collective-permute-start.2 = (f32[2,8,128]{2,1,0:T(8,128)S(1)}, f32[2,8,128]{2,1,0:T(8,128)S(1)}, u32[]{:S(2)}, u32[]{:S(2)}) collective-permute-start(f32[2,8,128]{2,1,0:T(8,128)S(1)} %get-tuple-element.19), channel_id=1, source_target_pairs={{0,1008},{16,0},{32,16},{48,32},{64,48},{80,64},{96,80},{112,96},{... | collective-permute-start | bytes 24584 | tf_op jit(solution)/shard_map/ppermute | solution.py:11
  7.8 21.2 %collective-permute-start.1 = (f32[2,8,128]{2,1,0:T(8,128)S(1)}, f32[2,8,128]{2,1,0:T(8,128)S(1)}, u32[]{:S(2)}, u32[]{:S(2)}) collective-permute-start(f32[2,8,128]{2,1,0:T(8,128)S(1)} %bitcast.204), channel_id=1, source_target_pairs={{0,15},{1,0},{2,1},{3,2},{4,3},{5,4},{6,5},{7,6},{8,7},{9,8},{10,9... | collective-permute-start | bytes 24584 | tf_op jit(solution)/shard_map/ppermute | solution.py:11
  29.1 1.9 %collective-permute-start = (f32[2,8,128]{2,1,0:T(8,128)S(1)}, f32[2,8,128]{2,1,0:T(8,128)S(1)}, u32[]{:S(2)}, u32[]{:S(2)}) collective-permute-start(f32[2,8,128]{2,1,0:T(8,128)S(1)} %bitcast.203), channel_id=1, source_target_pairs={{0,1},{1,2},{2,3},{3,4},{4,5},{5,6},{6,7},{7,8},{8,9},{9,10},{10,1... | collective-permute-start | bytes 24584 | tf_op jit(solution)/shard_map/ppermute | solution.py:11
  36.9 3.8 %collective-permute-done = f32[2,8,128]{2,1,0:T(8,128)S(1)} collective-permute-done((f32[2,8,128]{2,1,0:T(8,128)S(1)}, f32[2,8,128]{2,1,0:T(8,128)S(1)}, u32[]{:S(2)}, u32[]{:S(2)}) %collective-permute-start) | collective-permute-done | bytes 8224 | tf_op jit(solution)/shard_map/ppermute | solution.py:11
  44.7 4.5 %collective-permute-start.4 = (f32[36,128]{1,0:T(8,128)S(1)}, f32[36,128]{1,0:T(8,128)S(1)}, u32[]{:S(2)}, u32[]{:S(2)}) collective-permute-start(f32[36,128]{1,0:T(8,128)S(1)} %constant_dynamic-update-slice_fusion), channel_id=1, source_target_pairs={{0,32},{1,33},{2,34},{3,35},{4,36},{5,37},{6,38},{7,39},{8,40},{9,... | collective-permute-start | bytes 55304 | tf_op jit(solution)/shard_map/ppermute | solution.py:165
  51.0 1.9 %collective-permute-start.5 = (f32[44,128]{1,0:T(8,128)S(1)}, f32[44,128]{1,0:T(8,128)S(1)}, u32[]{:S(2)}, u32[]{:S(2)}) collective-permute-start(f32[44,128]{1,0:T(8,128)S(1)} %pad_maximum_fusion.21), channel_id=1, source_target_pairs={{0,16},{1,17},{2,18},{3,19},{4,20},{5,21},{6,22},{7,23},{8,24},{9,... | collective-permute-start | bytes 67592 | tf_op jit(solution)/shard_map/ppermute | solution.py:170
  54.1 1.9 %collective-permute-start.7 = (f32[44,128]{1,0:T(8,128)S(1)}, f32[44,128]{1,0:T(8,128)S(1)}, u32[]{:S(2)}, u32[]{:S(2)}) collective-permute-start(f32[44,128]{1,0:T(8,128)S(1)} %pad_maximum_fusion.22), channel_id=1, source_target_pairs={{0,1},{1,0},{2,3},{3,2},{4,5},{5,4},{6,7},{7,6},{8,9},{9,8},{10,11... | collective-permute-start | bytes 67592 | tf_op jit(solution)/shard_map/ppermute | solution.py:170
  56.1 3.7 %collective-permute-start.6 = (f32[8,128]{1,0:T(8,128)S(1)}, f32[8,128]{1,0:T(8,128)S(1)}, u32[]{:S(2)}, u32[]{:S(2)}) collective-permute-start(f32[8,128]{1,0:T(8,128)S(1)} %get-tuple-element.15), channel_id=1, source_target_pairs={{0,1008},{16,32},{32,16},{48,64},{64,48},{80,96},{96,80},{112,128}... | collective-permute-start | bytes 12296 | tf_op jit(solution)/shard_map/ppermute | solution.py:149
  60.1 3.6 %collective-permute-done.7 = f32[44,128]{1,0:T(8,128)S(1)} collective-permute-done((f32[44,128]{1,0:T(8,128)S(1)}, f32[44,128]{1,0:T(8,128)S(1)}, u32[]{:S(2)}, u32[]{:S(2)}) %collective-permute-start.7) | collective-permute-done | bytes 22560 | tf_op jit(solution)/shard_map/ppermute | solution.py:170
  63.7 3.7 %collective-permute-start.9 = (f32[36,128]{1,0:T(8,128)S(1)}, f32[36,128]{1,0:T(8,128)S(1)}, u32[]{:S(2)}, u32[]{:S(2)}) collective-permute-start(f32[36,128]{1,0:T(8,128)S(1)} %slice_add_fusion), channel_id=1, source_target_pairs={{0,64},{1,65},{2,66},{3,67},{4,68},{5,69},{6,70},{7,71},{8,72},{9,... | collective-permute-start | bytes 55304 | tf_op jit(solution)/shard_map/ppermute | solution.py:165
  68.1 2.2 %collective-permute-done.9 = f32[36,128]{1,0:T(8,128)S(1)} collective-permute-done((f32[36,128]{1,0:T(8,128)S(1)}, f32[36,128]{1,0:T(8,128)S(1)}, u32[]{:S(2)}, u32[]{:S(2)}) %collective-permute-start.9) | collective-permute-done | bytes 18464 | tf_op jit(solution)/shard_map/ppermute | solution.py:165
  70.3 5.6 %collective-permute-start.10 = (f32[36,128]{1,0:T(8,128)S(1)}, f32[36,128]{1,0:T(8,128)S(1)}, u32[]{:S(2)}, u32[]{:S(2)}) collective-permute-start(f32[36,128]{1,0:T(8,128)S(1)} %add.154), channel_id=1, source_target_pairs={{0,224},{1,225},{2,226},{3,227},{4,228},{5,229},{6,230},{7,231},{8... | collective-permute-start | bytes 55304 | tf_op jit(solution)/shard_map/ppermute | solution.py:165
  76.5 2.4 %collective-permute-done.10 = f32[36,128]{1,0:T(8,128)S(1)} collective-permute-done((f32[36,128]{1,0:T(8,128)S(1)}, f32[36,128]{1,0:T(8,128)S(1)}, u32[]{:S(2)}, u32[]{:S(2)}) %collective-permute-start.10) | collective-permute-done | bytes 18464 | tf_op jit(solution)/shard_map/ppermute | solution.py:165
  79.0 2.7 %collective-permute-start.11 = (f32[36,128]{1,0:T(8,128)S(1)}, f32[36,128]{1,0:T(8,128)S(1)}, u32[]{:S(2)}, u32[]{:S(2)}) collective-permute-start(f32[36,128]{1,0:T(8,128)S(1)} %add.155), channel_id=1, source_target_pairs={{0,256},{1,257},{2,258},{3,259},{4,260},{5,261},{6,262},{7,263},{8... | collective-permute-start | bytes 55304 | tf_op jit(solution)/shard_map/ppermute | solution.py:165
  81.7 3.0 %collective-permute-done.11 = f32[36,128]{1,0:T(8,128)S(1)} collective-permute-done((f32[36,128]{1,0:T(8,128)S(1)}, f32[36,128]{1,0:T(8,128)S(1)}, u32[]{:S(2)}, u32[]{:S(2)}) %collective-permute-start.11) | collective-permute-done | bytes 18464 | tf_op jit(solution)/shard_map/ppermute | solution.py:165
  84.7 5.6 %collective-permute-start.12 = (f32[36,128]{1,0:T(8,128)S(1)}, f32[36,128]{1,0:T(8,128)S(1)}, u32[]{:S(2)}, u32[]{:S(2)}) collective-permute-start(f32[36,128]{1,0:T(8,128)S(1)} %add.156), channel_id=1, source_target_pairs={{0,512},{1,513},{2,514},{3,515},{4,516},{5,517},{6,518},{7,519},{8... | collective-permute-start | bytes 55304 | tf_op jit(solution)/shard_map/ppermute | solution.py:165
  90.4 6.2 %collective-permute-start.8 = (f32[8,128]{1,0:T(8,128)S(1)}, f32[8,128]{1,0:T(8,128)S(1)}, u32[]{:S(2)}, u32[]{:S(2)}) collective-permute-start(f32[8,128]{1,0:T(8,128)S(1)} %get-tuple-element.31), channel_id=1, source_target_pairs={{0,15},{1,2},{2,1},{3,4},{4,3},{5,6},{6,5},{7,8},{8,7},{9,10},{10,... | collective-permute-start | bytes 12296 | tf_op jit(solution)/shard_map/ppermute | solution.py:152
  96.7 1.9 %collective-permute-start.13 = (f32[36,128]{1,0:T(8,128)S(1)}, f32[36,128]{1,0:T(8,128)S(1)}, u32[]{:S(2)}, u32[]{:S(2)}) collective-permute-start(f32[36,128]{1,0:T(8,128)S(1)} %add.157), channel_id=1, source_target_pairs={{0,2},{1,3},{2,0},{3,1},{4,6},{5,7},{6,4},{7,5},{8,10},{9,11},{10,... | collective-permute-start | bytes 55304 | tf_op jit(solution)/shard_map/ppermute | solution.py:165
  98.6 3.7 %collective-permute-done.13 = f32[36,128]{1,0:T(8,128)S(1)} collective-permute-done((f32[36,128]{1,0:T(8,128)S(1)}, f32[36,128]{1,0:T(8,128)S(1)}, u32[]{:S(2)}, u32[]{:S(2)}) %collective-permute-start.13) | collective-permute-done | bytes 18464 | tf_op jit(solution)/shard_map/ppermute | solution.py:165
  102.3 1.9 %collective-permute-start.14 = (f32[36,128]{1,0:T(8,128)S(1)}, f32[36,128]{1,0:T(8,128)S(1)}, u32[]{:S(2)}, u32[]{:S(2)}) collective-permute-start(f32[36,128]{1,0:T(8,128)S(1)} %add.158), channel_id=1, source_target_pairs={{0,4},{1,5},{2,6},{3,7},{4,0},{5,1},{6,2},{7,3},{8,12},{9,13},{10,... | collective-permute-start | bytes 55304 | tf_op jit(solution)/shard_map/ppermute | solution.py:165
  104.3 4.6 %collective-permute-done.14 = f32[36,128]{1,0:T(8,128)S(1)} collective-permute-done((f32[36,128]{1,0:T(8,128)S(1)}, f32[36,128]{1,0:T(8,128)S(1)}, u32[]{:S(2)}, u32[]{:S(2)}) %collective-permute-start.14) | collective-permute-done | bytes 18464 | tf_op jit(solution)/shard_map/ppermute | solution.py:165
  108.9 1.9 %collective-permute-start.15 = (f32[36,128]{1,0:T(8,128)S(1)}, f32[36,128]{1,0:T(8,128)S(1)}, u32[]{:S(2)}, u32[]{:S(2)}) collective-permute-start(f32[36,128]{1,0:T(8,128)S(1)} %add.159), channel_id=1, source_target_pairs={{0,14},{1,15},{2,12},{3,13},{4,10},{5,11},{6,8},{7,9},{8,6},{9,7},... | collective-permute-start | bytes 55304 | tf_op jit(solution)/shard_map/ppermute | solution.py:165
  111.5 4.2 %collective-permute-done.15 = f32[36,128]{1,0:T(8,128)S(1)} collective-permute-done((f32[36,128]{1,0:T(8,128)S(1)}, f32[36,128]{1,0:T(8,128)S(1)}, u32[]{:S(2)}, u32[]{:S(2)}) %collective-permute-start.15) | collective-permute-done | bytes 18464 | tf_op jit(solution)/shard_map/ppermute | solution.py:165
  (101 shorter events, 17.9 us)
Async XLA Ops:
  0.6 41.0 %copy-start = (bf16[64,64]{1,0:T(8,128)(2,1)S(1)}, bf16[64,64]{1,0:T(8,128)(2,1)}, u32[]{:S(2)}) copy-start(bf16[64,64]{1,0:T(8,128)(2,1)} %param.14) | copy-start | bytes 24580
  1.4 35.4 %collective-permute-start.3 = (f32[2,8,128]{2,1,0:T(8,128)S(1)}, f32[2,8,128]{2,1,0:T(8,128)S(1)}, u32[]{:S(2)}, u32[]{:S(2)}) collective-permute-start(f32[2,8,128]{2,1,0:T(8,128)S(1)} %get-tuple-element.18), channel_id=1, source_target_pairs={{0,16},{16,32},{32,48},{48,64},{64,80},{80,96},{96,112},{112,128},... | collective-permute-start | bytes 24584 | tf_op jit(solution)/shard_map/ppermute | solution.py:11
  3.3 33.5 %collective-permute-start.2 = (f32[2,8,128]{2,1,0:T(8,128)S(1)}, f32[2,8,128]{2,1,0:T(8,128)S(1)}, u32[]{:S(2)}, u32[]{:S(2)}) collective-permute-start(f32[2,8,128]{2,1,0:T(8,128)S(1)} %get-tuple-element.19), channel_id=1, source_target_pairs={{0,1008},{16,0},{32,16},{48,32},{64,48},{80,64},{96,80},{112,96},{... | collective-permute-start | bytes 24584 | tf_op jit(solution)/shard_map/ppermute | solution.py:11
  7.8 29.0 %collective-permute-start.1 = (f32[2,8,128]{2,1,0:T(8,128)S(1)}, f32[2,8,128]{2,1,0:T(8,128)S(1)}, u32[]{:S(2)}, u32[]{:S(2)}) collective-permute-start(f32[2,8,128]{2,1,0:T(8,128)S(1)} %bitcast.204), channel_id=1, source_target_pairs={{0,15},{1,0},{2,1},{3,2},{4,3},{5,4},{6,5},{7,6},{8,7},{9,8},{10,9... | collective-permute-start | bytes 24584 | tf_op jit(solution)/shard_map/ppermute | solution.py:11
  29.1 11.6 %collective-permute-start = (f32[2,8,128]{2,1,0:T(8,128)S(1)}, f32[2,8,128]{2,1,0:T(8,128)S(1)}, u32[]{:S(2)}, u32[]{:S(2)}) collective-permute-start(f32[2,8,128]{2,1,0:T(8,128)S(1)} %bitcast.203), channel_id=1, source_target_pairs={{0,1},{1,2},{2,3},{3,4},{4,5},{5,6},{6,7},{7,8},{8,9},{9,10},{10,1... | collective-permute-start | bytes 24584 | tf_op jit(solution)/shard_map/ppermute | solution.py:11
  35.0 1.6 %copy-start.2 = (f32[8,8,128]{2,1,0:T(8,128)S(1)}, f32[8,8,128]{2,1,0:T(8,128)}, u32[]{:S(2)}) copy-start(f32[8,8,128]{2,1,0:T(8,128)} %param.9) | copy-start | bytes 98308
  35.7 0.9 copy-start.4
  35.7 1.0 copy-start.1
  35.7 5.4 %copy-start.3 = (bf16[64,7]{0,1:T(8,128)(2,1)S(1)}, bf16[64,7]{0,1:T(8,128)(2,1)}, u32[]{:S(2)}) copy-start(bf16[64,7]{0,1:T(8,128)(2,1)} %param.13) | copy-start | bytes 2692
  44.7 6.2 %collective-permute-start.4 = (f32[36,128]{1,0:T(8,128)S(1)}, f32[36,128]{1,0:T(8,128)S(1)}, u32[]{:S(2)}, u32[]{:S(2)}) collective-permute-start(f32[36,128]{1,0:T(8,128)S(1)} %constant_dynamic-update-slice_fusion), channel_id=1, source_target_pairs={{0,32},{1,33},{2,34},{3,35},{4,36},{5,37},{6,38},{7,39},{8,40},{9,... | collective-permute-start | bytes 55304 | tf_op jit(solution)/shard_map/ppermute | solution.py:165
  51.0 3.1 %collective-permute-start.5 = (f32[44,128]{1,0:T(8,128)S(1)}, f32[44,128]{1,0:T(8,128)S(1)}, u32[]{:S(2)}, u32[]{:S(2)}) collective-permute-start(f32[44,128]{1,0:T(8,128)S(1)} %pad_maximum_fusion.21), channel_id=1, source_target_pairs={{0,16},{1,17},{2,18},{3,19},{4,20},{5,21},{6,22},{7,23},{8,24},{9,... | collective-permute-start | bytes 67592 | tf_op jit(solution)/shard_map/ppermute | solution.py:170
  54.1 9.6 %collective-permute-start.7 = (f32[44,128]{1,0:T(8,128)S(1)}, f32[44,128]{1,0:T(8,128)S(1)}, u32[]{:S(2)}, u32[]{:S(2)}) collective-permute-start(f32[44,128]{1,0:T(8,128)S(1)} %pad_maximum_fusion.22), channel_id=1, source_target_pairs={{0,1},{1,0},{2,3},{3,2},{4,5},{5,4},{6,7},{7,6},{8,9},{9,8},{10,11... | collective-permute-start | bytes 67592 | tf_op jit(solution)/shard_map/ppermute | solution.py:170
  56.1 42.5 %collective-permute-start.6 = (f32[8,128]{1,0:T(8,128)S(1)}, f32[8,128]{1,0:T(8,128)S(1)}, u32[]{:S(2)}, u32[]{:S(2)}) collective-permute-start(f32[8,128]{1,0:T(8,128)S(1)} %get-tuple-element.15), channel_id=1, source_target_pairs={{0,1008},{16,32},{32,16},{48,64},{64,48},{80,96},{96,80},{112,128}... | collective-permute-start | bytes 12296 | tf_op jit(solution)/shard_map/ppermute | solution.py:149
  63.7 6.6 %collective-permute-start.9 = (f32[36,128]{1,0:T(8,128)S(1)}, f32[36,128]{1,0:T(8,128)S(1)}, u32[]{:S(2)}, u32[]{:S(2)}) collective-permute-start(f32[36,128]{1,0:T(8,128)S(1)} %slice_add_fusion), channel_id=1, source_target_pairs={{0,64},{1,65},{2,66},{3,67},{4,68},{5,69},{6,70},{7,71},{8,72},{9,... | collective-permute-start | bytes 55304 | tf_op jit(solution)/shard_map/ppermute | solution.py:165
  70.3 8.7 %collective-permute-start.10 = (f32[36,128]{1,0:T(8,128)S(1)}, f32[36,128]{1,0:T(8,128)S(1)}, u32[]{:S(2)}, u32[]{:S(2)}) collective-permute-start(f32[36,128]{1,0:T(8,128)S(1)} %add.154), channel_id=1, source_target_pairs={{0,224},{1,225},{2,226},{3,227},{4,228},{5,229},{6,230},{7,231},{8... | collective-permute-start | bytes 55304 | tf_op jit(solution)/shard_map/ppermute | solution.py:165
  79.0 5.7 %collective-permute-start.11 = (f32[36,128]{1,0:T(8,128)S(1)}, f32[36,128]{1,0:T(8,128)S(1)}, u32[]{:S(2)}, u32[]{:S(2)}) collective-permute-start(f32[36,128]{1,0:T(8,128)S(1)} %add.155), channel_id=1, source_target_pairs={{0,256},{1,257},{2,258},{3,259},{4,260},{5,261},{6,262},{7,263},{8... | collective-permute-start | bytes 55304 | tf_op jit(solution)/shard_map/ppermute | solution.py:165
  84.7 12.0 %collective-permute-start.12 = (f32[36,128]{1,0:T(8,128)S(1)}, f32[36,128]{1,0:T(8,128)S(1)}, u32[]{:S(2)}, u32[]{:S(2)}) collective-permute-start(f32[36,128]{1,0:T(8,128)S(1)} %add.156), channel_id=1, source_target_pairs={{0,512},{1,513},{2,514},{3,515},{4,516},{5,517},{6,518},{7,519},{8... | collective-permute-start | bytes 55304 | tf_op jit(solution)/shard_map/ppermute | solution.py:165
  90.4 13.8 %collective-permute-start.8 = (f32[8,128]{1,0:T(8,128)S(1)}, f32[8,128]{1,0:T(8,128)S(1)}, u32[]{:S(2)}, u32[]{:S(2)}) collective-permute-start(f32[8,128]{1,0:T(8,128)S(1)} %get-tuple-element.31), channel_id=1, source_target_pairs={{0,15},{1,2},{2,1},{3,4},{4,3},{5,6},{6,5},{7,8},{8,7},{9,10},{10,... | collective-permute-start | bytes 12296 | tf_op jit(solution)/shard_map/ppermute | solution.py:152
  96.7 5.7 %collective-permute-start.13 = (f32[36,128]{1,0:T(8,128)S(1)}, f32[36,128]{1,0:T(8,128)S(1)}, u32[]{:S(2)}, u32[]{:S(2)}) collective-permute-start(f32[36,128]{1,0:T(8,128)S(1)} %add.157), channel_id=1, source_target_pairs={{0,2},{1,3},{2,0},{3,1},{4,6},{5,7},{6,4},{7,5},{8,10},{9,11},{10,... | collective-permute-start | bytes 55304 | tf_op jit(solution)/shard_map/ppermute | solution.py:165
  102.3 6.6 %collective-permute-start.14 = (f32[36,128]{1,0:T(8,128)S(1)}, f32[36,128]{1,0:T(8,128)S(1)}, u32[]{:S(2)}, u32[]{:S(2)}) collective-permute-start(f32[36,128]{1,0:T(8,128)S(1)} %add.158), channel_id=1, source_target_pairs={{0,4},{1,5},{2,6},{3,7},{4,0},{5,1},{6,2},{7,3},{8,12},{9,13},{10,... | collective-permute-start | bytes 55304 | tf_op jit(solution)/shard_map/ppermute | solution.py:165
  108.9 6.9 %collective-permute-start.15 = (f32[36,128]{1,0:T(8,128)S(1)}, f32[36,128]{1,0:T(8,128)S(1)}, u32[]{:S(2)}, u32[]{:S(2)}) collective-permute-start(f32[36,128]{1,0:T(8,128)S(1)} %add.159), channel_id=1, source_target_pairs={{0,14},{1,15},{2,12},{3,13},{4,10},{5,11},{6,8},{7,9},{8,6},{9,7},... | collective-permute-start | bytes 55304 | tf_op jit(solution)/shard_map/ppermute | solution.py:165
